TPU v7x, 32 devices: a whole 2x2x4 slice. The times are simulated.
32 devices in a mesh: slab: 4 (over y, core), tile: 8 (over z, x).
Axes of the slice: x: 2, y: 2, z: 4, core: 2. Of those that a mesh axis runs over, the one named last changes fastest.
Arguments:
- a_tiles: float32 [512, 8, 128, 128], P(('slab', 'tile')), may hold values from -0.5 to 0.5
- a_cols: int32 [512, 8], P(('slab', 'tile')), may hold values from 0 to 511, as said below
- p_tiles: float32 [512, 2, 128, 128], P(('slab', 'tile')), may hold values from -1 to 1
- p_cols: int32 [512, 2], P(('slab', 'tile')), may hold values from 0 to 31, as said below
- c_cols: int32 [32, 15], P(('slab', 'tile')), may hold values from 0 to 31, as said below
Outputs:
- galerkin: float32 [32, 15, 128, 128], P(('slab', 'tile'))
Inputs may be any that keep to these rules, and one draw needn't show every extreme that they name: `a_cols`: row block g, held by the device at slab s and tile t, names 8 different row blocks: g itself first, the others among the row blocks of its own device, the last 4 row blocks of the device at slab s - 1 and tile t, and the first 4 of the device at slab s + 1 and tile t. `p_cols`: each row names 2 different coarse blocks, owned by devices of its own slab whose tile index is t - 1, t or t + 1 modulo the number of tiles, t being the tile of the row's device. `c_cols`: the row of coarse block r, owned by the device at slab s and tile t, names each coarse block owned by a device at slab s - 1, s or s + 1 and tile t - 2 to t + 2 (both modulo the axis sizes) exactly once, in a drawn order; so every coarse block that the product reaches from row r is stored.
All inputs are finite; a program needn't handle non-finite values.
Results may differ from a plain program's by a relative error of at most 0.0003.
Values sent between devices are 32-bit elements; how exact they have to be, the bound alone decides.
No kernel may reach another device: no remote copies, remote signals or barrier semaphores. Data moves between devices by JAX's collectives and lax.ppermute only.
A program may use at most 192 MiB of HBM per device.

v0:
```python
import jax
import jax.numpy as jnp
from jax import lax
from jax.sharding import PartitionSpec as P

RIM = 4


def extended(cells, sides, width, closed):
    for axis, dim in sides:
        count = lax.axis_size(axis)
        ends = count if closed else count - 1
        head = lax.slice_in_dim(cells, 0, width, axis=dim)
        tail = lax.slice_in_dim(cells, cells.shape[dim] - width, cells.shape[dim], axis=dim)
        cells = jnp.concatenate(
            [
                lax.ppermute(tail, axis, [(i, (i + 1) % count) for i in range(ends)]),
                cells,
                lax.ppermute(head, axis, [((i + 1) % count, i) for i in range(ends)]),
            ],
            axis=dim,
        )
    return cells


def passed_along(value, axis, steps):
    count = lax.axis_size(axis)
    pairs = [(source, (source + steps) % count) for source in range(count)]
    return lax.ppermute(value, axis, pairs)


def shards(a_tiles, a_cols, p_tiles, p_cols, c_cols):
    row_count = a_tiles.shape[0]
    coupling_slots = a_tiles.shape[1]
    tile_width = a_tiles.shape[2]
    interp_slots = p_tiles.shape[1]
    block_count = c_cols.shape[0]
    pattern_slots = c_cols.shape[1]
    tile_count = lax.axis_size("tile")
    tile_index = lax.axis_index("tile")
    slab_index = lax.axis_index("slab")
    device = slab_index * tile_count + tile_index
    ext_tiles, ext_keys = (
        extended(p_tiles, (("slab", 0),), RIM, False),
        extended(p_cols.astype(jnp.float32), (("slab", 0),), RIM, False),
    )
    ext_keys = ext_keys.astype(jnp.int32)
    own_base = device * row_count
    lower_base = (device - tile_count) * row_count + row_count - RIM
    upper_base = (device + tile_count) * row_count
    local_index = jnp.where(
        a_cols < own_base,
        a_cols - lower_base,
        jnp.where(
            a_cols < own_base + row_count,
            RIM + a_cols - own_base,
            RIM + row_count + a_cols - upper_base,
        ),
    )
    picked = ext_tiles[local_index]
    picked_cols = ext_keys[local_index]
    products = jnp.einsum("jaxy,japyz->japxz", a_tiles, picked, precision=lax.Precision.HIGHEST)
    flat_products = products.reshape(
        row_count, coupling_slots * interp_slots, tile_width, tile_width
    )
    flat_keys = picked_cols.reshape(row_count, coupling_slots * interp_slots)
    pattern = extended(c_cols, (("tile", 0),), block_count, True)
    slab_first = slab_index * tile_count * block_count
    targets = p_cols - slab_first
    owner_tile = targets // block_count
    relative = jnp.remainder(owner_tile - tile_index + 1, tile_count)
    local_owner = relative * block_count + targets % block_count
    wanted = pattern[local_owner]
    matches = (flat_keys[:, None, None, :] == wanted[:, :, :, None]).astype(jnp.float32)
    contrib_terms = jnp.einsum(
        "jqyx,jnyz->jqnxz", p_tiles, flat_products, precision=lax.Precision.HIGHEST
    )
    summed = jnp.einsum(
        "jqmn,jqnxz->jqmxz", matches, contrib_terms, precision=lax.Precision.HIGHEST
    )
    summed = summed.reshape(row_count * interp_slots, pattern_slots, tile_width, tile_width)
    owners = local_owner.reshape(-1)
    wanted_rows = jnp.arange(3 * block_count, dtype=jnp.int32)
    onehot = (owners[None, :] == wanted_rows[:, None]).astype(jnp.float32)
    parts = jnp.einsum("rk,kmxz->rmxz", onehot, summed, precision=lax.Precision.HIGHEST)
    to_lower = parts[:block_count]
    own_part = parts[block_count : 2 * block_count]
    to_upper = parts[2 * block_count :]
    from_lower = passed_along(to_upper, "tile", 1)
    from_upper = passed_along(to_lower, "tile", -1)
    return own_part + from_lower + from_upper


def solution(mesh):
    return jax.shard_map(
        shards,
        mesh=mesh,
        in_specs=(
            P(("slab", "tile"), None, None, None),
            P(("slab", "tile"), None),
            P(("slab", "tile"), None, None, None),
            P(("slab", "tile"), None),
            P(("slab", "tile"), None),
        ),
        out_specs=P(("slab", "tile"), None, None, None),
        check_vma=False,
    )
```

profile of v0, /device:TPU:1, one launch (start us, length us, event | category | flops | bytes accessed | tf_op | source)
XLA Modules:
  0.0 242.0 jit_solution(16884151482735224986)
XLA Ops:
  0.0 2.0 collective-permute-start.2
  2.0 3.0 %collective-permute-start.3 = (s32[1,15]{1,0:T(1,128)}, s32[1,15]{1,0:T(1,128)S(1)}, u32[]{:S(2)}, u32[]{:S(2)}) collective-permute-start(s32[1,15]{1,0:T(1,128)} %param.9), channel_id=1, source_target_pairs={{1,0},{2,1},{3,2},{4,3},{5,4},{6,5},{7,6},{0,7},{9,8},{10,9},{11,1... | collective-permute-start | bytes 188 | tf_op jit(solution)/shard_map/ppermute | solution.py:19
  5.1 0.8 compare_select_fusion.1
  5.9 4.2 %collective-permute-start = (f32[4,2]{0,1:T(2,128)S(1)}, f32[4,2]{0,1:T(2,128)S(1)}, u32[]{:S(2)}, u32[]{:S(2)}) collective-permute-start(f32[4,2]{0,1:T(2,128)S(1)} %get-tuple-element.11), channel_id=1, source_target_pairs={{0,8},{8,16},{16,24},{1,9},{9,17},{17,25},{2,10},{10,18},{18,26},{... | collective-permute-start | bytes 104 | tf_op jit(solution)/shard_map/ppermute | solution.py:17
  10.1 1.3 fusion.16
  11.4 1.9 collective-permute-start.4
  13.3 2.4 %collective-permute-start.5 = (f32[4,2,128,128]{3,2,1,0:T(8,128)S(1)}, f32[4,2,128,128]{3,2,1,0:T(8,128)}, u32[]{:S(2)}, u32[]{:S(2)}) collective-permute-start(f32[4,2,128,128]{3,2,1,0:T(8,128)S(1)} %get-tuple-element.10), channel_id=1, source_target_pairs={{8,0},{16,8},{24,16},{9,1},{17,9},{25,17},{10,2},{18,10},{26,18},{... | collective-permute-start | bytes 1572872 | tf_op jit(solution)/shard_map/ppermute | solution.py:19
  15.8 0.7 compare_select_fusion
  16.5 0.1 reshape.13
  16.6 0.1 copy.31
  16.7 0.1 reshape.21
  16.8 0.1 copy.28
  16.9 0.1 eq.33
  17.0 1.9 collective-permute-start.1
  18.9 5.0 %collective-permute-done.1 = f32[4,2]{0,1:T(2,128)S(1)} collective-permute-done((f32[4,2]{0,1:T(2,128)S(1)}, f32[4,2]{0,1:T(2,128)S(1)}, u32[]{:S(2)}, u32[]{:S(2)}) %collective-permute-start.1) | collective-permute-done | bytes 64 | tf_op jit(solution)/shard_map/ppermute | solution.py:19
  24.0 0.1 copy.30
  24.1 0.6 gather_fusion
  24.8 0.7 pad_add_fusion
  25.5 0.6 gather_fusion.1
  26.1 0.8 copy-done.1
  26.9 2.0 pad_maximum_fusion
  28.9 7.4 %gather_fusion.2 = f32[128,2,128,128]{3,2,1,0:T(8,128)} fusion(f32[24,2,128,128]{3,2,1,0:T(8,128)S(1)} %pad_maximum_fusion, s32[1024]{0:T(1024)S(1)} %pad_clamp_fusion.1), kind=kCustom, calls=%fused_computation.2 | custom fusion | bytes 33554944 | tf_op jit(solution)/shard_map/gather | solution.py:60
  36.3 32.7 %fusion.2 = f32[16,8,2,128,128]{4,3,2,1,0:T(8,128)S(1)} fusion(f32[16,8,2,128,128]{4,3,2,1,0:T(8,128)} %bitcast.38, f32[16,8,128,128]{3,2,1,0:T(8,128)} %param.5), kind=kOutput, calls=%fused_computation.6 | convolution fusion | flops 6442450944 | bytes 41943040 | tf_op jit(solution)/shard_map/jaxy,japyz->japxz/dot_general | solution.py:62
  69.0 30.3 %convolution_bitcast_fusion = f32[16,2,16,128,128]{3,4,1,2,0:T(8,128)} fusion(f32[16,16,128,128,1]{2,3,4,1,0:T(8,128)S(1)} %bitcast.37, f32[16,2,128,128]{3,2,1,0:T(8,128)S(1)} %copy-done), kind=kOutput, calls=%fused_computation.5 | convolution fusion | flops 12884901888 | bytes 52428800 | tf_op jit(solution)/shard_map/jqyx,jnyz->jqnxz/dot_general | solution.py:75
  99.2 34.6 %copy.33 = f32[16,2,16,128,128]{4,2,3,1,0:T(8,128)} copy(f32[16,2,16,128,128]{3,4,1,2,0:T(8,128)} %convolution_bitcast_fusion) | data formatting | bytes 67108864 | tf_op jit(solution)/shard_map/jqyx,jnyz->jqnxz/transpose | solution.py:75
  133.9 28.5 %fusion.6 = f32[16,2,15,128,128]{4,2,3,1,0:T(8,128)} fusion(f32[16,2,16,128,128]{4,2,3,1,0:T(8,128)} %copy.33, s32[16,2,15]{2,1,0:T(2,128)S(1)} %bitcast.39, s32[16,16]{1,0:T(8,128)S(1)} %eq.37), kind=kOutput, calls=%fused_computation.12 | convolution fusion | flops 1509957120 | bytes 65014656 | tf_op jit(solution)/shard_map/jqmn,jqnxz->jqmxz/dot_general | solution.py:78
  162.4 28.0 %fusion = f32[3,15,128,128]{3,0,2,1:T(4,128)} fusion(f32[32,15,128,128]{3,1,2,0:T(8,128)} %bitcast.36, s32[32]{0:T(128)S(1)} %eq.33), kind=kOutput, calls=%fused_computation.3 | convolution fusion | flops 283115616 | bytes 34406528 | tf_op jit(solution)/shard_map/rk,kmxz->rmxz/dot_general | solution.py:85
  190.4 5.3 %fusion.15 = (f32[1,15,128,128]{3,0,2,1:T(1,128)S(1)}, f32[1,15,128,128]{3,0,2,1:T(1,128)S(1)}) fusion(f32[3,15,128,128]{3,0,2,1:T(4,128)} %fusion), kind=kLoop, calls=%fused_computation.30 | loop fusion | bytes 3932160 | tf_op jit(solution)/shard_map/slice | solution.py:88
  195.8 4.1 %collective-permute-start.7 = (f32[1,15,128,128]{3,0,2,1:T(1,128)S(1)}, f32[1,15,128,128]{3,0,2,1:T(1,128)S(1)}, u32[]{:S(2)}, u32[]{:S(2)}) collective-permute-start(f32[1,15,128,128]{3,0,2,1:T(1,128)S(1)} %get-tuple-element.8), channel_id=1, source_target_pairs={{0,7},{1,0},{2,1},{3,2},{4,3},{5,4},{6,5},{7,6},{8,15},{9,8},{10,9... | collective-permute-start | bytes 2949128 | tf_op jit(solution)/shard_map/ppermute | solution.py:29
  200.0 34.8 %collective-permute-done.6 = f32[1,15,128,128]{3,0,2,1:T(1,128)S(1)} collective-permute-done((f32[1,15,128,128]{3,0,2,1:T(1,128)S(1)}, f32[1,15,128,128]{3,0,2,1:T(1,128)S(1)}, u32[]{:S(2)}, u32[]{:S(2)}) %collective-permute-start.6) | collective-permute-done | bytes 983072 | tf_op jit(solution)/shard_map/ppermute | solution.py:29
  234.8 2.2 collective-permute-done.7
  237.0 5.0 %fusion.5 = f32[1,15,128,128]{3,0,2,1:T(1,128)} fusion(f32[1,15,128,128]{3,0,2,1:T(1,128)S(1)} %collective-permute-done.7, f32[1,15,128,128]{3,0,2,1:T(1,128)S(1)} %collective-permute-done.6, f32[3,15,128,128]{3,0,2,1:T(4,128)} %fusion), kind=kLoop, calls=%fused_computation.11 | loop fusion | flops 491520 | bytes 3932160 | tf_op jit(solution)/shard_map/add | solution.py:91
  (15 shorter events, 0.4 us)
Async XLA Ops:
  0.0 24.8 %collective-permute-start.2 = (s32[1,15]{1,0:T(1,128)}, s32[1,15]{1,0:T(1,128)S(1)}, u32[]{:S(2)}, u32[]{:S(2)}) collective-permute-start(s32[1,15]{1,0:T(1,128)} %param.9), channel_id=1, source_target_pairs={{0,1},{1,2},{2,3},{3,4},{4,5},{5,6},{6,7},{7,0},{8,9},{9,10},{10,1... | collective-permute-start | bytes 188 | tf_op jit(solution)/shard_map/ppermute | solution.py:17
  2.0 22.8 %collective-permute-start.3 = (s32[1,15]{1,0:T(1,128)}, s32[1,15]{1,0:T(1,128)S(1)}, u32[]{:S(2)}, u32[]{:S(2)}) collective-permute-start(s32[1,15]{1,0:T(1,128)} %param.9), channel_id=1, source_target_pairs={{1,0},{2,1},{3,2},{4,3},{5,4},{6,5},{7,6},{0,7},{9,8},{10,9},{11,1... | collective-permute-start | bytes 188 | tf_op jit(solution)/shard_map/ppermute | solution.py:19
  5.9 11.1 %collective-permute-start = (f32[4,2]{0,1:T(2,128)S(1)}, f32[4,2]{0,1:T(2,128)S(1)}, u32[]{:S(2)}, u32[]{:S(2)}) collective-permute-start(f32[4,2]{0,1:T(2,128)S(1)} %get-tuple-element.11), channel_id=1, source_target_pairs={{0,8},{8,16},{16,24},{1,9},{9,17},{17,25},{2,10},{10,18},{18,26},{... | collective-permute-start | bytes 104 | tf_op jit(solution)/shard_map/ppermute | solution.py:17
  11.4 14.7 %collective-permute-start.4 = (f32[4,2,128,128]{3,2,1,0:T(8,128)S(1)}, f32[4,2,128,128]{3,2,1,0:T(8,128)S(1)}, u32[]{:S(2)}, u32[]{:S(2)}) collective-permute-start(f32[4,2,128,128]{3,2,1,0:T(8,128)S(1)} %get-tuple-element.9), channel_id=1, source_target_pairs={{0,8},{8,16},{16,24},{1,9},{9,17},{17,25},{2,10},{10,18},{18,26},{... | collective-permute-start | bytes 1572872 | tf_op jit(solution)/shard_map/ppermute | solution.py:17
  13.3 13.6 %collective-permute-start.5 = (f32[4,2,128,128]{3,2,1,0:T(8,128)S(1)}, f32[4,2,128,128]{3,2,1,0:T(8,128)}, u32[]{:S(2)}, u32[]{:S(2)}) collective-permute-start(f32[4,2,128,128]{3,2,1,0:T(8,128)S(1)} %get-tuple-element.10), channel_id=1, source_target_pairs={{8,0},{16,8},{24,16},{9,1},{17,9},{25,17},{10,2},{18,10},{26,18},{... | collective-permute-start | bytes 1572872 | tf_op jit(solution)/shard_map/ppermute | solution.py:19
  17.0 6.9 %collective-permute-start.1 = (f32[4,2]{0,1:T(2,128)S(1)}, f32[4,2]{0,1:T(2,128)S(1)}, u32[]{:S(2)}, u32[]{:S(2)}) collective-permute-start(f32[4,2]{0,1:T(2,128)S(1)} %get-tuple-element.12), channel_id=1, source_target_pairs={{8,0},{16,8},{24,16},{9,1},{17,9},{25,17},{10,2},{18,10},{26,18},{... | collective-permute-start | bytes 104 | tf_op jit(solution)/shard_map/ppermute | solution.py:19
  26.1 0.8 copy-start.1
  36.3 32.7 %copy-start = (f32[16,2,128,128]{3,2,1,0:T(8,128)S(1)}, f32[16,2,128,128]{3,2,1,0:T(8,128)}, u32[]{:S(2)}) copy-start(f32[16,2,128,128]{3,2,1,0:T(8,128)} %param.7) | copy-start | bytes 6291460
  195.7 39.0 %collective-permute-start.6 = (f32[1,15,128,128]{3,0,2,1:T(1,128)S(1)}, f32[1,15,128,128]{3,0,2,1:T(1,128)S(1)}, u32[]{:S(2)}, u32[]{:S(2)}) collective-permute-start(f32[1,15,128,128]{3,0,2,1:T(1,128)S(1)} %get-tuple-element.7), channel_id=1, source_target_pairs={{0,1},{1,2},{2,3},{3,4},{4,5},{5,6},{6,7},{7,0},{8,9},{9,10},{10,1... | collective-permute-start | bytes 2949128 | tf_op jit(solution)/shard_map/ppermute | solution.py:29
  195.8 41.2 %collective-permute-start.7 = (f32[1,15,128,128]{3,0,2,1:T(1,128)S(1)}, f32[1,15,128,128]{3,0,2,1:T(1,128)S(1)}, u32[]{:S(2)}, u32[]{:S(2)}) collective-permute-start(f32[1,15,128,128]{3,0,2,1:T(1,128)S(1)} %get-tuple-element.8), channel_id=1, source_target_pairs={{0,7},{1,0},{2,1},{3,2},{4,3},{5,4},{6,5},{7,6},{8,15},{9,8},{10,9... | collective-permute-start | bytes 2949128 | tf_op jit(solution)/shard_map/ppermute | solution.py:29
where the time goes:
time: 243 us; the launch traced here: 242 us
  matrix products  119 us (49%)
  local copies, waits for them, and re-layouts  51.3 us (21%)
  waiting for transfers between devices  42 us (17%)
  starting transfers between devices  19.7 us (8%)
  other arithmetic  9.29 us (4%)
    ppermute x2, waiting for transfers between devices, passed_along(): return lax.ppermute(value, axis, pairs)  37 us
    transpose x1, local copies, waits for them, and re-layouts, shards(): jnp.einsum('jqyx,jnyz->jqnxz', p_tiles, flat_products, precision=lax.Prec...  34.6 us
    dot_general x1, matrix products, shards(): jnp.einsum('jaxy,japyz->japxz', a_tiles, picked, precision=lax.Precision....  32.7 us
    dot_general x1, matrix products, shards(): jnp.einsum('jqyx,jnyz->jqnxz', p_tiles, flat_products, precision=lax.Prec...  30.3 us
    dot_general x1, matrix products, shards(): jnp.einsum('jqmn,jqnxz->jqmxz', matches, contrib_terms, precision=lax.Pre...  28.5 us
    dot_general x1, matrix products, shards(): jnp.einsum('rk,kmxz->rmxz', onehot, summed, precision=lax.Precision.HIGHEST)  28 us
    ppermute x3, starting transfers between devices, extended(): lax.ppermute(tail, axis, [(i, (i + 1) % count) for i in range(ends)])  8.13 us
    ppermute x3, starting transfers between devices, extended(): lax.ppermute(head, axis, [((i + 1) % count, i) for i in range(ends)])  7.4 us
  transfers between devices with their start and end apart: 8, of which 3 were waited for; matrix products, arithmetic and copies ran while one was open for 2% of the time, Pallas kernels for 0%

commit v1 on v0

v1 whole, which is shorter than its diff:
```python
import functools

import jax
import jax.numpy as jnp
from jax import lax
from jax.experimental import pallas as pl
from jax.experimental.pallas import tpu as pltpu
from jax.sharding import PartitionSpec as P

RIM = 4
HIGHEST = lax.Precision.HIGHEST


def extended(cells, axis, width):
    count = lax.axis_size(axis)
    head = cells[:width]
    tail = cells[cells.shape[0] - width :]
    return jnp.concatenate(
        [
            lax.ppermute(tail, axis, [(i, i + 1) for i in range(count - 1)]),
            cells,
            lax.ppermute(head, axis, [(i + 1, i) for i in range(count - 1)]),
        ],
        axis=0,
    )


def passed_along(value, axis, steps):
    count = lax.axis_size(axis)
    pairs = [(source, (source + steps) % count) for source in range(count)]
    return lax.ppermute(value, axis, pairs)


def triple_kernel(
    coupling_slots, interp_slots, blocks, region, lidx_ref, slot_ref, own_ref, a_ref, ext_ref, out_ref, y_ref
):
    g = pl.program_id(0)
    bs = a_ref.shape[2]

    @pl.when(g == 0)
    def _():
        out_ref[...] = jnp.zeros_like(out_ref)

    y_ref[...] = jnp.zeros_like(y_ref)
    for a in range(coupling_slots):
        row = lidx_ref[g * coupling_slots + a]
        prod = jnp.dot(
            a_ref[0, a], ext_ref[row], precision=HIGHEST, preferred_element_type=jnp.float32
        )
        for p in range(interp_slots):
            slot = slot_ref[(g * coupling_slots + a) * interp_slots + p]
            y_ref[slot] += prod[:, p * bs : (p + 1) * bs]
    pt = ext_ref[RIM + g].T
    owners = [own_ref[g * interp_slots + q] for q in range(interp_slots)]
    for c in range(region):
        res = jnp.dot(pt, y_ref[c], precision=HIGHEST, preferred_element_type=jnp.float32)
        for q in range(interp_slots):
            out_ref[owners[q], c] += res[q * bs : (q + 1) * bs]


def shards(a_tiles, a_cols, p_tiles, p_cols, c_cols):
    rows, coupling_slots, bs, _ = a_tiles.shape
    interp_slots = p_tiles.shape[1]
    blocks, pattern_slots = c_cols.shape
    tiles = lax.axis_size("tile")
    slabs = lax.axis_size("slab")
    t = lax.axis_index("tile")
    s = lax.axis_index("slab")
    device = s * tiles + t
    region = 9 * blocks

    p_cat = p_tiles.transpose(0, 2, 1, 3).reshape(rows, bs, interp_slots * bs)
    ext = extended(p_cat, "slab", RIM)
    ext_keys = extended(p_cols, "slab", RIM)

    own_base = device * rows
    lower_base = (device - tiles) * rows + rows - RIM
    upper_base = (device + tiles) * rows
    local_index = jnp.where(
        a_cols < own_base,
        a_cols - lower_base,
        jnp.where(
            a_cols < own_base + rows,
            RIM + a_cols - own_base,
            RIM + rows + a_cols - upper_base,
        ),
    )
    local_index = jnp.clip(local_index, 0, rows + 2 * RIM - 1)
    keys = ext_keys[local_index]
    k_slab = keys // (tiles * blocks)
    k_tile = (keys // blocks) % tiles
    k_dt = (k_tile - t + 1) % tiles - 1
    slot = ((k_slab - s + 1) * 3 + (k_dt + 1)) * blocks + keys % blocks
    slot = jnp.clip(slot, 0, region - 1)

    targets = p_cols - s * tiles * blocks
    relative = jnp.remainder(targets // blocks - t + 1, tiles)
    owner = jnp.clip(relative * blocks + targets % blocks, 0, 3 * blocks - 1)

    kernel = functools.partial(triple_kernel, coupling_slots, interp_slots, blocks, region)
    out = pl.pallas_call(
        kernel,
        out_shape=jax.ShapeDtypeStruct((3 * blocks, region, bs, bs), jnp.float32),
        grid_spec=pltpu.PrefetchScalarGridSpec(
            num_scalar_prefetch=3,
            grid=(rows,),
            in_specs=[
                pl.BlockSpec((1, coupling_slots, bs, bs), lambda g, *_: (g, 0, 0, 0)),
                pl.BlockSpec(ext.shape, lambda g, *_: (0, 0, 0)),
            ],
            out_specs=pl.BlockSpec((3 * blocks, region, bs, bs), lambda g, *_: (0, 0, 0, 0)),
            scratch_shapes=[pltpu.VMEM((region, bs, bs), jnp.float32)],
        ),
        compiler_params=pltpu.CompilerParams(dimension_semantics=("arbitrary",)),
    )(
        local_index.reshape(-1).astype(jnp.int32),
        slot.reshape(-1).astype(jnp.int32),
        owner.reshape(-1).astype(jnp.int32),
        a_tiles,
        ext,
    )

    own_part = out[blocks : 2 * blocks]
    from_lower = passed_along(out[2 * blocks :], "tile", 1)
    from_upper = passed_along(out[:blocks], "tile", -1)

    c_slab = c_cols // (tiles * blocks)
    c_tile = (c_cols // blocks) % tiles
    c_w = c_cols % blocks
    c_ds = (c_slab - s + 1) % slabs - 1
    c_dt = (c_tile - t + 2) % tiles - 2
    base = (c_ds + 1) * 3
    r_idx = jnp.arange(blocks, dtype=jnp.int32)[:, None]

    def pick(part, dt):
        valid = (dt >= -1) & (dt <= 1)
        idx = jnp.clip((base + dt + 1) * blocks + c_w, 0, region - 1)
        tiles_picked = part[r_idx, idx]
        return jnp.where(valid[:, :, None, None], tiles_picked, 0.0)

    return pick(own_part, c_dt) + pick(from_lower, c_dt + 1) + pick(from_upper, c_dt - 1)


def solution(mesh):
    return jax.shard_map(
        shards,
        mesh=mesh,
        in_specs=(
            P(("slab", "tile"), None, None, None),
            P(("slab", "tile"), None),
            P(("slab", "tile"), None, None, None),
            P(("slab", "tile"), None),
            P(("slab", "tile"), None),
        ),
        out_specs=P(("slab", "tile"), None, None, None),
        check_vma=False,
    )
```

time: 243 us -> 98.8 us (0.41)
  matrix products: 119 us -> 0 us
  Pallas kernels: 0 us -> 42.1 us
  local copies, waits for them, and re-layouts: 51.3 us -> 13.4 us
  waiting for transfers between devices: 42 us -> 22.6 us
  other arithmetic: 9.29 us -> 3.92 us
  starting transfers between devices: 19.7 us -> 16.2 us
    dot_general x4 -> x0, matrix products: 119 us -> none  [the longest x1 32.7 us: shards(): jnp.einsum('jaxy,japyz->japxz', a_tiles, picked, precision=lax.Precision....]
    pallas_call x0 -> x1, Pallas kernels: none -> 42.1 us  [shards(): pl.pallas_call(kernel, out_shape=jax.ShapeDtypeStruct((3 * blocks, region...]
    transpose x1 -> x0, local copies, waits for them, and re-layouts: 34.6 us -> none  [shards(): jnp.einsum('jqyx,jnyz->jqnxz', p_tiles, flat_products, precision=lax.Prec...]
    ppermute x2, waiting for transfers between devices: 37 us -> 19 us  [passed_along(): return lax.ppermute(value, axis, pairs)]
    gather x3 -> x5, local copies, waits for them, and re-layouts: 8.57 us -> 3.68 us  [the longest x3 2.9 us: pick(): tiles_picked = part[r_idx, idx]]
    add x1, other arithmetic: 5.03 us -> 1.22 us  [shards(): pick(own_part, c_dt) + pick(from_lower, c_dt + 1)]
    ppermute x6 -> x4, starting transfers between devices: 15.5 us -> 12 us  [the longest x2 8.16 us: extended(): lax.ppermute(tail, axis, [(i, i + 1) for i in range(count - 1)])]
    reshape x0 -> x3, local copies, waits for them, and re-layouts: none -> 3.06 us  [the longest x1 1.78 us: shards(): p_cat = p_tiles.transpose(0, 2, 1, 3).reshape(rows, bs, interp_slots * bs)]
  transfers between devices with their start and end apart: 8 -> 6, of which waited for: 3 -> 3; matrix products, arithmetic and copies ran while one was open for 2% -> 9% of each run, Pallas kernels for 0% -> 0%
where the time goes in v1:
time: 98.8 us; the launch traced here: 98.4 us
  Pallas kernels  42.1 us (43%)
  waiting for transfers between devices  22.6 us (23%)
  starting transfers between devices  16.2 us (16%)
  local copies, waits for them, and re-layouts  13.4 us (14%)
  other arithmetic  3.92 us (4%)
    pallas_call x1, Pallas kernels, shards(): pl.pallas_call(kernel, out_shape=jax.ShapeDtypeStruct((3 * blocks, region...  42.1 us
    ppermute x2, waiting for transfers between devices, passed_along(): return lax.ppermute(value, axis, pairs)  19 us
    ppermute x2, starting transfers between devices, extended(): lax.ppermute(tail, axis, [(i, i + 1) for i in range(count - 1)])  8.16 us
    ppermute x2, starting transfers between devices, passed_along(): return lax.ppermute(value, axis, pairs)  4.25 us
    ppermute x2, starting transfers between devices, extended(): lax.ppermute(head, axis, [(i + 1, i) for i in range(count - 1)])  3.83 us
    ppermute x2, waiting for transfers between devices, extended(): lax.ppermute(head, axis, [(i + 1, i) for i in range(count - 1)])  3.6 us
    gather x3, local copies, waits for them, and re-layouts, pick(): tiles_picked = part[r_idx, idx]  2.9 us
    slice x1, local copies, waits for them, and re-layouts, shards(): own_part = out[blocks:2 * blocks]  2.37 us
  transfers between devices with their start and end apart: 6, of which 3 were waited for; matrix products, arithmetic and copies ran while one was open for 9% of the time, Pallas kernels for 0%

profile of v1, /device:TPU:1, one launch (start us, length us, event | category | flops | bytes accessed | tf_op | source)
XLA Modules:
  0.0 98.4 jit_solution(3324208805366279688)
XLA Ops:
  0.0 0.8 fusion.18
  0.8 4.5 %collective-permute-start = (s32[4,2]{0,1:T(2,128)S(1)}, s32[4,2]{0,1:T(2,128)S(1)}, u32[]{:S(2)}, u32[]{:S(2)}) collective-permute-start(s32[4,2]{0,1:T(2,128)S(1)} %get-tuple-element.18), channel_id=1, source_target_pairs={{0,8},{8,16},{16,24},{1,9},{9,17},{17,25},{2,10},{10,18},{18,26},{... | collective-permute-start | bytes 104 | tf_op jit(solution)/shard_map/ppermute | solution.py:20
  5.4 1.9 %collective-permute-start.1 = (s32[4,2]{0,1:T(2,128)S(1)}, s32[4,2]{0,1:T(2,128)S(1)}, u32[]{:S(2)}, u32[]{:S(2)}) collective-permute-start(s32[4,2]{0,1:T(2,128)S(1)} %get-tuple-element.19), channel_id=1, source_target_pairs={{8,0},{16,8},{24,16},{9,1},{17,9},{25,17},{10,2},{18,10},{26,18},{... | collective-permute-start | bytes 104 | tf_op jit(solution)/shard_map/ppermute | solution.py:22
  7.3 1.3 %slice_bitcast_fusion.1 = (f32[4,2,16,8,128]{4,3,2,1,0:T(8,128)S(1)}, f32[4,2,16,8,128]{4,3,2,1,0:T(8,128)S(1)}) fusion(f32[16,128,2,128]{3,1,2,0:T(8,128)} %bitcast.54), kind=kLoop, calls=%fused_computation.14 | loop fusion | bytes 2097152
  8.6 0.8 copy.38
  9.4 3.6 %collective-permute-start.2 = (f32[4,128,256]{2,1,0:T(8,128)}, f32[4,128,256]{2,1,0:T(8,128)S(1)}, u32[]{:S(2)}, u32[]{:S(2)}) collective-permute-start(f32[4,128,256]{2,1,0:T(8,128)} %bitcast.53), channel_id=1, source_target_pairs={{0,8},{8,16},{16,24},{1,9},{9,17},{17,25},{2,10},{10,18},{18,26},{... | collective-permute-start | bytes 1572872 | tf_op jit(solution)/shard_map/ppermute | solution.py:20
  13.1 0.8 copy.37
  13.9 1.9 %collective-permute-start.3 = (f32[4,128,256]{2,1,0:T(8,128)}, f32[4,128,256]{2,1,0:T(8,128)S(1)}, u32[]{:S(2)}, u32[]{:S(2)}) collective-permute-start(f32[4,128,256]{2,1,0:T(8,128)} %bitcast.52), channel_id=1, source_target_pairs={{8,0},{16,8},{24,16},{9,1},{17,9},{25,17},{10,2},{18,10},{26,18},{... | collective-permute-start | bytes 1572872 | tf_op jit(solution)/shard_map/ppermute | solution.py:22
  15.9 1.8 %copy_bitcast_fusion = f32[16,128,256]{2,1,0:T(8,128)S(1)} fusion(f32[16,2,128,128]{3,2,1,0:T(8,128)} %param.7), kind=kLoop, calls=%fused_computation.5 | loop fusion | bytes 4194304 | tf_op jit(solution)/shard_map/reshape | solution.py:72
  17.8 0.1 copy.25
  17.9 0.1 reshape.61
  18.0 0.1 copy.24
  18.0 0.7 reshape.56.lidx_ref
  18.7 0.1 copy.27
  18.8 0.6 reshape.57.own_ref
  19.5 0.1 pad_add_fusion
  19.5 0.1 copy.26
  19.6 0.6 gather_fusion
  20.3 0.1 gather.15
  20.4 0.6 fusion.7.slot_ref
  21.0 3.6 %collective-permute-done.3 = f32[4,128,256]{2,1,0:T(8,128)S(1)} collective-permute-done((f32[4,128,256]{2,1,0:T(8,128)}, f32[4,128,256]{2,1,0:T(8,128)S(1)}, u32[]{:S(2)}, u32[]{:S(2)}) %collective-permute-start.3) | collective-permute-done | bytes 524320 | tf_op jit(solution)/shard_map/ppermute | solution.py:22
  24.6 1.9 %pad_maximum_fusion.ext_ref = f32[24,128,256]{2,1,0:T(8,128)} fusion(f32[4,128,256]{2,1,0:T(8,128)S(1)} %collective-permute-done.3, f32[16,128,256]{2,1,0:T(8,128)S(1)} %copy_bitcast_fusion, f32[4,128,256]{2,1,0:T(8,128)S(1)} %collective-permute-done.2), kind=kLoop, calls=%fused_computation.4 | loop fusion | flops 1572864 | bytes 6291456 | tf_op jit(solution)/shard_map/concatenate | solution.py:18
  26.5 42.1 %shard_map.55 = f32[3,9,128,128]{3,2,1,0:T(8,128)} custom-call(s32[128]{0:T(128)} %reshape.56.lidx_ref, s32[256]{0:T(256)} %fusion.7.slot_ref, s32[32]{0:T(128)} %reshape.57.own_ref, f32[16,8,128,128]{3,2,1,0:T(8,128)} %a_ref.1, f32[24,128,256]{2,1,0:T(8,128)} %pad_maximum_fusion.ext_ref), custom_call_target="tpu_custom_call" | custom-call | tf_op jit(solution)/shard_map/pallas_call | solution.py:101
  68.6 2.4 %fusion.17 = (f32[1,9,128,128]{3,2,1,0:T(8,128)S(1)}, f32[1,9,128,128]{3,2,1,0:T(8,128)}, f32[1,9,128,128]{3,2,1,0:T(8,128)S(1)}) fusion(f32[3,9,128,128]{3,2,1,0:T(8,128)} %shard_map.55), kind=kLoop, calls=%fused_computation.67 | loop fusion | bytes 3538944 | tf_op jit(solution)/shard_map/slice | solution.py:123
  71.0 1.2 %collective-permute-start.4 = (f32[1,9,128,128]{3,2,1,0:T(8,128)S(1)}, f32[1,9,128,128]{3,2,1,0:T(8,128)S(1)}, u32[]{:S(2)}, u32[]{:S(2)}) collective-permute-start(f32[1,9,128,128]{3,2,1,0:T(8,128)S(1)} %get-tuple-element.15), channel_id=1, source_target_pairs={{0,1},{1,2},{2,3},{3,4},{4,5},{5,6},{6,7},{7,0},{8,9},{9,10},{10,1... | collective-permute-start | bytes 1769480 | tf_op jit(solution)/shard_map/ppermute | solution.py:31
  72.2 3.0 %collective-permute-start.5 = (f32[1,9,128,128]{3,2,1,0:T(8,128)}, f32[1,9,128,128]{3,2,1,0:T(8,128)}, u32[]{:S(2)}, u32[]{:S(2)}) collective-permute-start(f32[1,9,128,128]{3,2,1,0:T(8,128)} %get-tuple-element.14), channel_id=1, source_target_pairs={{0,7},{1,0},{2,1},{3,2},{4,3},{5,4},{6,5},{7,6},{8,15},{9,8},{10,9... | collective-permute-start | bytes 1769480 | tf_op jit(solution)/shard_map/ppermute | solution.py:31
  75.3 0.6 gather_fusion.1
  75.9 17.1 %collective-permute-done.4 = f32[1,9,128,128]{3,2,1,0:T(8,128)S(1)} collective-permute-done((f32[1,9,128,128]{3,2,1,0:T(8,128)S(1)}, f32[1,9,128,128]{3,2,1,0:T(8,128)S(1)}, u32[]{:S(2)}, u32[]{:S(2)}) %collective-permute-start.4) | collective-permute-done | bytes 589856 | tf_op jit(solution)/shard_map/ppermute | solution.py:31
  93.0 0.6 gather_fusion.2
  93.6 1.9 %collective-permute-done.5 = f32[1,9,128,128]{3,2,1,0:T(8,128)} collective-permute-done((f32[1,9,128,128]{3,2,1,0:T(8,128)}, f32[1,9,128,128]{3,2,1,0:T(8,128)}, u32[]{:S(2)}, u32[]{:S(2)}) %collective-permute-start.5) | collective-permute-done | bytes 589856 | tf_op jit(solution)/shard_map/ppermute | solution.py:31
  95.5 1.7 %gather_fusion.3 = f32[15,128,128]{2,1,0:T(8,128)S(1)} fusion(f32[1,9,128,128]{3,2,1,0:T(8,128)} %collective-permute-done.5, s32[15]{0:T(128)S(1)} %or_bitcast_fusion), kind=kCustom, calls=%fused_computation.3 | custom fusion | bytes 1966200 | tf_op jit(solution)/shard_map/gather | solution.py:138
  97.2 1.2 %fusion = f32[1,15,128,128]{3,2,1,0:T(8,128)} fusion(f32[15,128,128]{2,1,0:T(8,128)S(1)} %gather_fusion.3, f32[15,128,128]{2,1,0:T(8,128)S(1)} %gather_fusion.2, f32[15,128,128]{2,1,0:T(8,128)S(1)} %gather_fusion.1, pred[15]{0:T(512)(128)(4,1)S(1)} %get-tuple-element.21, pred[15]{0:T(512)(128)(4,1)S(1)} %get-tuple-element.20, ...), kind=kLoop, calls=%fused_computation.7 | loop fusion | flops 1228800 | bytes 3932205 | tf_op jit(solution)/shard_map/add | solution.py:141
  (22 shorter events, 0.2 us)
Async XLA Ops:
  0.8 18.6 %collective-permute-start = (s32[4,2]{0,1:T(2,128)S(1)}, s32[4,2]{0,1:T(2,128)S(1)}, u32[]{:S(2)}, u32[]{:S(2)}) collective-permute-start(s32[4,2]{0,1:T(2,128)S(1)} %get-tuple-element.18), channel_id=1, source_target_pairs={{0,8},{8,16},{16,24},{1,9},{9,17},{17,25},{2,10},{10,18},{18,26},{... | collective-permute-start | bytes 104 | tf_op jit(solution)/shard_map/ppermute | solution.py:20
  5.4 14.1 %collective-permute-start.1 = (s32[4,2]{0,1:T(2,128)S(1)}, s32[4,2]{0,1:T(2,128)S(1)}, u32[]{:S(2)}, u32[]{:S(2)}) collective-permute-start(s32[4,2]{0,1:T(2,128)S(1)} %get-tuple-element.19), channel_id=1, source_target_pairs={{8,0},{16,8},{24,16},{9,1},{17,9},{25,17},{10,2},{18,10},{26,18},{... | collective-permute-start | bytes 104 | tf_op jit(solution)/shard_map/ppermute | solution.py:22
  7.3 8.6 %copy-start = (s32[16,2]{0,1:T(2,128)S(1)}, s32[16,2]{0,1:T(2,128)}, u32[]{:S(2)}) copy-start(s32[16,2]{0,1:T(2,128)} %param.8) | copy-start | bytes 388
  9.4 11.6 %collective-permute-start.2 = (f32[4,128,256]{2,1,0:T(8,128)}, f32[4,128,256]{2,1,0:T(8,128)S(1)}, u32[]{:S(2)}, u32[]{:S(2)}) collective-permute-start(f32[4,128,256]{2,1,0:T(8,128)} %bitcast.53), channel_id=1, source_target_pairs={{0,8},{8,16},{16,24},{1,9},{9,17},{17,25},{2,10},{10,18},{18,26},{... | collective-permute-start | bytes 1572872 | tf_op jit(solution)/shard_map/ppermute | solution.py:20
  13.9 10.7 %collective-permute-start.3 = (f32[4,128,256]{2,1,0:T(8,128)}, f32[4,128,256]{2,1,0:T(8,128)S(1)}, u32[]{:S(2)}, u32[]{:S(2)}) collective-permute-start(f32[4,128,256]{2,1,0:T(8,128)} %bitcast.52), channel_id=1, source_target_pairs={{8,0},{16,8},{24,16},{9,1},{17,9},{25,17},{10,2},{18,10},{26,18},{... | collective-permute-start | bytes 1572872 | tf_op jit(solution)/shard_map/ppermute | solution.py:22
  15.9 1.8 %copy-start.2 = (s32[1,15]{1,0:T(1,128)S(1)}, s32[1,15]{1,0:T(1,128)}, u32[]{:S(2)}) copy-start(s32[1,15]{1,0:T(1,128)} %param.9) | copy-start | bytes 184
  15.9 1.9 %copy-start.1 = (s32[16,8]{0,1:T(8,128)S(1)}, s32[16,8]{0,1:T(8,128)}, u32[]{:S(2)}) copy-start(s32[16,8]{0,1:T(8,128)} %param.6) | copy-start | bytes 1540
  71.0 22.0 %collective-permute-start.4 = (f32[1,9,128,128]{3,2,1,0:T(8,128)S(1)}, f32[1,9,128,128]{3,2,1,0:T(8,128)S(1)}, u32[]{:S(2)}, u32[]{:S(2)}) collective-permute-start(f32[1,9,128,128]{3,2,1,0:T(8,128)S(1)} %get-tuple-element.15), channel_id=1, source_target_pairs={{0,1},{1,2},{2,3},{3,4},{4,5},{5,6},{6,7},{7,0},{8,9},{9,10},{10,1... | collective-permute-start | bytes 1769480 | tf_op jit(solution)/shard_map/ppermute | solution.py:31
  72.2 23.3 %collective-permute-start.5 = (f32[1,9,128,128]{3,2,1,0:T(8,128)}, f32[1,9,128,128]{3,2,1,0:T(8,128)}, u32[]{:S(2)}, u32[]{:S(2)}) collective-permute-start(f32[1,9,128,128]{3,2,1,0:T(8,128)} %get-tuple-element.14), channel_id=1, source_target_pairs={{0,7},{1,0},{2,1},{3,2},{4,3},{5,4},{6,5},{7,6},{8,15},{9,8},{10,9... | collective-permute-start | bytes 1769480 | tf_op jit(solution)/shard_map/ppermute | solution.py:31

commit v2 on v1

--- a/solution.py
+++ b/solution.py
@@ -8,7 +8,6 @@
 from jax.sharding import PartitionSpec as P
 
 RIM = 4
-HIGHEST = lax.Precision.HIGHEST
 
 
 def extended(cells, axis, width):
@@ -31,31 +30,53 @@
     return lax.ppermute(value, axis, pairs)
 
 
-def triple_kernel(
-    coupling_slots, interp_slots, blocks, region, lidx_ref, slot_ref, own_ref, a_ref, ext_ref, out_ref, y_ref
-):
+def split(x):
+    hi = x.astype(jnp.bfloat16)
+    lo = (x - hi.astype(jnp.float32)).astype(jnp.bfloat16)
+    return hi, lo
+
+
+def dot3(x, y):
+    xh, xl = x
+    yh, yl = y
+    f32 = jnp.float32
+    return (
+        jnp.dot(xh, yh, preferred_element_type=f32)
+        + jnp.dot(xh, yl, preferred_element_type=f32)
+        + jnp.dot(xl, yh, preferred_element_type=f32)
+    )
+
+
+def triple_kernel(coupling_slots, interp_slots, blocks, region, idx_ref, a_ref, ext_ref, lo_ref, own_ref, hi_ref, y_ref, acc_ref):
     g = pl.program_id(0)
+    rows = pl.num_programs(0)
     bs = a_ref.shape[2]
+    slot_base = rows * coupling_slots
+    owner_base = slot_base + rows * coupling_slots * interp_slots
 
     @pl.when(g == 0)
     def _():
-        out_ref[...] = jnp.zeros_like(out_ref)
+        acc_ref[...] = jnp.zeros_like(acc_ref)
 
     y_ref[...] = jnp.zeros_like(y_ref)
     for a in range(coupling_slots):
-        row = lidx_ref[g * coupling_slots + a]
-        prod = jnp.dot(
-            a_ref[0, a], ext_ref[row], precision=HIGHEST, preferred_element_type=jnp.float32
-        )
+        row = idx_ref[g * coupling_slots + a]
+        prod = dot3(split(a_ref[0, a]), split(ext_ref[row]))
         for p in range(interp_slots):
-            slot = slot_ref[(g * coupling_slots + a) * interp_slots + p]
+            slot = idx_ref[slot_base + (g * coupling_slots + a) * interp_slots + p]
             y_ref[slot] += prod[:, p * bs : (p + 1) * bs]
-    pt = ext_ref[RIM + g].T
-    owners = [own_ref[g * interp_slots + q] for q in range(interp_slots)]
+    pt = split(ext_ref[RIM + g].T)
+    owners = [idx_ref[owner_base + g * interp_slots + q] for q in range(interp_slots)]
     for c in range(region):
-        res = jnp.dot(pt, y_ref[c], precision=HIGHEST, preferred_element_type=jnp.float32)
+        res = dot3(pt, split(y_ref[c]))
         for q in range(interp_slots):
-            out_ref[owners[q], c] += res[q * bs : (q + 1) * bs]
+            acc_ref[owners[q], c] += res[q * bs : (q + 1) * bs]
+
+    @pl.when(g == rows - 1)
+    def _():
+        lo_ref[...] = acc_ref[:blocks]
+        own_ref[...] = acc_ref[blocks : 2 * blocks]
+        hi_ref[...] = acc_ref[2 * blocks :]
 
 
 def shards(a_tiles, a_cols, p_tiles, p_cols, c_cols):
@@ -98,31 +119,32 @@
     owner = jnp.clip(relative * blocks + targets % blocks, 0, 3 * blocks - 1)
 
     kernel = functools.partial(triple_kernel, coupling_slots, interp_slots, blocks, region)
-    out = pl.pallas_call(
+    part = jax.ShapeDtypeStruct((blocks, region, bs, bs), jnp.float32)
+    part_spec = pl.BlockSpec((blocks, region, bs, bs), lambda g, *_: (0, 0, 0, 0))
+    table = jnp.concatenate(
+        [local_index.reshape(-1), slot.reshape(-1), owner.reshape(-1)]
+    ).astype(jnp.int32)
+    to_lower, own_part, to_upper = pl.pallas_call(
         kernel,
-        out_shape=jax.ShapeDtypeStruct((3 * blocks, region, bs, bs), jnp.float32),
+        out_shape=(part, part, part),
         grid_spec=pltpu.PrefetchScalarGridSpec(
-            num_scalar_prefetch=3,
+            num_scalar_prefetch=1,
             grid=(rows,),
             in_specs=[
                 pl.BlockSpec((1, coupling_slots, bs, bs), lambda g, *_: (g, 0, 0, 0)),
                 pl.BlockSpec(ext.shape, lambda g, *_: (0, 0, 0)),
             ],
-            out_specs=pl.BlockSpec((3 * blocks, region, bs, bs), lambda g, *_: (0, 0, 0, 0)),
-            scratch_shapes=[pltpu.VMEM((region, bs, bs), jnp.float32)],
+            out_specs=(part_spec, part_spec, part_spec),
+            scratch_shapes=[
+                pltpu.VMEM((region, bs, bs), jnp.float32),
+                pltpu.VMEM((3 * blocks, region, bs, bs), jnp.float32),
+            ],
         ),
         compiler_params=pltpu.CompilerParams(dimension_semantics=("arbitrary",)),
-    )(
-        local_index.reshape(-1).astype(jnp.int32),
-        slot.reshape(-1).astype(jnp.int32),
-        owner.reshape(-1).astype(jnp.int32),
-        a_tiles,
-        ext,
-    )
+    )(table, a_tiles, ext)
 
-    own_part = out[blocks : 2 * blocks]
-    from_lower = passed_along(out[2 * blocks :], "tile", 1)
-    from_upper = passed_along(out[:blocks], "tile", -1)
+    from_lower = passed_along(to_upper, "tile", 1)
+    from_upper = passed_along(to_lower, "tile", -1)
 
     c_slab = c_cols // (tiles * blocks)
     c_tile = (c_cols // blocks) % tiles

time: 98.8 us -> 80.2 us (0.81)
  Pallas kernels: 42.1 us -> 25.9 us
  local copies, waits for them, and re-layouts: 13.4 us -> 9.9 us
  other arithmetic: 3.92 us -> 6.25 us
  waiting for transfers between devices: 22.6 us -> 21.4 us
    pallas_call x1, Pallas kernels: 42.1 us -> 25.9 us  [shards(): pl.pallas_call(kernel, out_shape=(part, part, part), grid_spec=pltpu.Pref...]
    slice x1 -> x0, local copies, waits for them, and re-layouts: 2.37 us -> none  [shards(): own_part = out[blocks:2 * blocks]]
    broadcast_in_dim x2, other arithmetic: 0.03 us -> 1.15 us  [pick(): tiles_picked = part[r_idx, idx]]
    reshape x2, local copies, waits for them, and re-layouts: 1.28 us -> 0.18 us  [the longest x1 0.09 us: shards(): local_index.reshape(-1)]
  transfers between devices with their start and end apart: 6 -> 6, of which waited for: 3 -> 3; matrix products, arithmetic and copies ran while one was open for 9% -> 14% of each run, Pallas kernels for 0% -> 0%
where the time goes in v2:
time: 80.2 us; the launch traced here: 79.9 us
  Pallas kernels  25.9 us (32%)
  waiting for transfers between devices  21.4 us (27%)
  starting transfers between devices  16.2 us (20%)
  local copies, waits for them, and re-layouts  9.9 us (12%)
  other arithmetic  6.25 us (8%)
    pallas_call x1, Pallas kernels, shards(): pl.pallas_call(kernel, out_shape=(part, part, part), grid_spec=pltpu.Pref...  25.9 us
    ppermute x2, waiting for transfers between devices, passed_along(): return lax.ppermute(value, axis, pairs)  18.4 us
    ppermute x2, starting transfers between devices, extended(): lax.ppermute(tail, axis, [(i, i + 1) for i in range(count - 1)])  8.16 us
    ppermute x2, starting transfers between devices, passed_along(): return lax.ppermute(value, axis, pairs)  4.25 us
    ppermute x2, starting transfers between devices, extended(): lax.ppermute(head, axis, [(i + 1, i) for i in range(count - 1)])  3.83 us
    ppermute x2, waiting for transfers between devices, extended(): lax.ppermute(head, axis, [(i + 1, i) for i in range(count - 1)])  3.05 us
    gather x3, local copies, waits for them, and re-layouts, pick(): tiles_picked = part[r_idx, idx]  2.9 us
    concatenate x2, other arithmetic, extended(): jnp.concatenate([lax.ppermute(tail, axis, [(i, i + 1) for i in range(coun...  1.96 us
  transfers between devices with their start and end apart: 6, of which 3 were waited for; matrix products, arithmetic and copies ran while one was open for 14% of the time, Pallas kernels for 0%

profile of v2, /device:TPU:1, one launch (start us, length us, event | category | flops | bytes accessed | tf_op | source)
XLA Modules:
  0.0 79.9 jit_solution(12821737604566254264)
XLA Ops:
  0.0 0.8 %fusion.17 = (s32[4,2]{0,1:T(2,128)S(1)}, s32[4,2]{0,1:T(2,128)S(1)}) fusion(s32[16,2]{0,1:T(2,128)} %param.8), kind=kLoop, calls=%fused_computation.68 | loop fusion | bytes 128 | tf_op jit(solution)/shard_map/slice | solution.py:16
  0.8 4.5 %collective-permute-start = (s32[4,2]{0,1:T(2,128)S(1)}, s32[4,2]{0,1:T(2,128)S(1)}, u32[]{:S(2)}, u32[]{:S(2)}) collective-permute-start(s32[4,2]{0,1:T(2,128)S(1)} %get-tuple-element.21), channel_id=1, source_target_pairs={{0,8},{8,16},{16,24},{1,9},{9,17},{17,25},{2,10},{10,18},{18,26},{... | collective-permute-start | bytes 104 | tf_op jit(solution)/shard_map/ppermute | solution.py:19
  5.4 1.9 %collective-permute-start.1 = (s32[4,2]{0,1:T(2,128)S(1)}, s32[4,2]{0,1:T(2,128)S(1)}, u32[]{:S(2)}, u32[]{:S(2)}) collective-permute-start(s32[4,2]{0,1:T(2,128)S(1)} %get-tuple-element.22), channel_id=1, source_target_pairs={{8,0},{16,8},{24,16},{9,1},{17,9},{25,17},{10,2},{18,10},{26,18},{... | collective-permute-start | bytes 104 | tf_op jit(solution)/shard_map/ppermute | solution.py:21
  7.3 1.3 %slice_bitcast_fusion.1 = (f32[4,2,16,8,128]{4,3,2,1,0:T(8,128)S(1)}, f32[4,2,16,8,128]{4,3,2,1,0:T(8,128)S(1)}) fusion(f32[16,128,2,128]{3,1,2,0:T(8,128)} %bitcast.54), kind=kLoop, calls=%fused_computation.14 | loop fusion | bytes 2097152
  8.6 0.9 %copy.38 = f32[4,2,16,8,128]{4,3,1,2,0:T(8,128)} copy(f32[4,2,16,8,128]{4,3,2,1,0:T(8,128)S(1)} %get-tuple-element.17) | data formatting | bytes 1048576 | tf_op jit(solution)/shard_map/slice | solution.py:16
  9.5 3.6 %collective-permute-start.2 = (f32[4,128,256]{2,1,0:T(8,128)}, f32[4,128,256]{2,1,0:T(8,128)S(1)}, u32[]{:S(2)}, u32[]{:S(2)}) collective-permute-start(f32[4,128,256]{2,1,0:T(8,128)} %bitcast.53), channel_id=1, source_target_pairs={{0,8},{8,16},{16,24},{1,9},{9,17},{17,25},{2,10},{10,18},{18,26},{... | collective-permute-start | bytes 1572872 | tf_op jit(solution)/shard_map/ppermute | solution.py:19
  13.1 0.8 %copy.37 = f32[4,2,16,8,128]{4,3,1,2,0:T(8,128)} copy(f32[4,2,16,8,128]{4,3,2,1,0:T(8,128)S(1)} %get-tuple-element.18) | data formatting | bytes 1048576 | tf_op jit(solution)/shard_map/slice | solution.py:15
  13.9 1.9 %collective-permute-start.3 = (f32[4,128,256]{2,1,0:T(8,128)}, f32[4,128,256]{2,1,0:T(8,128)S(1)}, u32[]{:S(2)}, u32[]{:S(2)}) collective-permute-start(f32[4,128,256]{2,1,0:T(8,128)} %bitcast.52), channel_id=1, source_target_pairs={{8,0},{16,8},{24,16},{9,1},{17,9},{25,17},{10,2},{18,10},{26,18},{... | collective-permute-start | bytes 1572872 | tf_op jit(solution)/shard_map/ppermute | solution.py:21
  15.9 1.8 %copy_bitcast_fusion = f32[16,128,256]{2,1,0:T(8,128)S(1)} fusion(f32[16,2,128,128]{3,2,1,0:T(8,128)} %param.7), kind=kLoop, calls=%fused_computation.5 | loop fusion | bytes 4194304 | tf_op jit(solution)/shard_map/reshape | solution.py:93
  17.7 0.6 fusion.13
  18.3 0.6 and_bitcast_fusion.1
  19.0 0.1 reshape.61
  19.1 0.1 reshape.56
  19.2 0.1 copy.27
  19.3 0.1 reshape.57
  19.4 0.6 fusion.14
  20.0 0.1 pad_add_fusion.1
  20.1 0.1 copy.26
  20.2 0.6 gather_fusion
  20.8 0.1 gather.15
  21.0 0.6 pad_add_fusion.idx_ref
  21.6 3.0 %collective-permute-done.3 = f32[4,128,256]{2,1,0:T(8,128)S(1)} collective-permute-done((f32[4,128,256]{2,1,0:T(8,128)}, f32[4,128,256]{2,1,0:T(8,128)S(1)}, u32[]{:S(2)}, u32[]{:S(2)}) %collective-permute-start.3) | collective-permute-done | bytes 524320 | tf_op jit(solution)/shard_map/ppermute | solution.py:21
  24.6 1.9 %pad_maximum_fusion.ext_ref = f32[24,128,256]{2,1,0:T(8,128)} fusion(f32[4,128,256]{2,1,0:T(8,128)S(1)} %collective-permute-done.3, f32[16,128,256]{2,1,0:T(8,128)S(1)} %copy_bitcast_fusion, f32[4,128,256]{2,1,0:T(8,128)S(1)} %collective-permute-done.2), kind=kLoop, calls=%fused_computation.4 | loop fusion | flops 1572864 | bytes 6291456 | tf_op jit(solution)/shard_map/concatenate | solution.py:17
  26.5 25.9 %shard_map.55 = (f32[1,9,128,128]{3,2,1,0:T(8,128)}, f32[1,9,128,128]{3,2,1,0:T(8,128)}, f32[1,9,128,128]{3,2,1,0:T(8,128)}) custom-call(s32[416]{0:T(512)} %pad_add_fusion.idx_ref, f32[16,8,128,128]{3,2,1,0:T(8,128)} %a_ref.1, f32[24,128,256]{2,1,0:T(8,128)} %pad_maximum_fusion.ext_ref), custom_call_target="tpu_custom_call" | custom-call | tf_op jit(solution)/shard_map/pallas_call | solution.py:127
  52.4 1.2 %collective-permute-start.4 = (f32[1,9,128,128]{3,2,1,0:T(8,128)}, f32[1,9,128,128]{3,2,1,0:T(8,128)S(1)}, u32[]{:S(2)}, u32[]{:S(2)}) collective-permute-start(f32[1,9,128,128]{3,2,1,0:T(8,128)} %get-tuple-element.9), channel_id=1, source_target_pairs={{0,1},{1,2},{2,3},{3,4},{4,5},{5,6},{6,7},{7,0},{8,9},{9,10},{10,1... | collective-permute-start | bytes 1769480 | tf_op jit(solution)/shard_map/ppermute | solution.py:30
  53.6 3.0 %collective-permute-start.5 = (f32[1,9,128,128]{3,2,1,0:T(8,128)}, f32[1,9,128,128]{3,2,1,0:T(8,128)S(1)}, u32[]{:S(2)}, u32[]{:S(2)}) collective-permute-start(f32[1,9,128,128]{3,2,1,0:T(8,128)} %get-tuple-element.10), channel_id=1, source_target_pairs={{0,7},{1,0},{2,1},{3,2},{4,3},{5,4},{6,5},{7,6},{8,15},{9,8},{10,9... | collective-permute-start | bytes 1769480 | tf_op jit(solution)/shard_map/ppermute | solution.py:30
  56.7 1.7 %gather_fusion.1 = f32[15,128,128]{2,1,0:T(8,128)S(1)} fusion(f32[1,9,128,128]{3,2,1,0:T(8,128)} %get-tuple-element.8, s32[15]{0:T(128)S(1)} %or_bitcast_fusion.2), kind=kCustom, calls=%fused_computation.1 | custom fusion | bytes 1966200 | tf_op jit(solution)/shard_map/gather | solution.py:160
  58.4 16.9 %collective-permute-done.4 = f32[1,9,128,128]{3,2,1,0:T(8,128)S(1)} collective-permute-done((f32[1,9,128,128]{3,2,1,0:T(8,128)}, f32[1,9,128,128]{3,2,1,0:T(8,128)S(1)}, u32[]{:S(2)}, u32[]{:S(2)}) %collective-permute-start.4) | collective-permute-done | bytes 589856 | tf_op jit(solution)/shard_map/ppermute | solution.py:30
  75.3 0.6 gather_fusion.2
  75.9 1.5 %collective-permute-done.5 = f32[1,9,128,128]{3,2,1,0:T(8,128)S(1)} collective-permute-done((f32[1,9,128,128]{3,2,1,0:T(8,128)}, f32[1,9,128,128]{3,2,1,0:T(8,128)S(1)}, u32[]{:S(2)}, u32[]{:S(2)}) %collective-permute-start.5) | collective-permute-done | bytes 589856 | tf_op jit(solution)/shard_map/ppermute | solution.py:30
  77.4 0.6 gather_fusion.3
  78.0 1.9 %fusion = f32[1,15,128,128]{3,2,1,0:T(8,128)} fusion(f32[15,128,128]{2,1,0:T(8,128)S(1)} %gather_fusion.3, f32[15,128,128]{2,1,0:T(8,128)S(1)} %gather_fusion.2, f32[15,128,128]{2,1,0:T(8,128)S(1)} %gather_fusion.1, pred[15]{0:T(512)(128)(4,1)} %get-tuple-element.24, pred[15]{0:T(512)(128)(4,1)S(1)} %get-tuple-element.23, pred[15]{0:T(512)(128)(4,1)S(1)} %get-tuple-element.11), kind=kLoop, calls=%fused_computation.7 | loop fusion | flops 1228800 | bytes 3932205 | tf_op jit(solution)/shard_map/add | solution.py:163
  (26 shorter events, 0.3 us)
Async XLA Ops:
  0.8 19.2 %collective-permute-start = (s32[4,2]{0,1:T(2,128)S(1)}, s32[4,2]{0,1:T(2,128)S(1)}, u32[]{:S(2)}, u32[]{:S(2)}) collective-permute-start(s32[4,2]{0,1:T(2,128)S(1)} %get-tuple-element.21), channel_id=1, source_target_pairs={{0,8},{8,16},{16,24},{1,9},{9,17},{17,25},{2,10},{10,18},{18,26},{... | collective-permute-start | bytes 104 | tf_op jit(solution)/shard_map/ppermute | solution.py:19
  5.4 14.7 %collective-permute-start.1 = (s32[4,2]{0,1:T(2,128)S(1)}, s32[4,2]{0,1:T(2,128)S(1)}, u32[]{:S(2)}, u32[]{:S(2)}) collective-permute-start(s32[4,2]{0,1:T(2,128)S(1)} %get-tuple-element.22), channel_id=1, source_target_pairs={{8,0},{16,8},{24,16},{9,1},{17,9},{25,17},{10,2},{18,10},{26,18},{... | collective-permute-start | bytes 104 | tf_op jit(solution)/shard_map/ppermute | solution.py:21
  7.3 8.6 %copy-start = (s32[16,2]{0,1:T(2,128)S(1)}, s32[16,2]{0,1:T(2,128)}, u32[]{:S(2)}) copy-start(s32[16,2]{0,1:T(2,128)} %param.8) | copy-start | bytes 388
  9.5 12.1 %collective-permute-start.2 = (f32[4,128,256]{2,1,0:T(8,128)}, f32[4,128,256]{2,1,0:T(8,128)S(1)}, u32[]{:S(2)}, u32[]{:S(2)}) collective-permute-start(f32[4,128,256]{2,1,0:T(8,128)} %bitcast.53), channel_id=1, source_target_pairs={{0,8},{8,16},{16,24},{1,9},{9,17},{17,25},{2,10},{10,18},{18,26},{... | collective-permute-start | bytes 1572872 | tf_op jit(solution)/shard_map/ppermute | solution.py:19
  13.9 10.7 %collective-permute-start.3 = (f32[4,128,256]{2,1,0:T(8,128)}, f32[4,128,256]{2,1,0:T(8,128)S(1)}, u32[]{:S(2)}, u32[]{:S(2)}) collective-permute-start(f32[4,128,256]{2,1,0:T(8,128)} %bitcast.52), channel_id=1, source_target_pairs={{8,0},{16,8},{24,16},{9,1},{17,9},{25,17},{10,2},{18,10},{26,18},{... | collective-permute-start | bytes 1572872 | tf_op jit(solution)/shard_map/ppermute | solution.py:21
  15.9 1.8 %copy-start.2 = (s32[1,15]{1,0:T(1,128)S(1)}, s32[1,15]{1,0:T(1,128)}, u32[]{:S(2)}) copy-start(s32[1,15]{1,0:T(1,128)} %param.9) | copy-start | bytes 184
  15.9 3.0 %copy-start.1 = (s32[16,8]{0,1:T(8,128)S(1)}, s32[16,8]{0,1:T(8,128)}, u32[]{:S(2)}) copy-start(s32[16,8]{0,1:T(8,128)} %param.6) | copy-start | bytes 1540
  26.5 30.1 %copy-start.4 = (s32[1,15,1]{1,2,0:T(1,128)S(1)}, s32[1,15,1]{1,2,0:T(1,128)}, u32[]{:S(2)}) copy-start(s32[1,15,1]{1,2,0:T(1,128)} %get-tuple-element.20) | copy-start | bytes 184
  26.5 30.1 %copy-start.3 = (s32[1,15,1]{1,2,0:T(1,128)S(1)}, s32[1,15,1]{1,2,0:T(1,128)}, u32[]{:S(2)}) copy-start(s32[1,15,1]{1,2,0:T(1,128)} %get-tuple-element.13) | copy-start | bytes 184
  52.4 22.9 %collective-permute-start.4 = (f32[1,9,128,128]{3,2,1,0:T(8,128)}, f32[1,9,128,128]{3,2,1,0:T(8,128)S(1)}, u32[]{:S(2)}, u32[]{:S(2)}) collective-permute-start(f32[1,9,128,128]{3,2,1,0:T(8,128)} %get-tuple-element.9), channel_id=1, source_target_pairs={{0,1},{1,2},{2,3},{3,4},{4,5},{5,6},{6,7},{7,0},{8,9},{9,10},{10,1... | collective-permute-start | bytes 1769480 | tf_op jit(solution)/shard_map/ppermute | solution.py:30
  53.6 23.8 %collective-permute-start.5 = (f32[1,9,128,128]{3,2,1,0:T(8,128)}, f32[1,9,128,128]{3,2,1,0:T(8,128)S(1)}, u32[]{:S(2)}, u32[]{:S(2)}) collective-permute-start(f32[1,9,128,128]{3,2,1,0:T(8,128)} %get-tuple-element.10), channel_id=1, source_target_pairs={{0,7},{1,0},{2,1},{3,2},{4,3},{5,4},{6,5},{7,6},{8,15},{9,8},{10,9... | collective-permute-start | bytes 1769480 | tf_op jit(solution)/shard_map/ppermute | solution.py:30

commit v3 on v2

v3 whole, which is shorter than its diff:
```python
import functools

import jax
import jax.numpy as jnp
from jax import lax
from jax.experimental import pallas as pl
from jax.experimental.pallas import tpu as pltpu
from jax.sharding import PartitionSpec as P

RIM = 4


def passed_along(value, axis, steps):
    count = lax.axis_size(axis)
    pairs = [(source, (source + steps) % count) for source in range(count)]
    return lax.ppermute(value, axis, pairs)


def split(x):
    hi = x.astype(jnp.bfloat16)
    lo = (x - hi.astype(jnp.float32)).astype(jnp.bfloat16)
    return hi, lo


def dot3(x, y):
    xh, xl = x
    yh, yl = y
    f32 = jnp.float32
    return (
        jnp.dot(xh, yh, preferred_element_type=f32)
        + jnp.dot(xh, yl, preferred_element_type=f32)
        + jnp.dot(xl, yh, preferred_element_type=f32)
    )


def slab_kernel(
    coupling_slots, interp_slots, blocks,
    tbl_ref, a_ref, prow_ref, pown_ref, lo_ref, own_ref, hi_ref,
    y_ref, ph_ref, pl_ref, acc_ref,
):
    g = pl.program_id(0)
    rows = pl.num_programs(0)
    bs = a_ref.shape[2]
    slots = 3 * blocks
    slot_base = rows * coupling_slots
    owner_base = slot_base + rows * coupling_slots * interp_slots
    nz_base = owner_base + rows * interp_slots

    @pl.when(g == 0)
    def _():
        acc_ref[...] = jnp.zeros_like(acc_ref)

        def body(r, carry):
            hi, lo = split(prow_ref[r])
            ph_ref[r] = hi
            pl_ref[r] = lo
            return carry

        lax.fori_loop(0, prow_ref.shape[0], body, 0)

    y_ref[...] = jnp.zeros_like(y_ref)
    for a in range(coupling_slots):
        row = tbl_ref[g * coupling_slots + a]

        @pl.when(row >= 0)
        def _():
            ahl = split(a_ref[0, a])
            j = jnp.maximum(row, 0)
            for p in range(interp_slots):
                prod = dot3(ahl, (ph_ref[j, p], pl_ref[j, p]))
                slot = tbl_ref[slot_base + (g * coupling_slots + a) * interp_slots + p]
                y_ref[slot] += prod

    pt = split(jnp.concatenate([pown_ref[0, q].T for q in range(interp_slots)], axis=0))
    owners = [tbl_ref[owner_base + g * interp_slots + q] for q in range(interp_slots)]
    for c in range(slots):

        @pl.when(tbl_ref[nz_base + g * slots + c] != 0)
        def _():
            res = dot3(pt, split(y_ref[c]))
            for q in range(interp_slots):
                acc_ref[owners[q], c] += res[q * bs : (q + 1) * bs]

    @pl.when(g == rows - 1)
    def _():
        lo_ref[...] = acc_ref[:blocks]
        own_ref[...] = acc_ref[blocks : 2 * blocks]
        hi_ref[...] = acc_ref[2 * blocks :]


def slab_call(table, a_tiles, prow, p_tiles, blocks):
    rows, coupling_slots, bs, _ = a_tiles.shape
    interp_slots = p_tiles.shape[1]
    slots = 3 * blocks
    part = jax.ShapeDtypeStruct((blocks, slots, bs, bs), jnp.float32)
    part_spec = pl.BlockSpec((blocks, slots, bs, bs), lambda g, *_: (0, 0, 0, 0))
    kernel = functools.partial(slab_kernel, coupling_slots, interp_slots, blocks)
    return pl.pallas_call(
        kernel,
        out_shape=(part, part, part),
        grid_spec=pltpu.PrefetchScalarGridSpec(
            num_scalar_prefetch=1,
            grid=(rows,),
            in_specs=[
                pl.BlockSpec((1, coupling_slots, bs, bs), lambda g, *_: (g, 0, 0, 0)),
                pl.BlockSpec(prow.shape, lambda g, *_: (0, 0, 0, 0)),
                pl.BlockSpec((1, interp_slots, bs, bs), lambda g, *_: (g, 0, 0, 0)),
            ],
            out_specs=(part_spec, part_spec, part_spec),
            scratch_shapes=[
                pltpu.VMEM((slots, bs, bs), jnp.float32),
                pltpu.VMEM(prow.shape, jnp.bfloat16),
                pltpu.VMEM(prow.shape, jnp.bfloat16),
                pltpu.VMEM((3 * blocks, slots, bs, bs), jnp.float32),
            ],
        ),
        compiler_params=pltpu.CompilerParams(dimension_semantics=("arbitrary",)),
    )(table, a_tiles, prow, p_tiles)


def shards(a_tiles, a_cols, p_tiles, p_cols, c_cols):
    rows, coupling_slots, bs, _ = a_tiles.shape
    interp_slots = p_tiles.shape[1]
    blocks, pattern_slots = c_cols.shape
    tiles = lax.axis_size("tile")
    slabs = lax.axis_size("slab")
    t = lax.axis_index("tile")
    s = lax.axis_index("slab")
    device = s * tiles + t
    slots = 3 * blocks

    up = [(i, i + 1) for i in range(slabs - 1)]
    down = [(i + 1, i) for i in range(slabs - 1)]
    lower_p, lower_keys = lax.ppermute((p_tiles[rows - RIM :], p_cols[rows - RIM :]), "slab", up)
    upper_p, upper_keys = lax.ppermute((p_tiles[:RIM], p_cols[:RIM]), "slab", down)

    targets = p_cols - s * tiles * blocks
    relative = jnp.remainder(targets // blocks - t + 1, tiles)
    owner = jnp.clip(relative * blocks + targets % blocks, 0, 3 * blocks - 1)

    own_base = device * rows
    lower_base = (device - tiles) * rows + rows - RIM
    upper_base = (device + tiles) * rows
    groups = (
        (a_cols < own_base, a_cols - lower_base, RIM, lower_p, lower_keys),
        ((a_cols >= own_base) & (a_cols < own_base + rows), a_cols - own_base, rows, p_tiles, p_cols),
        (a_cols >= own_base + rows, a_cols - upper_base, RIM, upper_p, upper_keys),
    )
    parts = []
    for inside, local, count, prow, pkeys in groups:
        local = jnp.clip(local, 0, count - 1)
        keys = pkeys[local]
        k_tile = (keys // blocks) % tiles
        slot = ((k_tile - t + 1) % tiles) * blocks + keys % blocks
        slot = jnp.where(inside[:, :, None], jnp.clip(slot, 0, slots - 1), 0)
        hit = inside[:, :, None, None] & (slot[:, :, :, None] == jnp.arange(slots, dtype=jnp.int32))
        nonzero = jnp.any(hit, axis=(1, 2))
        table = jnp.concatenate(
            [
                jnp.where(inside, local, -1).reshape(-1),
                slot.reshape(-1),
                owner.reshape(-1),
                nonzero.astype(jnp.int32).reshape(-1),
            ]
        ).astype(jnp.int32)
        parts.append(slab_call(table, a_tiles, prow, p_tiles, blocks))

    to_lower = [part[0] for part in parts]
    own_part = jnp.concatenate([part[1] for part in parts], axis=1)
    from_lower = jnp.concatenate([passed_along(part[2], "tile", 1) for part in parts], axis=1)
    from_upper = jnp.concatenate([passed_along(x, "tile", -1) for x in to_lower], axis=1)

    region = 9 * blocks
    c_slab = c_cols // (tiles * blocks)
    c_tile = (c_cols // blocks) % tiles
    c_w = c_cols % blocks
    c_ds = (c_slab - s + 1) % slabs - 1
    c_dt = (c_tile - t + 2) % tiles - 2
    base = (c_ds + 1) * 3
    r_idx = jnp.arange(blocks, dtype=jnp.int32)[:, None]

    def pick(part, dt):
        valid = (dt >= -1) & (dt <= 1)
        idx = jnp.clip((base + dt + 1) * blocks + c_w, 0, region - 1)
        tiles_picked = part[r_idx, idx]
        return jnp.where(valid[:, :, None, None], tiles_picked, 0.0)

    return pick(own_part, c_dt) + pick(from_lower, c_dt + 1) + pick(from_upper, c_dt - 1)


def solution(mesh):
    return jax.shard_map(
        shards,
        mesh=mesh,
        in_specs=(
            P(("slab", "tile"), None, None, None),
            P(("slab", "tile"), None),
            P(("slab", "tile"), None, None, None),
            P(("slab", "tile"), None),
            P(("slab", "tile"), None),
        ),
        out_specs=P(("slab", "tile"), None, None, None),
        check_vma=False,
    )
```

time: 80.2 us -> 119 us (1.48)
  Pallas kernels: 25.9 us -> 75 us
  waiting for transfers between devices: 21.4 us -> 10.3 us
  other arithmetic: 6.25 us -> 3.47 us
  starting transfers between devices: 16.2 us -> 17.7 us
    pallas_call x1 -> x3, Pallas kernels: 25.9 us -> 75 us  [slab_call(): pl.pallas_call(kernel, out_shape=(part, part, part), grid_spec=pltpu.Pref...]
    ppermute x2 -> x6, waiting for transfers between devices: 18.4 us -> 10.2 us  [passed_along(): return lax.ppermute(value, axis, pairs)]
    ppermute x4, waiting for transfers between devices: 3.05 us -> 0.01 us  [the longest x2 0.01 us: shards(): lax.ppermute((p_tiles[rows - RIM:], p_cols[rows - RIM:]), 'slab', up)]
    ppermute x2 -> x6, starting transfers between devices: 4.25 us -> 6.86 us  [passed_along(): return lax.ppermute(value, axis, pairs)]
    reshape x2 -> x3, local copies, waits for them, and re-layouts: 1.87 us -> 0.27 us  [shards(): jnp.where(inside, local, -1).reshape(-1)]
    gather x2 -> x6, local copies, waits for them, and re-layouts: 0.78 us -> 2.35 us  [shards(): keys = pkeys[local]]
    slice x3 -> x2, local copies, waits for them, and re-layouts: 2.51 us -> 1.28 us  [the longest x1 1.27 us: shards(): p_tiles[rows - RIM:]]
    unnamed x11 -> x15, local copies, waits for them, and re-layouts: 1.32 us -> 2.42 us
  transfers between devices with their start and end apart: 6 -> 10, of which waited for: 3 -> 2; matrix products, arithmetic and copies ran while one was open for 14% -> 9% of each run, Pallas kernels for 0% -> 64%
where the time goes in v3:
time: 119 us; the launch traced here: 118 us
  Pallas kernels  75 us (63%)
  starting transfers between devices  17.7 us (15%)
  local copies, waits for them, and re-layouts  10.9 us (9%)
  waiting for transfers between devices  10.3 us (9%)
  other arithmetic  3.47 us (3%)
    pallas_call x3, Pallas kernels, slab_call(): pl.pallas_call(kernel, out_shape=(part, part, part), grid_spec=pltpu.Pref...  75 us
    ppermute x6, waiting for transfers between devices, passed_along(): return lax.ppermute(value, axis, pairs)  10.2 us
    ppermute x2, starting transfers between devices, shards(): lax.ppermute((p_tiles[rows - RIM:], p_cols[rows - RIM:]), 'slab', up)  6.89 us
    ppermute x6, starting transfers between devices, passed_along(): return lax.ppermute(value, axis, pairs)  6.86 us
    ppermute x2, starting transfers between devices, shards(): lax.ppermute((p_tiles[:RIM], p_cols[:RIM]), 'slab', down)  3.91 us
    unnamed x15, local copies, waits for them, and re-layouts  2.42 us
  transfers between devices with their start and end apart: 10, of which 2 were waited for; matrix products, arithmetic and copies ran while one was open for 9% of the time, Pallas kernels for 64%

profile of v3, /device:TPU:1, one launch (start us, length us, event | category | flops | bytes accessed | tf_op | source)
XLA Modules:
  0.0 117.7 jit_solution(16467560027239736697)
XLA Ops:
  0.0 0.8 copy.40
  0.8 2.0 %collective-permute-start.2 = (s32[4,2]{1,0:T(4,128)S(1)}, s32[4,2]{1,0:T(4,128)S(1)}, u32[]{:S(2)}, u32[]{:S(2)}) collective-permute-start(s32[4,2]{1,0:T(4,128)S(1)} %get-tuple-element.30), channel_id=1, source_target_pairs={{8,0},{16,8},{24,16},{9,1},{17,9},{25,17},{10,2},{18,10},{26,18},{... | collective-permute-start | bytes 104 | tf_op jit(solution)/shard_map/ppermute | solution.py:135
  2.8 4.5 %collective-permute-start = (s32[4,2]{1,0:T(4,128)S(1)}, s32[4,2]{1,0:T(4,128)S(1)}, u32[]{:S(2)}, u32[]{:S(2)}) collective-permute-start(s32[4,2]{1,0:T(4,128)S(1)} %get-tuple-element.29), channel_id=1, source_target_pairs={{0,8},{8,16},{16,24},{1,9},{9,17},{17,25},{2,10},{10,18},{18,26},{... | collective-permute-start | bytes 104 | tf_op jit(solution)/shard_map/ppermute | solution.py:134
  7.3 1.3 %fusion.61 = (f32[4,2,128,128]{3,2,1,0:T(8,128)S(1)}, f32[4,2,128,128]{3,2,1,0:T(8,128)S(1)}) fusion(f32[16,2,128,128]{3,2,1,0:T(8,128)} %pown_ref.5), kind=kLoop, calls=%fused_computation.152 | loop fusion | bytes 2097152 | tf_op jit(solution)/shard_map/slice | solution.py:134
  8.6 2.4 %collective-permute-start.1 = (f32[4,2,128,128]{3,2,1,0:T(8,128)S(1)}, f32[4,2,128,128]{3,2,1,0:T(8,128)S(1)}, u32[]{:S(2)}, u32[]{:S(2)}) collective-permute-start(f32[4,2,128,128]{3,2,1,0:T(8,128)S(1)} %get-tuple-element.27), channel_id=1, source_target_pairs={{0,8},{8,16},{16,24},{1,9},{9,17},{17,25},{2,10},{10,18},{18,26},{... | collective-permute-start | bytes 1572872 | tf_op jit(solution)/shard_map/ppermute | solution.py:134
  11.0 2.0 %collective-permute-start.3 = (f32[4,2,128,128]{3,2,1,0:T(8,128)S(1)}, f32[4,2,128,128]{3,2,1,0:T(8,128)S(1)}, u32[]{:S(2)}, u32[]{:S(2)}) collective-permute-start(f32[4,2,128,128]{3,2,1,0:T(8,128)S(1)} %get-tuple-element.28), channel_id=1, source_target_pairs={{8,0},{16,8},{24,16},{9,1},{17,9},{25,17},{10,2},{18,10},{26,18},{... | collective-permute-start | bytes 1572872 | tf_op jit(solution)/shard_map/ppermute | solution.py:135
  13.8 0.6 gather_fusion.1
  14.5 0.1 gather.27
  14.7 0.1 broadcast_in_dim.101
  15.1 0.1 broadcast_in_dim.104
  15.7 0.1 broadcast_in_dim.107
  16.6 0.6 gather_fusion
  17.3 0.1 gather.25
  17.4 0.6 gather_fusion.2
  18.1 0.1 fusion.7
  18.2 0.1 gather.29
  19.1 0.7 fusion.29
  19.8 33.9 %shard_map.56 = (f32[1,3,128,128]{3,2,1,0:T(8,128)}, f32[1,3,128,128]{3,2,1,0:T(8,128)}, f32[1,3,128,128]{3,2,1,0:T(8,128)}) custom-call(s32[464]{0:T(512)} %get-tuple-element.45.tbl_ref, f32[16,8,128,128]{3,2,1,0:T(8,128)} %a_ref.5, f32[16,2,128,128]{3,2,1,0:T(8,128)} %pown_ref.5, f32[16,2,128,128]{3,2,1,0:T(8,128)} %pown_ref.5), custom_call_target="tpu_custom_call" | custom-call | tf_op jit(solution)/shard_map/pallas_call | solution.py:98
  53.7 2.3 %collective-permute-start.5 = (f32[1,3,128,128]{3,2,1,0:T(8,128)}, f32[1,3,128,128]{3,2,1,0:T(8,128)S(1)}, u32[]{:S(2)}, u32[]{:S(2)}) collective-permute-start(f32[1,3,128,128]{3,2,1,0:T(8,128)} %get-tuple-element.18), channel_id=1, source_target_pairs={{0,1},{1,2},{2,3},{3,4},{4,5},{5,6},{6,7},{7,0},{8,9},{9,10},{10,1... | collective-permute-start | bytes 589832 | tf_op jit(solution)/shard_map/ppermute | solution.py:16
  55.9 0.8 copy-done.1
  56.7 20.1 %shard_map.55 = (f32[1,3,128,128]{3,2,1,0:T(8,128)}, f32[1,3,128,128]{3,2,1,0:T(8,128)}, f32[1,3,128,128]{3,2,1,0:T(8,128)}) custom-call(s32[464]{0:T(512)} %get-tuple-element.44.tbl_ref, f32[16,8,128,128]{3,2,1,0:T(8,128)} %a_ref.5, f32[4,2,128,128]{3,2,1,0:T(8,128)} %copy-done.1, f32[16,2,128,128]{3,2,1,0:T(8,128)} %pown_ref.5), custom_call_target="tpu_custom_call" | custom-call | tf_op jit(solution)/shard_map/pallas_call | solution.py:98
  76.9 0.8 copy-done
  77.7 21.0 %shard_map.57 = (f32[1,3,128,128]{3,2,1,0:T(8,128)}, f32[1,3,128,128]{3,2,1,0:T(8,128)}, f32[1,3,128,128]{3,2,1,0:T(8,128)}) custom-call(s32[464]{0:T(512)} %get-tuple-element.46.tbl_ref, f32[16,8,128,128]{3,2,1,0:T(8,128)} %a_ref.5, f32[4,2,128,128]{3,2,1,0:T(8,128)} %copy-done, f32[16,2,128,128]{3,2,1,0:T(8,128)} %pown_ref.5), custom_call_target="tpu_custom_call" | custom-call | tf_op jit(solution)/shard_map/pallas_call | solution.py:98
  98.7 1.0 collective-permute-start.6
  99.7 3.2 %collective-permute-start.8 = (f32[1,3,128,128]{3,2,1,0:T(8,128)}, f32[1,3,128,128]{3,2,1,0:T(8,128)S(1)}, u32[]{:S(2)}, u32[]{:S(2)}) collective-permute-start(f32[1,3,128,128]{3,2,1,0:T(8,128)} %get-tuple-element.21), channel_id=1, source_target_pairs={{0,7},{1,0},{2,1},{3,2},{4,3},{5,4},{6,5},{7,6},{8,15},{9,8},{10,9... | collective-permute-start | bytes 589832 | tf_op jit(solution)/shard_map/ppermute | solution.py:16
  102.9 0.4 collective-permute-start.7
  103.3 1.0 pad_maximum_fusion
  104.3 0.6 gather_fusion.3
  104.9 10.1 %collective-permute-done.6 = f32[1,3,128,128]{3,2,1,0:T(8,128)S(1)} collective-permute-done((f32[1,3,128,128]{3,2,1,0:T(8,128)}, f32[1,3,128,128]{3,2,1,0:T(8,128)S(1)}, u32[]{:S(2)}, u32[]{:S(2)}) %collective-permute-start.6) | collective-permute-done | bytes 196640 | tf_op jit(solution)/shard_map/ppermute | solution.py:16
  115.1 0.6 gather_fusion.4
  115.9 0.6 gather_fusion.5
  116.5 1.2 %fusion = f32[1,15,128,128]{3,2,1,0:T(8,128)} fusion(f32[15,128,128]{2,1,0:T(8,128)S(1)} %gather_fusion.5, f32[15,128,128]{2,1,0:T(8,128)S(1)} %gather_fusion.4, f32[15,128,128]{2,1,0:T(8,128)S(1)} %gather_fusion.3, pred[15]{0:T(512)(128)(4,1)S(1)} %get-tuple-element.43, pred[15]{0:T(512)(128)(4,1)S(1)} %get-tuple-element.42, ...), kind=kLoop, calls=%fused_computation.7 | loop fusion | flops 1228800 | bytes 3932205 | tf_op jit(solution)/shard_map/add | solution.py:188
  (80 shorter events, 3.2 us)
Async XLA Ops:
  0.0 13.0 %copy-start.5 = (s32[16,2]{0,1:T(2,128)S(1)}, s32[16,2]{0,1:T(2,128)}, u32[]{:S(2)}) copy-start(s32[16,2]{0,1:T(2,128)} %param.8) | copy-start | bytes 388
  0.0 13.0 %copy-start.6 = (s32[1,15]{1,0:T(1,128)S(1)}, s32[1,15]{1,0:T(1,128)}, u32[]{:S(2)}) copy-start(s32[1,15]{1,0:T(1,128)} %param.9) | copy-start | bytes 184
  0.0 13.1 %copy-start.4 = (s32[16,8]{0,1:T(8,128)S(1)}, s32[16,8]{0,1:T(8,128)}, u32[]{:S(2)}) copy-start(s32[16,8]{0,1:T(8,128)} %param.6) | copy-start | bytes 1540
  0.8 16.6 %collective-permute-start.2 = (s32[4,2]{1,0:T(4,128)S(1)}, s32[4,2]{1,0:T(4,128)S(1)}, u32[]{:S(2)}, u32[]{:S(2)}) collective-permute-start(s32[4,2]{1,0:T(4,128)S(1)} %get-tuple-element.30), channel_id=1, source_target_pairs={{8,0},{16,8},{24,16},{9,1},{17,9},{25,17},{10,2},{18,10},{26,18},{... | collective-permute-start | bytes 104 | tf_op jit(solution)/shard_map/ppermute | solution.py:135
  2.8 13.8 %collective-permute-start = (s32[4,2]{1,0:T(4,128)S(1)}, s32[4,2]{1,0:T(4,128)S(1)}, u32[]{:S(2)}, u32[]{:S(2)}) collective-permute-start(s32[4,2]{1,0:T(4,128)S(1)} %get-tuple-element.29), channel_id=1, source_target_pairs={{0,8},{8,16},{16,24},{1,9},{9,17},{17,25},{2,10},{10,18},{18,26},{... | collective-permute-start | bytes 104 | tf_op jit(solution)/shard_map/ppermute | solution.py:134
  8.6 47.4 %collective-permute-start.1 = (f32[4,2,128,128]{3,2,1,0:T(8,128)S(1)}, f32[4,2,128,128]{3,2,1,0:T(8,128)S(1)}, u32[]{:S(2)}, u32[]{:S(2)}) collective-permute-start(f32[4,2,128,128]{3,2,1,0:T(8,128)S(1)} %get-tuple-element.27), channel_id=1, source_target_pairs={{0,8},{8,16},{16,24},{1,9},{9,17},{17,25},{2,10},{10,18},{18,26},{... | collective-permute-start | bytes 1572872 | tf_op jit(solution)/shard_map/ppermute | solution.py:134
  11.0 65.9 %collective-permute-start.3 = (f32[4,2,128,128]{3,2,1,0:T(8,128)S(1)}, f32[4,2,128,128]{3,2,1,0:T(8,128)S(1)}, u32[]{:S(2)}, u32[]{:S(2)}) collective-permute-start(f32[4,2,128,128]{3,2,1,0:T(8,128)S(1)} %get-tuple-element.28), channel_id=1, source_target_pairs={{8,0},{16,8},{24,16},{9,1},{17,9},{25,17},{10,2},{18,10},{26,18},{... | collective-permute-start | bytes 1572872 | tf_op jit(solution)/shard_map/ppermute | solution.py:135
  53.7 49.6 %collective-permute-start.5 = (f32[1,3,128,128]{3,2,1,0:T(8,128)}, f32[1,3,128,128]{3,2,1,0:T(8,128)S(1)}, u32[]{:S(2)}, u32[]{:S(2)}) collective-permute-start(f32[1,3,128,128]{3,2,1,0:T(8,128)} %get-tuple-element.18), channel_id=1, source_target_pairs={{0,1},{1,2},{2,3},{3,4},{4,5},{5,6},{6,7},{7,0},{8,9},{9,10},{10,1... | collective-permute-start | bytes 589832 | tf_op jit(solution)/shard_map/ppermute | solution.py:16
  55.9 0.8 copy-start.1
  76.9 28.0 %collective-permute-start.4 = (f32[1,3,128,128]{3,2,1,0:T(8,128)}, f32[1,3,128,128]{3,2,1,0:T(8,128)S(1)}, u32[]{:S(2)}, u32[]{:S(2)}) collective-permute-start(f32[1,3,128,128]{3,2,1,0:T(8,128)} %get-tuple-element.17), channel_id=1, source_target_pairs={{0,1},{1,2},{2,3},{3,4},{4,5},{5,6},{6,7},{7,0},{8,9},{9,10},{10,1... | collective-permute-start | bytes 589832 | tf_op jit(solution)/shard_map/ppermute | solution.py:16
  76.9 0.8 copy-start
  77.7 25.6 %copy-start.2 = (f32[1,3,128,128]{3,2,1,0:T(8,128)S(1)}, f32[1,3,128,128]{3,2,1,0:T(8,128)}, u32[]{:S(2)}) copy-start(f32[1,3,128,128]{3,2,1,0:T(8,128)} %get-tuple-element.15) | copy-start | bytes 589828
  77.7 25.6 %copy-start.3 = (f32[1,3,128,128]{3,2,1,0:T(8,128)S(1)}, f32[1,3,128,128]{3,2,1,0:T(8,128)}, u32[]{:S(2)}) copy-start(f32[1,3,128,128]{3,2,1,0:T(8,128)} %get-tuple-element.14) | copy-start | bytes 589828
  98.7 16.4 %collective-permute-start.6 = (f32[1,3,128,128]{3,2,1,0:T(8,128)}, f32[1,3,128,128]{3,2,1,0:T(8,128)S(1)}, u32[]{:S(2)}, u32[]{:S(2)}) collective-permute-start(f32[1,3,128,128]{3,2,1,0:T(8,128)} %get-tuple-element.19), channel_id=1, source_target_pairs={{0,1},{1,2},{2,3},{3,4},{4,5},{5,6},{6,7},{7,0},{8,9},{9,10},{10,1... | collective-permute-start | bytes 589832 | tf_op jit(solution)/shard_map/ppermute | solution.py:16
  99.7 16.0 %collective-permute-start.8 = (f32[1,3,128,128]{3,2,1,0:T(8,128)}, f32[1,3,128,128]{3,2,1,0:T(8,128)S(1)}, u32[]{:S(2)}, u32[]{:S(2)}) collective-permute-start(f32[1,3,128,128]{3,2,1,0:T(8,128)} %get-tuple-element.21), channel_id=1, source_target_pairs={{0,7},{1,0},{2,1},{3,2},{4,3},{5,4},{6,5},{7,6},{8,15},{9,8},{10,9... | collective-permute-start | bytes 589832 | tf_op jit(solution)/shard_map/ppermute | solution.py:16
  102.9 12.9 %collective-permute-start.7 = (f32[1,3,128,128]{3,2,1,0:T(8,128)}, f32[1,3,128,128]{3,2,1,0:T(8,128)S(1)}, u32[]{:S(2)}, u32[]{:S(2)}) collective-permute-start(f32[1,3,128,128]{3,2,1,0:T(8,128)} %get-tuple-element.20), channel_id=1, source_target_pairs={{0,7},{1,0},{2,1},{3,2},{4,3},{5,4},{6,5},{7,6},{8,15},{9,8},{10,9... | collective-permute-start | bytes 589832 | tf_op jit(solution)/shard_map/ppermute | solution.py:16
  103.2 12.6 %collective-permute-start.9 = (f32[1,3,128,128]{3,2,1,0:T(8,128)}, f32[1,3,128,128]{3,2,1,0:T(8,128)S(1)}, u32[]{:S(2)}, u32[]{:S(2)}) collective-permute-start(f32[1,3,128,128]{3,2,1,0:T(8,128)} %get-tuple-element.22), channel_id=1, source_target_pairs={{0,7},{1,0},{2,1},{3,2},{4,3},{5,4},{6,5},{7,6},{8,15},{9,8},{10,9... | collective-permute-start | bytes 589832 | tf_op jit(solution)/shard_map/ppermute | solution.py:16

commit v4 on v2

--- a/solution.py
+++ b/solution.py
@@ -8,20 +8,6 @@
 from jax.sharding import PartitionSpec as P
 
 RIM = 4
-
-
-def extended(cells, axis, width):
-    count = lax.axis_size(axis)
-    head = cells[:width]
-    tail = cells[cells.shape[0] - width :]
-    return jnp.concatenate(
-        [
-            lax.ppermute(tail, axis, [(i, i + 1) for i in range(count - 1)]),
-            cells,
-            lax.ppermute(head, axis, [(i + 1, i) for i in range(count - 1)]),
-        ],
-        axis=0,
-    )
 
 
 def passed_along(value, axis, steps):
@@ -47,7 +33,11 @@
     )
 
 
-def triple_kernel(coupling_slots, interp_slots, blocks, region, idx_ref, a_ref, ext_ref, lo_ref, own_ref, hi_ref, y_ref, acc_ref):
+def triple_kernel(
+    coupling_slots, interp_slots, blocks, region,
+    idx_ref, a_ref, low_ref, mid_ref, up_ref, lo_ref, own_ref, hi_ref,
+    y_ref, acc_ref, ph_ref, pl_ref,
+):
     g = pl.program_id(0)
     rows = pl.num_programs(0)
     bs = a_ref.shape[2]
@@ -58,14 +48,28 @@
     def _():
         acc_ref[...] = jnp.zeros_like(acc_ref)
 
+        def fill(src, offset, count):
+            def body(r, carry):
+                for p in range(interp_slots):
+                    hi, lo = split(src[r, p])
+                    ph_ref[offset + r, :, p * bs : (p + 1) * bs] = hi
+                    pl_ref[offset + r, :, p * bs : (p + 1) * bs] = lo
+                return carry
+
+            lax.fori_loop(0, count, body, 0)
+
+        fill(low_ref, 0, RIM)
+        fill(mid_ref, RIM, rows)
+        fill(up_ref, RIM + rows, RIM)
+
     y_ref[...] = jnp.zeros_like(y_ref)
     for a in range(coupling_slots):
         row = idx_ref[g * coupling_slots + a]
-        prod = dot3(split(a_ref[0, a]), split(ext_ref[row]))
+        prod = dot3(split(a_ref[0, a]), (ph_ref[row], pl_ref[row]))
         for p in range(interp_slots):
             slot = idx_ref[slot_base + (g * coupling_slots + a) * interp_slots + p]
             y_ref[slot] += prod[:, p * bs : (p + 1) * bs]
-    pt = split(ext_ref[RIM + g].T)
+    pt = split(jnp.concatenate([mid_ref[g, q].T for q in range(interp_slots)], axis=0))
     owners = [idx_ref[owner_base + g * interp_slots + q] for q in range(interp_slots)]
     for c in range(region):
         res = dot3(pt, split(y_ref[c]))
@@ -90,9 +94,20 @@
     device = s * tiles + t
     region = 9 * blocks
 
-    p_cat = p_tiles.transpose(0, 2, 1, 3).reshape(rows, bs, interp_slots * bs)
-    ext = extended(p_cat, "slab", RIM)
-    ext_keys = extended(p_cols, "slab", RIM)
+    ext_rows = rows + 2 * RIM
+
+    def halo(first):
+        keys = p_cols[first : first + RIM].astype(jnp.float32).reshape(1, 1, 1, RIM * interp_slots)
+        key_tile = jnp.pad(keys, ((0, 0), (0, interp_slots - 1), (0, bs - 1), (0, bs - RIM * interp_slots)))
+        return jnp.concatenate([p_tiles[first : first + RIM], key_tile], axis=0)
+
+    low = lax.ppermute(halo(rows - RIM), "slab", [(i, i + 1) for i in range(slabs - 1)])
+    up = lax.ppermute(halo(0), "slab", [(i + 1, i) for i in range(slabs - 1)])
+
+    def halo_keys(block):
+        return block[RIM, 0, 0, : RIM * interp_slots].astype(jnp.int32).reshape(RIM, interp_slots)
+
+    ext_keys = jnp.concatenate([halo_keys(low), p_cols, halo_keys(up)], axis=0)
 
     own_base = device * rows
     lower_base = (device - tiles) * rows + rows - RIM
@@ -106,7 +121,7 @@
             RIM + rows + a_cols - upper_base,
         ),
     )
-    local_index = jnp.clip(local_index, 0, rows + 2 * RIM - 1)
+    local_index = jnp.clip(local_index, 0, ext_rows - 1)
     keys = ext_keys[local_index]
     k_slab = keys // (tiles * blocks)
     k_tile = (keys // blocks) % tiles
@@ -132,16 +147,20 @@
             grid=(rows,),
             in_specs=[
                 pl.BlockSpec((1, coupling_slots, bs, bs), lambda g, *_: (g, 0, 0, 0)),
-                pl.BlockSpec(ext.shape, lambda g, *_: (0, 0, 0)),
+                pl.BlockSpec(low.shape, lambda g, *_: (0, 0, 0, 0)),
+                pl.BlockSpec(p_tiles.shape, lambda g, *_: (0, 0, 0, 0)),
+                pl.BlockSpec(up.shape, lambda g, *_: (0, 0, 0, 0)),
             ],
             out_specs=(part_spec, part_spec, part_spec),
             scratch_shapes=[
                 pltpu.VMEM((region, bs, bs), jnp.float32),
                 pltpu.VMEM((3 * blocks, region, bs, bs), jnp.float32),
+                pltpu.VMEM((ext_rows, bs, interp_slots * bs), jnp.bfloat16),
+                pltpu.VMEM((ext_rows, bs, interp_slots * bs), jnp.bfloat16),
             ],
         ),
         compiler_params=pltpu.CompilerParams(dimension_semantics=("arbitrary",)),
-    )(table, a_tiles, ext)
+    )(table, a_tiles, low, p_tiles, up)
 
     from_lower = passed_along(to_upper, "tile", 1)
     from_upper = passed_along(to_lower, "tile", -1)

time: 80.2 us -> 70.5 us (0.88)
  starting transfers between devices: 16.2 us -> 10.7 us
  local copies, waits for them, and re-layouts: 9.9 us -> 6.14 us
  other arithmetic: 6.25 us -> 3.41 us
  waiting for transfers between devices: 21.4 us -> 23.9 us
    ppermute x4 -> x2, starting transfers between devices: 12 us -> 6.46 us  [the longest x1 4.54 us: shards(): lax.ppermute(halo(rows - RIM), 'slab', [(i, i + 1) for i in range(slabs -...]
    ppermute x4 -> x2, waiting for transfers between devices: 3.05 us -> 8.53 us  [the longest x1 4.52 us: shards(): up = lax.ppermute(halo(0), 'slab', [(i + 1, i) for i in range(slabs - 1)])]
    ppermute x2, waiting for transfers between devices: 18.4 us -> 15.3 us  [passed_along(): return lax.ppermute(value, axis, pairs)]
    concatenate x2 -> x3, other arithmetic: 1.96 us -> 0.1 us  [the longest x2 0.09 us: halo(): return jnp.concatenate([p_tiles[first:first + RIM], key_tile], axis=0)]
    reshape x1 -> x2, local copies, waits for them, and re-layouts: 1.78 us -> 0.17 us  [halo(): p_cols[first:first + RIM].astype(jnp.float32)]
    unnamed x11, local copies, waits for them, and re-layouts: 1.32 us -> 0.1 us
    slice x3 -> x1, local copies, waits for them, and re-layouts: 2.51 us -> 1.31 us  [halo(): return jnp.concatenate([p_tiles[first:first + RIM], key_tile], axis=0)]
    broadcast_in_dim x2, other arithmetic: 1.15 us -> 0.04 us  [pick(): tiles_picked = part[r_idx, idx]]
  transfers between devices with their start and end apart: 6 -> 4, of which waited for: 3 -> 4; matrix products, arithmetic and copies ran while one was open for 14% -> 6% of each run, Pallas kernels for 0% -> 0%
where the time goes in v4:
time: 70.5 us; the launch traced here: 70.3 us
  Pallas kernels  26 us (37%)
  waiting for transfers between devices  23.9 us (34%)
  starting transfers between devices  10.7 us (15%)
  local copies, waits for them, and re-layouts  6.14 us (9%)
  other arithmetic  3.41 us (5%)
    pallas_call x1, Pallas kernels, shards(): pl.pallas_call(kernel, out_shape=(part, part, part), grid_spec=pltpu.Pref...  26 us
    ppermute x2, waiting for transfers between devices, passed_along(): return lax.ppermute(value, axis, pairs)  15.3 us
    ppermute x1, starting transfers between devices, shards(): lax.ppermute(halo(rows - RIM), 'slab', [(i, i + 1) for i in range(slabs -...  4.54 us
    ppermute x1, waiting for transfers between devices, shards(): up = lax.ppermute(halo(0), 'slab', [(i + 1, i) for i in range(slabs - 1)])  4.52 us
    ppermute x2, starting transfers between devices, passed_along(): return lax.ppermute(value, axis, pairs)  4.25 us
    ppermute x1, waiting for transfers between devices, shards(): lax.ppermute(halo(rows - RIM), 'slab', [(i, i + 1) for i in range(slabs -...  4.01 us
    gather x3, local copies, waits for them, and re-layouts, pick(): tiles_picked = part[r_idx, idx]  2.9 us
    ppermute x1, starting transfers between devices, shards(): up = lax.ppermute(halo(0), 'slab', [(i + 1, i) for i in range(slabs - 1)])  1.92 us
  transfers between devices with their start and end apart: 4, of which 4 were waited for; matrix products, arithmetic and copies ran while one was open for 6% of the time, Pallas kernels for 0%

profile of v4, /device:TPU:1, one launch (start us, length us, event | category | flops | bytes accessed | tf_op | source)
XLA Modules:
  0.0 70.3 jit_solution(80575408348034596)
XLA Ops:
  0.0 1.3 %fusion.19 = (f32[4,2,128,128]{3,2,1,0:T(8,128)S(1)}, f32[4,2,128,128]{3,2,1,0:T(8,128)S(1)}) fusion(f32[16,2,128,128]{3,2,1,0:T(8,128)} %mid_ref.1), kind=kLoop, calls=%fused_computation.71 | loop fusion | bytes 2097152 | tf_op jit(solution)/shard_map/slice | solution.py:102
  1.3 0.1 slice_convert_fusion.1
  1.4 0.1 copy.27
  1.5 0.1 reshape.64
  1.6 4.5 %collective-permute-start = (f32[5,2,128,128]{3,2,1,0:T(8,128)S(1)}, f32[5,2,128,128]{3,2,1,0:T(8,128)S(1)}, u32[]{:S(2)}, u32[]{:S(2)}) collective-permute-start(f32[5,2,128,128]{3,2,1,0:T(8,128)S(1)} %select_maximum_fusion.1), channel_id=1, source_target_pairs={{0,8},{8,16},{16,24},{1,9},{9,17},{17,25},{2,10},{10,18},{18,26},{... | collective-permute-start | bytes 1966088 | tf_op jit(solution)/shard_map/ppermute | solution.py:104
  6.2 0.1 copy.28
  6.3 0.1 reshape.65
  6.4 1.9 %collective-permute-start.1 = (f32[5,2,128,128]{3,2,1,0:T(8,128)S(1)}, f32[5,2,128,128]{3,2,1,0:T(8,128)S(1)}, u32[]{:S(2)}, u32[]{:S(2)}) collective-permute-start(f32[5,2,128,128]{3,2,1,0:T(8,128)S(1)} %select_maximum_fusion), channel_id=1, source_target_pairs={{8,0},{16,8},{24,16},{9,1},{17,9},{25,17},{10,2},{18,10},{26,18},{... | collective-permute-start | bytes 1966088 | tf_op jit(solution)/shard_map/ppermute | solution.py:105
  8.4 0.1 copy.29
  8.5 0.1 copy.30
  8.6 0.1 reshape.69
  8.7 0.1 copy.26
  8.7 0.1 reshape.63
  8.8 0.1 copy.31
  8.9 0.1 reshape.66
  9.1 0.6 and_bitcast_fusion.1
  9.7 4.0 %collective-permute-done.low_ref = f32[5,2,128,128]{3,2,1,0:T(8,128)S(1)} collective-permute-done((f32[5,2,128,128]{3,2,1,0:T(8,128)S(1)}, f32[5,2,128,128]{3,2,1,0:T(8,128)S(1)}, u32[]{:S(2)}, u32[]{:S(2)}) %collective-permute-start) | collective-permute-done | bytes 655392 | tf_op jit(solution)/shard_map/ppermute | solution.py:104
  13.7 0.1 convert_element_type.25
  13.8 4.5 %collective-permute-done.1.up_ref = f32[5,2,128,128]{3,2,1,0:T(8,128)S(1)} collective-permute-done((f32[5,2,128,128]{3,2,1,0:T(8,128)S(1)}, f32[5,2,128,128]{3,2,1,0:T(8,128)S(1)}, u32[]{:S(2)}, u32[]{:S(2)}) %collective-permute-start.1) | collective-permute-done | bytes 655392 | tf_op jit(solution)/shard_map/ppermute | solution.py:105
  18.4 0.1 convert_element_type.28
  18.4 0.6 gather_fusion
  19.1 0.1 gather.15
  19.3 0.6 pad_add_fusion.1.idx_ref
  19.9 26.0 %shard_map.55 = (f32[1,9,128,128]{3,2,1,0:T(8,128)}, f32[1,9,128,128]{3,2,1,0:T(8,128)}, f32[1,9,128,128]{3,2,1,0:T(8,128)}) custom-call(s32[416]{0:T(512)} %pad_add_fusion.1.idx_ref, f32[16,8,128,128]{3,2,1,0:T(8,128)} %a_ref.1, f32[5,2,128,128]{3,2,1,0:T(8,128)} %copy-done, f32[16,2,128,128]{3,2,1,0:T(8,128)} %mid_ref.1, f32[5,2,128,128]{3,2,1,0:T(8,128)} %copy-done.1), custom_call_target="tpu_custom_call" | custom-call | tf_op jit(solution)/shard_map/pallas_call | solution.py:142
  45.8 1.2 %collective-permute-start.2 = (f32[1,9,128,128]{3,2,1,0:T(8,128)}, f32[1,9,128,128]{3,2,1,0:T(8,128)S(1)}, u32[]{:S(2)}, u32[]{:S(2)}) collective-permute-start(f32[1,9,128,128]{3,2,1,0:T(8,128)} %get-tuple-element.9), channel_id=1, source_target_pairs={{0,1},{1,2},{2,3},{3,4},{4,5},{5,6},{6,7},{7,0},{8,9},{9,10},{10,1... | collective-permute-start | bytes 1769480 | tf_op jit(solution)/shard_map/ppermute | solution.py:16
  47.0 3.1 %collective-permute-start.3 = (f32[1,9,128,128]{3,2,1,0:T(8,128)}, f32[1,9,128,128]{3,2,1,0:T(8,128)S(1)}, u32[]{:S(2)}, u32[]{:S(2)}) collective-permute-start(f32[1,9,128,128]{3,2,1,0:T(8,128)} %get-tuple-element.10), channel_id=1, source_target_pairs={{0,7},{1,0},{2,1},{3,2},{4,3},{5,4},{6,5},{7,6},{8,15},{9,8},{10,9... | collective-permute-start | bytes 1769480 | tf_op jit(solution)/shard_map/ppermute | solution.py:16
  50.1 1.7 %gather_fusion.1 = f32[15,128,128]{2,1,0:T(8,128)S(1)} fusion(f32[1,9,128,128]{3,2,1,0:T(8,128)} %get-tuple-element.8, s32[15]{0:T(128)S(1)} %or_bitcast_fusion.2), kind=kCustom, calls=%fused_computation.1 | custom fusion | bytes 1966200 | tf_op jit(solution)/shard_map/gather | solution.py:179
  51.8 13.9 %collective-permute-done.2 = f32[1,9,128,128]{3,2,1,0:T(8,128)S(1)} collective-permute-done((f32[1,9,128,128]{3,2,1,0:T(8,128)}, f32[1,9,128,128]{3,2,1,0:T(8,128)S(1)}, u32[]{:S(2)}, u32[]{:S(2)}) %collective-permute-start.2) | collective-permute-done | bytes 589856 | tf_op jit(solution)/shard_map/ppermute | solution.py:16
  65.7 0.6 gather_fusion.2
  66.3 1.5 %collective-permute-done.3 = f32[1,9,128,128]{3,2,1,0:T(8,128)S(1)} collective-permute-done((f32[1,9,128,128]{3,2,1,0:T(8,128)}, f32[1,9,128,128]{3,2,1,0:T(8,128)S(1)}, u32[]{:S(2)}, u32[]{:S(2)}) %collective-permute-start.3) | collective-permute-done | bytes 589856 | tf_op jit(solution)/shard_map/ppermute | solution.py:16
  67.8 0.6 gather_fusion.3
  68.4 1.9 %fusion = f32[1,15,128,128]{3,2,1,0:T(8,128)} fusion(f32[15,128,128]{2,1,0:T(8,128)S(1)} %gather_fusion.3, f32[15,128,128]{2,1,0:T(8,128)S(1)} %gather_fusion.2, f32[15,128,128]{2,1,0:T(8,128)S(1)} %gather_fusion.1, pred[15]{0:T(512)(128)(4,1)} %get-tuple-element.24, pred[15]{0:T(512)(128)(4,1)S(1)} %get-tuple-element.23, pred[15]{0:T(512)(128)(4,1)S(1)} %get-tuple-element.11), kind=kLoop, calls=%fused_computation.5 | loop fusion | flops 1228800 | bytes 3932205 | tf_op jit(solution)/shard_map/add | solution.py:182
  (28 shorter events, 0.3 us)
Async XLA Ops:
  0.0 1.3 %copy-start.2 = (s32[16,2]{0,1:T(2,128)S(1)}, s32[16,2]{0,1:T(2,128)}, u32[]{:S(2)}) copy-start(s32[16,2]{0,1:T(2,128)} %param.8) | copy-start | bytes 388
  0.0 8.5 %copy-start.3 = (s32[16,8]{0,1:T(8,128)S(1)}, s32[16,8]{0,1:T(8,128)}, u32[]{:S(2)}) copy-start(s32[16,8]{0,1:T(8,128)} %param.6) | copy-start | bytes 1540
  0.0 9.0 %copy-start.4 = (s32[1,15]{1,0:T(1,128)S(1)}, s32[1,15]{1,0:T(1,128)}, u32[]{:S(2)}) copy-start(s32[1,15]{1,0:T(1,128)} %param.9) | copy-start | bytes 184
  1.6 12.1 %collective-permute-start = (f32[5,2,128,128]{3,2,1,0:T(8,128)S(1)}, f32[5,2,128,128]{3,2,1,0:T(8,128)S(1)}, u32[]{:S(2)}, u32[]{:S(2)}) collective-permute-start(f32[5,2,128,128]{3,2,1,0:T(8,128)S(1)} %select_maximum_fusion.1), channel_id=1, source_target_pairs={{0,8},{8,16},{16,24},{1,9},{9,17},{17,25},{2,10},{10,18},{18,26},{... | collective-permute-start | bytes 1966088 | tf_op jit(solution)/shard_map/ppermute | solution.py:104
  6.4 11.9 %collective-permute-start.1 = (f32[5,2,128,128]{3,2,1,0:T(8,128)S(1)}, f32[5,2,128,128]{3,2,1,0:T(8,128)S(1)}, u32[]{:S(2)}, u32[]{:S(2)}) collective-permute-start(f32[5,2,128,128]{3,2,1,0:T(8,128)S(1)} %select_maximum_fusion), channel_id=1, source_target_pairs={{8,0},{16,8},{24,16},{9,1},{17,9},{25,17},{10,2},{18,10},{26,18},{... | collective-permute-start | bytes 1966088 | tf_op jit(solution)/shard_map/ppermute | solution.py:105
  13.7 6.2 %copy-start = (f32[5,2,128,128]{3,2,1,0:T(8,128)}, f32[5,2,128,128]{3,2,1,0:T(8,128)S(1)}, u32[]{:S(2)}) copy-start(f32[5,2,128,128]{3,2,1,0:T(8,128)S(1)} %collective-permute-done.low_ref) | copy-start | bytes 1966084
  18.3 1.5 %copy-start.1 = (f32[5,2,128,128]{3,2,1,0:T(8,128)}, f32[5,2,128,128]{3,2,1,0:T(8,128)S(1)}, u32[]{:S(2)}) copy-start(f32[5,2,128,128]{3,2,1,0:T(8,128)S(1)} %collective-permute-done.1.up_ref) | copy-start | bytes 1966084
  45.8 19.9 %collective-permute-start.2 = (f32[1,9,128,128]{3,2,1,0:T(8,128)}, f32[1,9,128,128]{3,2,1,0:T(8,128)S(1)}, u32[]{:S(2)}, u32[]{:S(2)}) collective-permute-start(f32[1,9,128,128]{3,2,1,0:T(8,128)} %get-tuple-element.9), channel_id=1, source_target_pairs={{0,1},{1,2},{2,3},{3,4},{4,5},{5,6},{6,7},{7,0},{8,9},{9,10},{10,1... | collective-permute-start | bytes 1769480 | tf_op jit(solution)/shard_map/ppermute | solution.py:16
  47.0 20.7 %collective-permute-start.3 = (f32[1,9,128,128]{3,2,1,0:T(8,128)}, f32[1,9,128,128]{3,2,1,0:T(8,128)S(1)}, u32[]{:S(2)}, u32[]{:S(2)}) collective-permute-start(f32[1,9,128,128]{3,2,1,0:T(8,128)} %get-tuple-element.10), channel_id=1, source_target_pairs={{0,7},{1,0},{2,1},{3,2},{4,3},{5,4},{6,5},{7,6},{8,15},{9,8},{10,9... | collective-permute-start | bytes 1769480 | tf_op jit(solution)/shard_map/ppermute | solution.py:16

commit v5 on v4

--- a/solution.py
+++ b/solution.py
@@ -71,10 +71,10 @@
             y_ref[slot] += prod[:, p * bs : (p + 1) * bs]
     pt = split(jnp.concatenate([mid_ref[g, q].T for q in range(interp_slots)], axis=0))
     owners = [idx_ref[owner_base + g * interp_slots + q] for q in range(interp_slots)]
-    for c in range(region):
-        res = dot3(pt, split(y_ref[c]))
-        for q in range(interp_slots):
-            acc_ref[owners[q], c] += res[q * bs : (q + 1) * bs]
+    wide = jnp.concatenate([y_ref[c] for c in range(region)], axis=1)
+    res = dot3(pt, split(wide))
+    for q in range(interp_slots):
+        acc_ref[owners[q]] += res[q * bs : (q + 1) * bs]
 
     @pl.when(g == rows - 1)
     def _():
@@ -134,8 +134,8 @@
     owner = jnp.clip(relative * blocks + targets % blocks, 0, 3 * blocks - 1)
 
     kernel = functools.partial(triple_kernel, coupling_slots, interp_slots, blocks, region)
-    part = jax.ShapeDtypeStruct((blocks, region, bs, bs), jnp.float32)
-    part_spec = pl.BlockSpec((blocks, region, bs, bs), lambda g, *_: (0, 0, 0, 0))
+    part = jax.ShapeDtypeStruct((blocks, bs, region * bs), jnp.float32)
+    part_spec = pl.BlockSpec((blocks, bs, region * bs), lambda g, *_: (0, 0, 0))
     table = jnp.concatenate(
         [local_index.reshape(-1), slot.reshape(-1), owner.reshape(-1)]
     ).astype(jnp.int32)
@@ -154,7 +154,7 @@
             out_specs=(part_spec, part_spec, part_spec),
             scratch_shapes=[
                 pltpu.VMEM((region, bs, bs), jnp.float32),
-                pltpu.VMEM((3 * blocks, region, bs, bs), jnp.float32),
+                pltpu.VMEM((3 * blocks, bs, region * bs), jnp.float32),
                 pltpu.VMEM((ext_rows, bs, interp_slots * bs), jnp.bfloat16),
                 pltpu.VMEM((ext_rows, bs, interp_slots * bs), jnp.bfloat16),
             ],
@@ -162,8 +162,12 @@
         compiler_params=pltpu.CompilerParams(dimension_semantics=("arbitrary",)),
     )(table, a_tiles, low, p_tiles, up)
 
-    from_lower = passed_along(to_upper, "tile", 1)
-    from_upper = passed_along(to_lower, "tile", -1)
+    def slot_major(part):
+        return part.reshape(blocks, bs, region, bs).transpose(0, 2, 1, 3)
+
+    own_part = slot_major(own_part)
+    from_lower = slot_major(passed_along(to_upper, "tile", 1))
+    from_upper = slot_major(passed_along(to_lower, "tile", -1))
 
     c_slab = c_cols // (tiles * blocks)
     c_tile = (c_cols // blocks) % tiles

time: 70.5 us -> 72.5 us (1.028)
  local copies, waits for them, and re-layouts: 6.14 us -> 8.5 us
    pallas_call x0 -> x1, local copies, waits for them, and re-layouts: none -> 1.29 us  [shards(): pl.pallas_call(kernel, out_shape=(part, part, part), grid_spec=pltpu.Pref...]
  transfers between devices with their start and end apart: 4 -> 4, of which waited for: 4 -> 4; matrix products, arithmetic and copies ran while one was open for 6% -> 5% of each run, Pallas kernels for 0% -> 0%
where the time goes in v5:
time: 72.5 us; the launch traced here: 72.2 us
  Pallas kernels  25.3 us (35%)
  waiting for transfers between devices  24.1 us (33%)
  starting transfers between devices  10.7 us (15%)
  local copies, waits for them, and re-layouts  8.5 us (12%)
  other arithmetic  3.37 us (5%)
    pallas_call x1, Pallas kernels, shards(): pl.pallas_call(kernel, out_shape=(part, part, part), grid_spec=pltpu.Pref...  25.3 us
    ppermute x2, waiting for transfers between devices, passed_along(): return lax.ppermute(value, axis, pairs)  15 us
    ppermute x1, waiting for transfers between devices, shards(): lax.ppermute(halo(rows - RIM), 'slab', [(i, i + 1) for i in range(slabs -...  4.57 us
    ppermute x1, starting transfers between devices, shards(): lax.ppermute(halo(rows - RIM), 'slab', [(i, i + 1) for i in range(slabs -...  4.54 us
    ppermute x1, waiting for transfers between devices, shards(): up = lax.ppermute(halo(0), 'slab', [(i + 1, i) for i in range(slabs - 1)])  4.52 us
    ppermute x2, starting transfers between devices, passed_along(): return lax.ppermute(value, axis, pairs)  4.25 us
    gather x3, local copies, waits for them, and re-layouts, pick(): tiles_picked = part[r_idx, idx]  2.8 us
    add x1, other arithmetic, shards(): pick(own_part, c_dt) + pick(from_lower, c_dt + 1)  2.42 us
  transfers between devices with their start and end apart: 4, of which 4 were waited for; matrix products, arithmetic and copies ran while one was open for 5% of the time, Pallas kernels for 0%

profile of v5, /device:TPU:1, one launch (start us, length us, event | category | flops | bytes accessed | tf_op | source)
XLA Modules:
  0.0 72.2 jit_solution(3668570880143596750)
XLA Ops:
  0.0 1.3 %fusion.19 = (f32[4,2,128,128]{3,2,1,0:T(8,128)S(1)}, f32[4,2,128,128]{3,2,1,0:T(8,128)S(1)}) fusion(f32[16,2,128,128]{3,2,1,0:T(8,128)} %mid_ref.1), kind=kLoop, calls=%fused_computation.71 | loop fusion | bytes 2097152 | tf_op jit(solution)/shard_map/slice | solution.py:102
  1.4 0.1 copy.39
  1.5 0.1 reshape.73
  1.7 4.5 %collective-permute-start = (f32[5,2,128,128]{3,2,1,0:T(8,128)S(1)}, f32[5,2,128,128]{3,2,1,0:T(8,128)S(1)}, u32[]{:S(2)}, u32[]{:S(2)}) collective-permute-start(f32[5,2,128,128]{3,2,1,0:T(8,128)S(1)} %select_maximum_fusion.1), channel_id=1, source_target_pairs={{0,8},{8,16},{16,24},{1,9},{9,17},{17,25},{2,10},{10,18},{18,26},{... | collective-permute-start | bytes 1966088 | tf_op jit(solution)/shard_map/ppermute | solution.py:104
  6.2 0.1 copy.40
  6.3 0.1 reshape.74
  6.4 1.9 %collective-permute-start.1 = (f32[5,2,128,128]{3,2,1,0:T(8,128)S(1)}, f32[5,2,128,128]{3,2,1,0:T(8,128)S(1)}, u32[]{:S(2)}, u32[]{:S(2)}) collective-permute-start(f32[5,2,128,128]{3,2,1,0:T(8,128)S(1)} %select_maximum_fusion), channel_id=1, source_target_pairs={{8,0},{16,8},{24,16},{9,1},{17,9},{25,17},{10,2},{18,10},{26,18},{... | collective-permute-start | bytes 1966088 | tf_op jit(solution)/shard_map/ppermute | solution.py:105
  8.7 0.1 reshape.81
  8.8 0.1 reshape.72
  9.0 0.1 reshape.75
  9.1 4.6 %collective-permute-done.low_ref = f32[5,2,128,128]{3,2,1,0:T(8,128)S(1)} collective-permute-done((f32[5,2,128,128]{3,2,1,0:T(8,128)S(1)}, f32[5,2,128,128]{3,2,1,0:T(8,128)S(1)}, u32[]{:S(2)}, u32[]{:S(2)}) %collective-permute-start) | collective-permute-done | bytes 655392 | tf_op jit(solution)/shard_map/ppermute | solution.py:104
  13.7 0.1 convert_element_type.25
  13.8 4.5 %collective-permute-done.1.up_ref = f32[5,2,128,128]{3,2,1,0:T(8,128)S(1)} collective-permute-done((f32[5,2,128,128]{3,2,1,0:T(8,128)S(1)}, f32[5,2,128,128]{3,2,1,0:T(8,128)S(1)}, u32[]{:S(2)}, u32[]{:S(2)}) %collective-permute-start.1) | collective-permute-done | bytes 655392 | tf_op jit(solution)/shard_map/ppermute | solution.py:105
  18.4 0.1 convert_element_type.28
  18.5 0.6 gather_fusion
  19.1 0.1 gather.15
  19.3 0.6 pad_add_fusion.1.idx_ref
  19.9 25.3 %shard_map.55 = (f32[1,128,1152]{2,1,0:T(8,128)}, f32[1,128,1152]{2,1,0:T(8,128)}, f32[1,128,1152]{2,1,0:T(8,128)}) custom-call(s32[416]{0:T(512)} %pad_add_fusion.1.idx_ref, f32[16,8,128,128]{3,2,1,0:T(8,128)} %a_ref.1, f32[5,2,128,128]{3,2,1,0:T(8,128)} %copy-done, f32[16,2,128,128]{3,2,1,0:T(8,128)} %mid_ref.1, f32[5,2,128,128]{3,2,1,0:T(8,128)} %copy-done.1), custom_call_target="tpu_custom_call" | custom-call | tf_op jit(solution)/shard_map/pallas_call | solution.py:142
  45.2 1.2 %collective-permute-start.2 = (f32[1,128,1152]{2,1,0:T(8,128)}, f32[1,128,1152]{2,1,0:T(8,128)S(1)}, u32[]{:S(2)}, u32[]{:S(2)}) collective-permute-start(f32[1,128,1152]{2,1,0:T(8,128)} %get-tuple-element.9), channel_id=1, source_target_pairs={{0,1},{1,2},{2,3},{3,4},{4,5},{5,6},{6,7},{7,0},{8,9},{9,10},{10,1... | collective-permute-start | bytes 1769480 | tf_op jit(solution)/shard_map/ppermute | solution.py:16
  46.4 3.0 %collective-permute-start.3 = (f32[1,128,1152]{2,1,0:T(8,128)}, f32[1,128,1152]{2,1,0:T(8,128)S(1)}, u32[]{:S(2)}, u32[]{:S(2)}) collective-permute-start(f32[1,128,1152]{2,1,0:T(8,128)} %get-tuple-element.10), channel_id=1, source_target_pairs={{0,7},{1,0},{2,1},{3,2},{4,3},{5,4},{6,5},{7,6},{8,15},{9,8},{10,9... | collective-permute-start | bytes 1769480 | tf_op jit(solution)/shard_map/ppermute | solution.py:16
  49.5 1.3 %copy.44 = f32[1,128,1152]{1,2,0:T(8,128)S(1)} copy(f32[1,128,1152]{2,1,0:T(8,128)} %get-tuple-element.8) | data formatting | bytes 1179648 | tf_op jit(solution)/shard_map/pallas_call | solution.py:142
  50.7 0.2 copy.45
  51.0 0.6 gather_fusion.1
  51.6 13.4 %collective-permute-done.2 = f32[1,128,1152]{2,1,0:T(8,128)S(1)} collective-permute-done((f32[1,128,1152]{2,1,0:T(8,128)}, f32[1,128,1152]{2,1,0:T(8,128)S(1)}, u32[]{:S(2)}, u32[]{:S(2)}) %collective-permute-start.2) | collective-permute-done | bytes 589856 | tf_op jit(solution)/shard_map/ppermute | solution.py:16
  65.0 0.2 copy.46
  65.3 0.2 copy.47
  65.5 1.6 %collective-permute-done.3 = f32[1,128,1152]{2,1,0:T(8,128)S(1)} collective-permute-done((f32[1,128,1152]{2,1,0:T(8,128)}, f32[1,128,1152]{2,1,0:T(8,128)S(1)}, u32[]{:S(2)}, u32[]{:S(2)}) %collective-permute-start.3) | collective-permute-done | bytes 589856 | tf_op jit(solution)/shard_map/ppermute | solution.py:16
  67.1 0.2 copy.48
  67.3 0.2 copy.49
  67.6 0.6 gather_fusion.2
  68.2 1.6 %gather_fusion.3 = f32[15,128,128]{2,1,0:T(8,128)} fusion(f32[1,9,128,128]{3,2,1,0:T(8,128)S(1)} %bitcast.45, s32[15]{0:T(128)S(1)} %or_bitcast_fusion), kind=kCustom, calls=%fused_computation.3 | custom fusion | bytes 1966200 | tf_op jit(solution)/shard_map/gather | solution.py:183
  69.8 2.4 %fusion = f32[1,15,128,128]{3,2,1,0:T(8,128)} fusion(f32[15,128,128]{2,1,0:T(8,128)} %gather_fusion.3, f32[15,128,128]{2,1,0:T(8,128)S(1)} %gather_fusion.2, f32[15,128,128]{2,1,0:T(8,128)S(1)} %gather_fusion.1, pred[15]{0:T(512)(128)(4,1)S(1)} %get-tuple-element.24, pred[15]{0:T(512)(128)(4,1)S(1)} %get-tuple-element.23, pred[15]{0:T(512)(128)(4,1)S(1)} %get-tuple-element.11), kind=kLoop, calls=%fused_computation.5 | loop fusion | flops 1228800 | bytes 3932205 | tf_op jit(solution)/shard_map/add | solution.py:186
  (33 shorter events, 0.7 us)
Async XLA Ops:
  0.0 1.3 %copy-start.2 = (s32[16,2]{0,1:T(2,128)S(1)}, s32[16,2]{0,1:T(2,128)}, u32[]{:S(2)}) copy-start(s32[16,2]{0,1:T(2,128)} %param.8) | copy-start | bytes 388
  0.0 8.4 %copy-start.4 = (s32[1,15]{1,0:T(1,128)S(1)}, s32[1,15]{1,0:T(1,128)}, u32[]{:S(2)}) copy-start(s32[1,15]{1,0:T(1,128)} %param.9) | copy-start | bytes 184
  0.0 8.5 %copy-start.3 = (s32[16,8]{0,1:T(8,128)S(1)}, s32[16,8]{0,1:T(8,128)}, u32[]{:S(2)}) copy-start(s32[16,8]{0,1:T(8,128)} %param.6) | copy-start | bytes 1540
  1.7 12.1 %collective-permute-start = (f32[5,2,128,128]{3,2,1,0:T(8,128)S(1)}, f32[5,2,128,128]{3,2,1,0:T(8,128)S(1)}, u32[]{:S(2)}, u32[]{:S(2)}) collective-permute-start(f32[5,2,128,128]{3,2,1,0:T(8,128)S(1)} %select_maximum_fusion.1), channel_id=1, source_target_pairs={{0,8},{8,16},{16,24},{1,9},{9,17},{17,25},{2,10},{10,18},{18,26},{... | collective-permute-start | bytes 1966088 | tf_op jit(solution)/shard_map/ppermute | solution.py:104
  6.4 11.9 %collective-permute-start.1 = (f32[5,2,128,128]{3,2,1,0:T(8,128)S(1)}, f32[5,2,128,128]{3,2,1,0:T(8,128)S(1)}, u32[]{:S(2)}, u32[]{:S(2)}) collective-permute-start(f32[5,2,128,128]{3,2,1,0:T(8,128)S(1)} %select_maximum_fusion), channel_id=1, source_target_pairs={{8,0},{16,8},{24,16},{9,1},{17,9},{25,17},{10,2},{18,10},{26,18},{... | collective-permute-start | bytes 1966088 | tf_op jit(solution)/shard_map/ppermute | solution.py:105
  13.7 6.2 %copy-start = (f32[5,2,128,128]{3,2,1,0:T(8,128)}, f32[5,2,128,128]{3,2,1,0:T(8,128)S(1)}, u32[]{:S(2)}) copy-start(f32[5,2,128,128]{3,2,1,0:T(8,128)S(1)} %collective-permute-done.low_ref) | copy-start | bytes 1966084
  18.3 1.5 %copy-start.1 = (f32[5,2,128,128]{3,2,1,0:T(8,128)}, f32[5,2,128,128]{3,2,1,0:T(8,128)S(1)}, u32[]{:S(2)}) copy-start(f32[5,2,128,128]{3,2,1,0:T(8,128)S(1)} %collective-permute-done.1.up_ref) | copy-start | bytes 1966084
  45.2 19.9 %collective-permute-start.2 = (f32[1,128,1152]{2,1,0:T(8,128)}, f32[1,128,1152]{2,1,0:T(8,128)S(1)}, u32[]{:S(2)}, u32[]{:S(2)}) collective-permute-start(f32[1,128,1152]{2,1,0:T(8,128)} %get-tuple-element.9), channel_id=1, source_target_pairs={{0,1},{1,2},{2,3},{3,4},{4,5},{5,6},{6,7},{7,0},{8,9},{9,10},{10,1... | collective-permute-start | bytes 1769480 | tf_op jit(solution)/shard_map/ppermute | solution.py:16
  46.4 20.7 %collective-permute-start.3 = (f32[1,128,1152]{2,1,0:T(8,128)}, f32[1,128,1152]{2,1,0:T(8,128)S(1)}, u32[]{:S(2)}, u32[]{:S(2)}) collective-permute-start(f32[1,128,1152]{2,1,0:T(8,128)} %get-tuple-element.10), channel_id=1, source_target_pairs={{0,7},{1,0},{2,1},{3,2},{4,3},{5,4},{6,5},{7,6},{8,15},{9,8},{10,9... | collective-permute-start | bytes 1769480 | tf_op jit(solution)/shard_map/ppermute | solution.py:16

commit v6 on v4

--- a/solution.py
+++ b/solution.py
@@ -22,21 +22,20 @@
     return hi, lo
 
 
-def dot3(x, y):
-    xh, xl = x
-    yh, yl = y
-    f32 = jnp.float32
-    return (
-        jnp.dot(xh, yh, preferred_element_type=f32)
-        + jnp.dot(xh, yl, preferred_element_type=f32)
-        + jnp.dot(xl, yh, preferred_element_type=f32)
-    )
+def stack_lhs(x):
+    hi, lo = split(x)
+    return jnp.concatenate([hi, hi, lo], axis=1)
+
+
+def stack_rhs(y):
+    hi, lo = split(y)
+    return jnp.concatenate([hi, lo, hi], axis=0)
 
 
 def triple_kernel(
     coupling_slots, interp_slots, blocks, region,
     idx_ref, a_ref, low_ref, mid_ref, up_ref, lo_ref, own_ref, hi_ref,
-    y_ref, acc_ref, ph_ref, pl_ref,
+    y_ref, acc_ref, p3_ref,
 ):
     g = pl.program_id(0)
     rows = pl.num_programs(0)
@@ -52,8 +51,10 @@
             def body(r, carry):
                 for p in range(interp_slots):
                     hi, lo = split(src[r, p])
-                    ph_ref[offset + r, :, p * bs : (p + 1) * bs] = hi
-                    pl_ref[offset + r, :, p * bs : (p + 1) * bs] = lo
+                    cols = slice(p * bs, (p + 1) * bs)
+                    p3_ref[offset + r, 0:bs, cols] = hi
+                    p3_ref[offset + r, bs : 2 * bs, cols] = lo
+                    p3_ref[offset + r, 2 * bs : 3 * bs, cols] = hi
                 return carry
 
             lax.fori_loop(0, count, body, 0)
@@ -65,14 +66,14 @@
     y_ref[...] = jnp.zeros_like(y_ref)
     for a in range(coupling_slots):
         row = idx_ref[g * coupling_slots + a]
-        prod = dot3(split(a_ref[0, a]), (ph_ref[row], pl_ref[row]))
+        prod = jnp.dot(stack_lhs(a_ref[0, a]), p3_ref[row], preferred_element_type=jnp.float32)
         for p in range(interp_slots):
             slot = idx_ref[slot_base + (g * coupling_slots + a) * interp_slots + p]
             y_ref[slot] += prod[:, p * bs : (p + 1) * bs]
-    pt = split(jnp.concatenate([mid_ref[g, q].T for q in range(interp_slots)], axis=0))
+    pt = stack_lhs(jnp.concatenate([mid_ref[g, q].T for q in range(interp_slots)], axis=0))
     owners = [idx_ref[owner_base + g * interp_slots + q] for q in range(interp_slots)]
     for c in range(region):
-        res = dot3(pt, split(y_ref[c]))
+        res = jnp.dot(pt, stack_rhs(y_ref[c]), preferred_element_type=jnp.float32)
         for q in range(interp_slots):
             acc_ref[owners[q], c] += res[q * bs : (q + 1) * bs]
 
@@ -155,8 +156,7 @@
             scratch_shapes=[
                 pltpu.VMEM((region, bs, bs), jnp.float32),
                 pltpu.VMEM((3 * blocks, region, bs, bs), jnp.float32),
-                pltpu.VMEM((ext_rows, bs, interp_slots * bs), jnp.bfloat16),
-                pltpu.VMEM((ext_rows, bs, interp_slots * bs), jnp.bfloat16),
+                pltpu.VMEM((ext_rows, 3 * bs, interp_slots * bs), jnp.bfloat16),
             ],
         ),
         compiler_params=pltpu.CompilerParams(dimension_semantics=("arbitrary",)),

time: 70.5 us -> 68.5 us (0.972)
  Pallas kernels: 26 us -> 23.9 us
    pallas_call x1, Pallas kernels: 26 us -> 23.9 us  [shards(): pl.pallas_call(kernel, out_shape=(part, part, part), grid_spec=pltpu.Pref...]
where the time goes in v6:
time: 68.5 us; the launch traced here: 68.2 us
  Pallas kernels  23.9 us (35%)
  waiting for transfers between devices  23.8 us (35%)
  starting transfers between devices  10.7 us (16%)
  local copies, waits for them, and re-layouts  6.14 us (9%)
  other arithmetic  3.41 us (5%)
    pallas_call x1, Pallas kernels, shards(): pl.pallas_call(kernel, out_shape=(part, part, part), grid_spec=pltpu.Pref...  23.9 us
    ppermute x2, waiting for transfers between devices, passed_along(): return lax.ppermute(value, axis, pairs)  15.3 us
    ppermute x1, starting transfers between devices, shards(): lax.ppermute(halo(rows - RIM), 'slab', [(i, i + 1) for i in range(slabs -...  4.54 us
    ppermute x1, waiting for transfers between devices, shards(): up = lax.ppermute(halo(0), 'slab', [(i + 1, i) for i in range(slabs - 1)])  4.52 us
    ppermute x2, starting transfers between devices, passed_along(): return lax.ppermute(value, axis, pairs)  4.25 us
    ppermute x1, waiting for transfers between devices, shards(): lax.ppermute(halo(rows - RIM), 'slab', [(i, i + 1) for i in range(slabs -...  4.01 us
    gather x3, local copies, waits for them, and re-layouts, pick(): tiles_picked = part[r_idx, idx]  2.9 us
    ppermute x1, starting transfers between devices, shards(): up = lax.ppermute(halo(0), 'slab', [(i + 1, i) for i in range(slabs - 1)])  1.92 us
  transfers between devices with their start and end apart: 4, of which 4 were waited for; matrix products, arithmetic and copies ran while one was open for 6% of the time, Pallas kernels for 0%

profile of v6, /device:TPU:1, one launch (start us, length us, event | category | flops | bytes accessed | tf_op | source)
XLA Modules:
  0.0 68.2 jit_solution(13487541025776616148)
XLA Ops:
  0.0 1.3 %fusion.19 = (f32[4,2,128,128]{3,2,1,0:T(8,128)S(1)}, f32[4,2,128,128]{3,2,1,0:T(8,128)S(1)}) fusion(f32[16,2,128,128]{3,2,1,0:T(8,128)} %mid_ref.1), kind=kLoop, calls=%fused_computation.71 | loop fusion | bytes 2097152 | tf_op jit(solution)/shard_map/slice | solution.py:103
  1.3 0.1 slice_convert_fusion.1
  1.4 0.1 copy.27
  1.5 0.1 reshape.64
  1.6 4.5 %collective-permute-start = (f32[5,2,128,128]{3,2,1,0:T(8,128)S(1)}, f32[5,2,128,128]{3,2,1,0:T(8,128)S(1)}, u32[]{:S(2)}, u32[]{:S(2)}) collective-permute-start(f32[5,2,128,128]{3,2,1,0:T(8,128)S(1)} %select_maximum_fusion.1), channel_id=1, source_target_pairs={{0,8},{8,16},{16,24},{1,9},{9,17},{17,25},{2,10},{10,18},{18,26},{... | collective-permute-start | bytes 1966088 | tf_op jit(solution)/shard_map/ppermute | solution.py:105
  6.2 0.1 copy.28
  6.3 0.1 reshape.65
  6.4 1.9 %collective-permute-start.1 = (f32[5,2,128,128]{3,2,1,0:T(8,128)S(1)}, f32[5,2,128,128]{3,2,1,0:T(8,128)S(1)}, u32[]{:S(2)}, u32[]{:S(2)}) collective-permute-start(f32[5,2,128,128]{3,2,1,0:T(8,128)S(1)} %select_maximum_fusion), channel_id=1, source_target_pairs={{8,0},{16,8},{24,16},{9,1},{17,9},{25,17},{10,2},{18,10},{26,18},{... | collective-permute-start | bytes 1966088 | tf_op jit(solution)/shard_map/ppermute | solution.py:106
  8.4 0.1 copy.29
  8.5 0.1 copy.30
  8.6 0.1 reshape.69
  8.7 0.1 copy.26
  8.7 0.1 reshape.63
  8.8 0.1 copy.31
  8.9 0.1 reshape.66
  9.1 0.6 and_bitcast_fusion.1
  9.7 4.0 %collective-permute-done.low_ref = f32[5,2,128,128]{3,2,1,0:T(8,128)S(1)} collective-permute-done((f32[5,2,128,128]{3,2,1,0:T(8,128)S(1)}, f32[5,2,128,128]{3,2,1,0:T(8,128)S(1)}, u32[]{:S(2)}, u32[]{:S(2)}) %collective-permute-start) | collective-permute-done | bytes 655392 | tf_op jit(solution)/shard_map/ppermute | solution.py:105
  13.7 0.1 convert_element_type.25
  13.8 4.5 %collective-permute-done.1.up_ref = f32[5,2,128,128]{3,2,1,0:T(8,128)S(1)} collective-permute-done((f32[5,2,128,128]{3,2,1,0:T(8,128)S(1)}, f32[5,2,128,128]{3,2,1,0:T(8,128)S(1)}, u32[]{:S(2)}, u32[]{:S(2)}) %collective-permute-start.1) | collective-permute-done | bytes 655392 | tf_op jit(solution)/shard_map/ppermute | solution.py:106
  18.4 0.1 convert_element_type.28
  18.4 0.6 gather_fusion
  19.1 0.1 gather.15
  19.3 0.6 pad_add_fusion.1.idx_ref
  19.9 23.9 %shard_map.55 = (f32[1,9,128,128]{3,2,1,0:T(8,128)}, f32[1,9,128,128]{3,2,1,0:T(8,128)}, f32[1,9,128,128]{3,2,1,0:T(8,128)}) custom-call(s32[416]{0:T(512)} %pad_add_fusion.1.idx_ref, f32[16,8,128,128]{3,2,1,0:T(8,128)} %a_ref.1, f32[5,2,128,128]{3,2,1,0:T(8,128)} %copy-done, f32[16,2,128,128]{3,2,1,0:T(8,128)} %mid_ref.1, f32[5,2,128,128]{3,2,1,0:T(8,128)} %copy-done.1), custom_call_target="tpu_custom_call" | custom-call | tf_op jit(solution)/shard_map/pallas_call | solution.py:143
  43.8 1.2 %collective-permute-start.2 = (f32[1,9,128,128]{3,2,1,0:T(8,128)}, f32[1,9,128,128]{3,2,1,0:T(8,128)S(1)}, u32[]{:S(2)}, u32[]{:S(2)}) collective-permute-start(f32[1,9,128,128]{3,2,1,0:T(8,128)} %get-tuple-element.9), channel_id=1, source_target_pairs={{0,1},{1,2},{2,3},{3,4},{4,5},{5,6},{6,7},{7,0},{8,9},{9,10},{10,1... | collective-permute-start | bytes 1769480 | tf_op jit(solution)/shard_map/ppermute | solution.py:16
  45.0 3.1 %collective-permute-start.3 = (f32[1,9,128,128]{3,2,1,0:T(8,128)}, f32[1,9,128,128]{3,2,1,0:T(8,128)S(1)}, u32[]{:S(2)}, u32[]{:S(2)}) collective-permute-start(f32[1,9,128,128]{3,2,1,0:T(8,128)} %get-tuple-element.10), channel_id=1, source_target_pairs={{0,7},{1,0},{2,1},{3,2},{4,3},{5,4},{6,5},{7,6},{8,15},{9,8},{10,9... | collective-permute-start | bytes 1769480 | tf_op jit(solution)/shard_map/ppermute | solution.py:16
  48.1 1.7 %gather_fusion.1 = f32[15,128,128]{2,1,0:T(8,128)S(1)} fusion(f32[1,9,128,128]{3,2,1,0:T(8,128)} %get-tuple-element.8, s32[15]{0:T(128)S(1)} %or_bitcast_fusion.2), kind=kCustom, calls=%fused_computation.1 | custom fusion | bytes 1966200 | tf_op jit(solution)/shard_map/gather | solution.py:179
  49.8 13.8 %collective-permute-done.2 = f32[1,9,128,128]{3,2,1,0:T(8,128)S(1)} collective-permute-done((f32[1,9,128,128]{3,2,1,0:T(8,128)}, f32[1,9,128,128]{3,2,1,0:T(8,128)S(1)}, u32[]{:S(2)}, u32[]{:S(2)}) %collective-permute-start.2) | collective-permute-done | bytes 589856 | tf_op jit(solution)/shard_map/ppermute | solution.py:16
  63.6 0.6 gather_fusion.2
  64.2 1.5 %collective-permute-done.3 = f32[1,9,128,128]{3,2,1,0:T(8,128)S(1)} collective-permute-done((f32[1,9,128,128]{3,2,1,0:T(8,128)}, f32[1,9,128,128]{3,2,1,0:T(8,128)S(1)}, u32[]{:S(2)}, u32[]{:S(2)}) %collective-permute-start.3) | collective-permute-done | bytes 589856 | tf_op jit(solution)/shard_map/ppermute | solution.py:16
  65.7 0.6 gather_fusion.3
  66.3 1.9 %fusion = f32[1,15,128,128]{3,2,1,0:T(8,128)} fusion(f32[15,128,128]{2,1,0:T(8,128)S(1)} %gather_fusion.3, f32[15,128,128]{2,1,0:T(8,128)S(1)} %gather_fusion.2, f32[15,128,128]{2,1,0:T(8,128)S(1)} %gather_fusion.1, pred[15]{0:T(512)(128)(4,1)} %get-tuple-element.24, pred[15]{0:T(512)(128)(4,1)S(1)} %get-tuple-element.23, pred[15]{0:T(512)(128)(4,1)S(1)} %get-tuple-element.11), kind=kLoop, calls=%fused_computation.5 | loop fusion | flops 1228800 | bytes 3932205 | tf_op jit(solution)/shard_map/add | solution.py:182
  (28 shorter events, 0.3 us)
Async XLA Ops:
  0.0 1.3 %copy-start.2 = (s32[16,2]{0,1:T(2,128)S(1)}, s32[16,2]{0,1:T(2,128)}, u32[]{:S(2)}) copy-start(s32[16,2]{0,1:T(2,128)} %param.8) | copy-start | bytes 388
  0.0 8.5 %copy-start.3 = (s32[16,8]{0,1:T(8,128)S(1)}, s32[16,8]{0,1:T(8,128)}, u32[]{:S(2)}) copy-start(s32[16,8]{0,1:T(8,128)} %param.6) | copy-start | bytes 1540
  0.0 9.0 %copy-start.4 = (s32[1,15]{1,0:T(1,128)S(1)}, s32[1,15]{1,0:T(1,128)}, u32[]{:S(2)}) copy-start(s32[1,15]{1,0:T(1,128)} %param.9) | copy-start | bytes 184
  1.6 12.1 %collective-permute-start = (f32[5,2,128,128]{3,2,1,0:T(8,128)S(1)}, f32[5,2,128,128]{3,2,1,0:T(8,128)S(1)}, u32[]{:S(2)}, u32[]{:S(2)}) collective-permute-start(f32[5,2,128,128]{3,2,1,0:T(8,128)S(1)} %select_maximum_fusion.1), channel_id=1, source_target_pairs={{0,8},{8,16},{16,24},{1,9},{9,17},{17,25},{2,10},{10,18},{18,26},{... | collective-permute-start | bytes 1966088 | tf_op jit(solution)/shard_map/ppermute | solution.py:105
  6.4 11.9 %collective-permute-start.1 = (f32[5,2,128,128]{3,2,1,0:T(8,128)S(1)}, f32[5,2,128,128]{3,2,1,0:T(8,128)S(1)}, u32[]{:S(2)}, u32[]{:S(2)}) collective-permute-start(f32[5,2,128,128]{3,2,1,0:T(8,128)S(1)} %select_maximum_fusion), channel_id=1, source_target_pairs={{8,0},{16,8},{24,16},{9,1},{17,9},{25,17},{10,2},{18,10},{26,18},{... | collective-permute-start | bytes 1966088 | tf_op jit(solution)/shard_map/ppermute | solution.py:106
  13.7 6.2 %copy-start = (f32[5,2,128,128]{3,2,1,0:T(8,128)}, f32[5,2,128,128]{3,2,1,0:T(8,128)S(1)}, u32[]{:S(2)}) copy-start(f32[5,2,128,128]{3,2,1,0:T(8,128)S(1)} %collective-permute-done.low_ref) | copy-start | bytes 1966084
  18.3 1.5 %copy-start.1 = (f32[5,2,128,128]{3,2,1,0:T(8,128)}, f32[5,2,128,128]{3,2,1,0:T(8,128)S(1)}, u32[]{:S(2)}) copy-start(f32[5,2,128,128]{3,2,1,0:T(8,128)S(1)} %collective-permute-done.1.up_ref) | copy-start | bytes 1966084
  43.8 19.8 %collective-permute-start.2 = (f32[1,9,128,128]{3,2,1,0:T(8,128)}, f32[1,9,128,128]{3,2,1,0:T(8,128)S(1)}, u32[]{:S(2)}, u32[]{:S(2)}) collective-permute-start(f32[1,9,128,128]{3,2,1,0:T(8,128)} %get-tuple-element.9), channel_id=1, source_target_pairs={{0,1},{1,2},{2,3},{3,4},{4,5},{5,6},{6,7},{7,0},{8,9},{9,10},{10,1... | collective-permute-start | bytes 1769480 | tf_op jit(solution)/shard_map/ppermute | solution.py:16
  45.0 20.7 %collective-permute-start.3 = (f32[1,9,128,128]{3,2,1,0:T(8,128)}, f32[1,9,128,128]{3,2,1,0:T(8,128)S(1)}, u32[]{:S(2)}, u32[]{:S(2)}) collective-permute-start(f32[1,9,128,128]{3,2,1,0:T(8,128)} %get-tuple-element.10), channel_id=1, source_target_pairs={{0,7},{1,0},{2,1},{3,2},{4,3},{5,4},{6,5},{7,6},{8,15},{9,8},{10,9... | collective-permute-start | bytes 1769480 | tf_op jit(solution)/shard_map/ppermute | solution.py:16

commit v7 on v6

--- a/solution.py
+++ b/solution.py
@@ -32,9 +32,26 @@
     return jnp.concatenate([hi, lo, hi], axis=0)
 
 
-def triple_kernel(
-    coupling_slots, interp_slots, blocks, region,
-    idx_ref, a_ref, low_ref, mid_ref, up_ref, lo_ref, own_ref, hi_ref,
+def accumulate(idx_ref, owner_base, interp_slots, g, pt, y_tiles, acc_ref):
+    bs = pt.shape[1] // 3
+    owners = [idx_ref[owner_base + g * interp_slots + q] for q in range(interp_slots)]
+    for c, y in enumerate(y_tiles):
+        res = jnp.dot(pt, stack_rhs(y), preferred_element_type=jnp.float32)
+        for q in range(interp_slots):
+            acc_ref[owners[q], c] += res[q * bs : (q + 1) * bs]
+
+
+def flush(g, rows, blocks, acc_ref, lo_ref, own_ref, hi_ref):
+    @pl.when(g == rows - 1)
+    def _():
+        lo_ref[...] = acc_ref[:blocks]
+        own_ref[...] = acc_ref[blocks : 2 * blocks]
+        hi_ref[...] = acc_ref[2 * blocks :]
+
+
+def product_kernel(
+    coupling_slots, interp_slots, blocks, group,
+    idx_ref, a_ref, low_ref, mid_ref, up_ref, lo_ref, own_ref, hi_ref, rest_ref,
     y_ref, acc_ref, p3_ref,
 ):
     g = pl.program_id(0)
@@ -70,18 +87,28 @@
         for p in range(interp_slots):
             slot = idx_ref[slot_base + (g * coupling_slots + a) * interp_slots + p]
             y_ref[slot] += prod[:, p * bs : (p + 1) * bs]
+    rest_ref[0] = y_ref[group:]
     pt = stack_lhs(jnp.concatenate([mid_ref[g, q].T for q in range(interp_slots)], axis=0))
-    owners = [idx_ref[owner_base + g * interp_slots + q] for q in range(interp_slots)]
-    for c in range(region):
-        res = jnp.dot(pt, stack_rhs(y_ref[c]), preferred_element_type=jnp.float32)
-        for q in range(interp_slots):
-            acc_ref[owners[q], c] += res[q * bs : (q + 1) * bs]
-
-    @pl.when(g == rows - 1)
+    accumulate(idx_ref, owner_base, interp_slots, g, pt, [y_ref[c] for c in range(group)], acc_ref)
+    flush(g, rows, blocks, acc_ref, lo_ref, own_ref, hi_ref)
+
+
+def group_kernel(
+    coupling_slots, interp_slots, blocks, group,
+    idx_ref, y_ref, p_ref, lo_ref, own_ref, hi_ref, acc_ref,
+):
+    g = pl.program_id(0)
+    rows = pl.num_programs(0)
+    slot_base = rows * coupling_slots
+    owner_base = slot_base + rows * coupling_slots * interp_slots
+
+    @pl.when(g == 0)
     def _():
-        lo_ref[...] = acc_ref[:blocks]
-        own_ref[...] = acc_ref[blocks : 2 * blocks]
-        hi_ref[...] = acc_ref[2 * blocks :]
+        acc_ref[...] = jnp.zeros_like(acc_ref)
+
+    pt = stack_lhs(jnp.concatenate([p_ref[0, q].T for q in range(interp_slots)], axis=0))
+    accumulate(idx_ref, owner_base, interp_slots, g, pt, [y_ref[0, c] for c in range(group)], acc_ref)
+    flush(g, rows, blocks, acc_ref, lo_ref, own_ref, hi_ref)
 
 
 def shards(a_tiles, a_cols, p_tiles, p_cols, c_cols):
@@ -134,15 +161,16 @@
     relative = jnp.remainder(targets // blocks - t + 1, tiles)
     owner = jnp.clip(relative * blocks + targets % blocks, 0, 3 * blocks - 1)
 
-    kernel = functools.partial(triple_kernel, coupling_slots, interp_slots, blocks, region)
-    part = jax.ShapeDtypeStruct((blocks, region, bs, bs), jnp.float32)
-    part_spec = pl.BlockSpec((blocks, region, bs, bs), lambda g, *_: (0, 0, 0, 0))
+    group = 3 * blocks
+    part = jax.ShapeDtypeStruct((blocks, group, bs, bs), jnp.float32)
+    part_spec = pl.BlockSpec((blocks, group, bs, bs), lambda g, *_: (0, 0, 0, 0))
+    params = pltpu.CompilerParams(dimension_semantics=("arbitrary",))
     table = jnp.concatenate(
         [local_index.reshape(-1), slot.reshape(-1), owner.reshape(-1)]
     ).astype(jnp.int32)
-    to_lower, own_part, to_upper = pl.pallas_call(
-        kernel,
-        out_shape=(part, part, part),
+    *first, rest = pl.pallas_call(
+        functools.partial(product_kernel, coupling_slots, interp_slots, blocks, group),
+        out_shape=(part, part, part, jax.ShapeDtypeStruct((rows, region - group, bs, bs), jnp.float32)),
         grid_spec=pltpu.PrefetchScalarGridSpec(
             num_scalar_prefetch=1,
             grid=(rows,),
@@ -152,18 +180,55 @@
                 pl.BlockSpec(p_tiles.shape, lambda g, *_: (0, 0, 0, 0)),
                 pl.BlockSpec(up.shape, lambda g, *_: (0, 0, 0, 0)),
             ],
-            out_specs=(part_spec, part_spec, part_spec),
+            out_specs=(
+                part_spec, part_spec, part_spec,
+                pl.BlockSpec((1, region - group, bs, bs), lambda g, *_: (g, 0, 0, 0)),
+            ),
             scratch_shapes=[
                 pltpu.VMEM((region, bs, bs), jnp.float32),
-                pltpu.VMEM((3 * blocks, region, bs, bs), jnp.float32),
+                pltpu.VMEM((3 * blocks, group, bs, bs), jnp.float32),
                 pltpu.VMEM((ext_rows, 3 * bs, interp_slots * bs), jnp.bfloat16),
             ],
         ),
-        compiler_params=pltpu.CompilerParams(dimension_semantics=("arbitrary",)),
+        compiler_params=params,
+        cost_estimate=pl.CostEstimate(
+            flops=6 * rows * bs * bs * bs * (coupling_slots * interp_slots + group * interp_slots),
+            transcendentals=0,
+            bytes_accessed=4 * bs * bs * rows * (coupling_slots + interp_slots + region),
+        ),
     )(table, a_tiles, low, p_tiles, up)
-
-    from_lower = passed_along(to_upper, "tile", 1)
-    from_upper = passed_along(to_lower, "tile", -1)
+    groups = [first]
+    received = [(passed_along(first[2], "tile", 1), passed_along(first[0], "tile", -1))]
+    for k in range(region // group - 1):
+        if k > 0:
+            received[-2], rest = lax.optimization_barrier((received[-2], rest))
+        groups.append(
+            pl.pallas_call(
+                functools.partial(group_kernel, coupling_slots, interp_slots, blocks, group),
+                out_shape=(part, part, part),
+                grid_spec=pltpu.PrefetchScalarGridSpec(
+                    num_scalar_prefetch=1,
+                    grid=(rows,),
+                    in_specs=[
+                        pl.BlockSpec((1, group, bs, bs), lambda g, *_, k=k: (g, k, 0, 0)),
+                        pl.BlockSpec((1, interp_slots, bs, bs), lambda g, *_: (g, 0, 0, 0)),
+                    ],
+                    out_specs=(part_spec, part_spec, part_spec),
+                    scratch_shapes=[pltpu.VMEM((3 * blocks, group, bs, bs), jnp.float32)],
+                ),
+                compiler_params=params,
+                cost_estimate=pl.CostEstimate(
+                    flops=6 * rows * bs * bs * bs * group * interp_slots,
+                    transcendentals=0,
+                    bytes_accessed=4 * bs * bs * rows * (group + interp_slots),
+                ),
+            )(table, rest, p_tiles)
+        )
+        received.append((passed_along(groups[-1][2], "tile", 1), passed_along(groups[-1][0], "tile", -1)))
+
+    own_part = jnp.concatenate([parts[1] for parts in groups], axis=1)
+    from_lower = jnp.concatenate([pair[0] for pair in received], axis=1)
+    from_upper = jnp.concatenate([pair[1] for pair in received], axis=1)
 
     c_slab = c_cols // (tiles * blocks)
     c_tile = (c_cols // blocks) % tiles

time: 68.5 us -> 85.3 us (1.25); the launches traced: 68.2 us -> 84.1 us
  Pallas kernels: 23.9 us -> 47.8 us
  waiting for transfers between devices: 23.8 us -> 7.47 us
  starting transfers between devices: 10.7 us -> 16.3 us
  other arithmetic: 3.41 us -> 6.63 us
    pallas_call x1 -> x3, Pallas kernels: 23.9 us -> 47.8 us  [the longest x2 26.7 us: shards(): pl.pallas_call(functools.partial(group_kernel, coupling_slots, interp_slo...]
    ppermute x2 -> x6, waiting for transfers between devices: 15.3 us -> 1.72 us  [passed_along(): return lax.ppermute(value, axis, pairs)]
    ppermute x2 -> x6, starting transfers between devices: 4.25 us -> 9.82 us  [passed_along(): return lax.ppermute(value, axis, pairs)]
    ppermute x1, waiting for transfers between devices: 4.01 us -> 1.22 us  [shards(): lax.ppermute(halo(rows - RIM), 'slab', [(i, i + 1) for i in range(slabs -...]
    gather x3, local copies, waits for them, and re-layouts: 2.9 us -> 1.84 us  [pick(): tiles_picked = part[r_idx, idx]]
    concatenate x0 -> x3, other arithmetic: none -> 1.04 us  [the longest x1 0.97 us: shards(): own_part = jnp.concatenate([parts[1] for parts in groups], axis=1)]
  transfers between devices with their start and end apart: 4 -> 8, of which waited for: 4 -> 4; matrix products, arithmetic and copies ran while one was open for 6% -> 8% of each run, Pallas kernels for 0% -> 32%
where the time goes in v7:
time: 85.3 us; the launch traced here: 84.1 us
  Pallas kernels  47.8 us (56%)
  starting transfers between devices  16.3 us (19%)
  waiting for transfers between devices  7.47 us (9%)
  other arithmetic  6.63 us (8%)
  local copies, waits for them, and re-layouts  5.72 us (7%)
    pallas_call x2, Pallas kernels, shards(): pl.pallas_call(functools.partial(group_kernel, coupling_slots, interp_slo...  26.7 us
    pallas_call x1, Pallas kernels, shards(): pl.pallas_call(functools.partial(product_kernel, coupling_slots, interp_s...  21.1 us
    ppermute x6, starting transfers between devices, passed_along(): return lax.ppermute(value, axis, pairs)  9.82 us
    ppermute x1, starting transfers between devices, shards(): lax.ppermute(halo(rows - RIM), 'slab', [(i, i + 1) for i in range(slabs -...  4.54 us
    ppermute x1, waiting for transfers between devices, shards(): up = lax.ppermute(halo(0), 'slab', [(i + 1, i) for i in range(slabs - 1)])  4.52 us
    ppermute x1, starting transfers between devices, shards(): up = lax.ppermute(halo(0), 'slab', [(i + 1, i) for i in range(slabs - 1)])  1.92 us
    gather x3, local copies, waits for them, and re-layouts, pick(): tiles_picked = part[r_idx, idx]  1.84 us
    ppermute x6, waiting for transfers between devices, passed_along(): return lax.ppermute(value, axis, pairs)  1.72 us
  transfers between devices with their start and end apart: 8, of which 4 were waited for; matrix products, arithmetic and copies ran while one was open for 8% of the time, Pallas kernels for 32%

profile of v7, /device:TPU:1, one launch (start us, length us, event | category | flops | bytes accessed | tf_op | source)
XLA Modules:
  0.0 84.1 jit_solution(10274130325446128295)
XLA Ops:
  0.0 1.3 %fusion.19 = (f32[4,2,128,128]{3,2,1,0:T(8,128)S(1)}, f32[4,2,128,128]{3,2,1,0:T(8,128)S(1)}) fusion(f32[16,2,128,128]{3,2,1,0:T(8,128)} %p_ref.3), kind=kLoop, calls=%fused_computation.74 | loop fusion | bytes 2097152 | tf_op jit(solution)/shard_map/slice | solution.py:130
  1.3 0.8 slice_convert_fusion.1
  2.1 0.1 copy.27
  2.3 4.5 %collective-permute-start = (f32[5,2,128,128]{3,2,1,0:T(8,128)S(1)}, f32[5,2,128,128]{3,2,1,0:T(8,128)S(1)}, u32[]{:S(2)}, u32[]{:S(2)}) collective-permute-start(f32[5,2,128,128]{3,2,1,0:T(8,128)S(1)} %select_maximum_fusion.1), channel_id=1, source_target_pairs={{0,8},{8,16},{16,24},{1,9},{9,17},{17,25},{2,10},{10,18},{18,26},{... | collective-permute-start | bytes 1966088 | tf_op jit(solution)/shard_map/ppermute | solution.py:132
  6.9 0.1 copy.28
  7.1 1.9 %collective-permute-start.1 = (f32[5,2,128,128]{3,2,1,0:T(8,128)S(1)}, f32[5,2,128,128]{3,2,1,0:T(8,128)S(1)}, u32[]{:S(2)}, u32[]{:S(2)}) collective-permute-start(f32[5,2,128,128]{3,2,1,0:T(8,128)S(1)} %select_maximum_fusion), channel_id=1, source_target_pairs={{8,0},{16,8},{24,16},{9,1},{17,9},{25,17},{10,2},{18,10},{26,18},{... | collective-permute-start | bytes 1966088 | tf_op jit(solution)/shard_map/ppermute | solution.py:133
  9.1 0.8 copy.29
  9.8 0.7 fusion.4
  10.5 0.7 and_bitcast_fusion.2
  11.2 0.7 fusion.13
  11.9 0.7 compare_select_fusion
  13.0 0.1 reshape.66
  13.2 1.2 %collective-permute-done.low_ref = f32[5,2,128,128]{3,2,1,0:T(8,128)S(1)} collective-permute-done((f32[5,2,128,128]{3,2,1,0:T(8,128)S(1)}, f32[5,2,128,128]{3,2,1,0:T(8,128)S(1)}, u32[]{:S(2)}, u32[]{:S(2)}) %collective-permute-start) | collective-permute-done | bytes 655392 | tf_op jit(solution)/shard_map/ppermute | solution.py:132
  14.5 4.5 %collective-permute-done.1.up_ref = f32[5,2,128,128]{3,2,1,0:T(8,128)S(1)} collective-permute-done((f32[5,2,128,128]{3,2,1,0:T(8,128)S(1)}, f32[5,2,128,128]{3,2,1,0:T(8,128)S(1)}, u32[]{:S(2)}, u32[]{:S(2)}) %collective-permute-start.1) | collective-permute-done | bytes 655392 | tf_op jit(solution)/shard_map/ppermute | solution.py:133
  19.1 0.6 gather_fusion
  19.8 0.1 gather.15
  20.0 0.6 pad_add_fusion.1.idx_ref
  20.5 21.1 %shard_map.55 = (f32[1,3,128,128]{3,2,1,0:T(8,128)}, f32[1,3,128,128]{3,2,1,0:T(8,128)}, f32[1,3,128,128]{3,2,1,0:T(8,128)}, f32[16,6,128,128]{3,2,1,0:T(8,128)}) custom-call(s32[416]{0:T(512)} %pad_add_fusion.1.idx_ref, f32[16,8,128,128]{3,2,1,0:T(8,128)} %a_ref.1, f32[5,2,128,128]{3,2,1,0:T(8,128)} %copy-done.2, f32[16,2,128,128]{3,2,1,0:T(8,128)} %p_ref.3, ...), custom_call_target="tpu_custom_call" | custom-call | flops 4429185024 | bytes 19922944 | tf_op jit(solution)/shard_map/pallas_call | solution.py:171
  41.6 1.2 %collective-permute-start.2 = (f32[1,3,128,128]{3,2,1,0:T(8,128)}, f32[1,3,128,128]{3,2,1,0:T(8,128)S(1)}, u32[]{:S(2)}, u32[]{:S(2)}) collective-permute-start(f32[1,3,128,128]{3,2,1,0:T(8,128)} %get-tuple-element.21), channel_id=1, source_target_pairs={{0,1},{1,2},{2,3},{3,4},{4,5},{5,6},{6,7},{7,0},{8,9},{9,10},{10,1... | collective-permute-start | bytes 589832 | tf_op jit(solution)/shard_map/ppermute | solution.py:16
  42.8 3.0 %collective-permute-start.3 = (f32[1,3,128,128]{3,2,1,0:T(8,128)}, f32[1,3,128,128]{3,2,1,0:T(8,128)S(1)}, u32[]{:S(2)}, u32[]{:S(2)}) collective-permute-start(f32[1,3,128,128]{3,2,1,0:T(8,128)} %get-tuple-element.22), channel_id=1, source_target_pairs={{0,7},{1,0},{2,1},{3,2},{4,3},{5,4},{6,5},{7,6},{8,15},{9,8},{10,9... | collective-permute-start | bytes 589832 | tf_op jit(solution)/shard_map/ppermute | solution.py:16
  45.9 13.3 %shard_map.56 = (f32[1,3,128,128]{3,2,1,0:T(8,128)}, f32[1,3,128,128]{3,2,1,0:T(8,128)}, f32[1,3,128,128]{3,2,1,0:T(8,128)}) custom-call(s32[416]{0:T(512)} %pad_add_fusion.1.idx_ref, f32[16,6,128,128]{3,2,1,0:T(8,128)} %get-tuple-element.23.y_ref, f32[16,2,128,128]{3,2,1,0:T(8,128)} %p_ref.3), custom_call_target="tpu_custom_call" | custom-call | flops 1207959552 | bytes 5242880 | tf_op jit(solution)/shard_map/pallas_call | solution.py:206
  59.3 13.4 %shard_map.57 = (f32[1,3,128,128]{3,2,1,0:T(8,128)}, f32[1,3,128,128]{3,2,1,0:T(8,128)}, f32[1,3,128,128]{3,2,1,0:T(8,128)}) custom-call(s32[416]{0:T(512)} %pad_add_fusion.1.idx_ref, f32[16,6,128,128]{3,2,1,0:T(8,128)} %get-tuple-element.23.y_ref, f32[16,2,128,128]{3,2,1,0:T(8,128)} %p_ref.3), custom_call_target="tpu_custom_call" | custom-call | flops 1207959552 | bytes 5242880 | tf_op jit(solution)/shard_map/pallas_call | solution.py:206
  72.7 0.4 collective-permute-start.5
  73.1 3.8 %collective-permute-start.6 = (f32[1,3,128,128]{3,2,1,0:T(8,128)S(1)}, f32[1,3,128,128]{3,2,1,0:T(8,128)S(1)}, u32[]{:S(2)}, u32[]{:S(2)}) collective-permute-start(f32[1,3,128,128]{3,2,1,0:T(8,128)S(1)} %copy-done.4), channel_id=1, source_target_pairs={{0,7},{1,0},{2,1},{3,2},{4,3},{5,4},{6,5},{7,6},{8,15},{9,8},{10,9... | collective-permute-start | bytes 589832 | tf_op jit(solution)/shard_map/ppermute | solution.py:16
  76.9 1.3 %collective-permute-start.7 = (f32[1,3,128,128]{3,2,1,0:T(8,128)}, f32[1,3,128,128]{3,2,1,0:T(8,128)S(1)}, u32[]{:S(2)}, u32[]{:S(2)}) collective-permute-start(f32[1,3,128,128]{3,2,1,0:T(8,128)} %get-tuple-element.30), channel_id=1, source_target_pairs={{0,7},{1,0},{2,1},{3,2},{4,3},{5,4},{6,5},{7,6},{8,15},{9,8},{10,9... | collective-permute-start | bytes 589832 | tf_op jit(solution)/shard_map/ppermute | solution.py:16
  78.2 1.0 %pad_maximum_fusion = f32[1,9,128,128]{3,2,1,0:T(8,128)S(1)} fusion(f32[1,3,128,128]{3,2,1,0:T(8,128)} %get-tuple-element.24, f32[1,3,128,128]{3,2,1,0:T(8,128)S(1)} %copy-done.1, f32[1,3,128,128]{3,2,1,0:T(8,128)S(1)} %copy-done), kind=kLoop, calls=%fused_computation.12 | loop fusion | flops 294912 | bytes 1179648 | tf_op jit(solution)/shard_map/concatenate | solution.py:229
  79.2 0.6 gather_fusion.1
  79.8 0.5 collective-permute-done.5
  80.3 0.6 gather_fusion.2
  81.0 1.3 %collective-permute-done.7 = f32[1,3,128,128]{3,2,1,0:T(8,128)S(1)} collective-permute-done((f32[1,3,128,128]{3,2,1,0:T(8,128)}, f32[1,3,128,128]{3,2,1,0:T(8,128)S(1)}, u32[]{:S(2)}, u32[]{:S(2)}) %collective-permute-start.7) | collective-permute-done | bytes 196640 | tf_op jit(solution)/shard_map/ppermute | solution.py:16
  82.3 0.6 gather_fusion.3
  82.9 1.2 %fusion = f32[1,15,128,128]{3,2,1,0:T(8,128)} fusion(f32[15,128,128]{2,1,0:T(8,128)S(1)} %gather_fusion.3, f32[15,128,128]{2,1,0:T(8,128)S(1)} %gather_fusion.2, f32[15,128,128]{2,1,0:T(8,128)S(1)} %gather_fusion.1, pred[15]{0:T(512)(128)(4,1)S(1)} %get-tuple-element.44, pred[15]{0:T(512)(128)(4,1)S(1)} %get-tuple-element.43, ...), kind=kLoop, calls=%fused_computation.5 | loop fusion | flops 1228800 | bytes 3932205 | tf_op jit(solution)/shard_map/add | solution.py:247
  (41 shorter events, 1.1 us)
Async XLA Ops:
  2.3 12.1 %collective-permute-start = (f32[5,2,128,128]{3,2,1,0:T(8,128)S(1)}, f32[5,2,128,128]{3,2,1,0:T(8,128)S(1)}, u32[]{:S(2)}, u32[]{:S(2)}) collective-permute-start(f32[5,2,128,128]{3,2,1,0:T(8,128)S(1)} %select_maximum_fusion.1), channel_id=1, source_target_pairs={{0,8},{8,16},{16,24},{1,9},{9,17},{17,25},{2,10},{10,18},{18,26},{... | collective-permute-start | bytes 1966088 | tf_op jit(solution)/shard_map/ppermute | solution.py:132
  7.1 11.9 %collective-permute-start.1 = (f32[5,2,128,128]{3,2,1,0:T(8,128)S(1)}, f32[5,2,128,128]{3,2,1,0:T(8,128)S(1)}, u32[]{:S(2)}, u32[]{:S(2)}) collective-permute-start(f32[5,2,128,128]{3,2,1,0:T(8,128)S(1)} %select_maximum_fusion), channel_id=1, source_target_pairs={{8,0},{16,8},{24,16},{9,1},{17,9},{25,17},{10,2},{18,10},{26,18},{... | collective-permute-start | bytes 1966088 | tf_op jit(solution)/shard_map/ppermute | solution.py:133
  14.4 6.1 %copy-start.2 = (f32[5,2,128,128]{3,2,1,0:T(8,128)}, f32[5,2,128,128]{3,2,1,0:T(8,128)S(1)}, u32[]{:S(2)}) copy-start(f32[5,2,128,128]{3,2,1,0:T(8,128)S(1)} %collective-permute-done.low_ref) | copy-start | bytes 1966084
  19.0 1.5 %copy-start.3 = (f32[5,2,128,128]{3,2,1,0:T(8,128)}, f32[5,2,128,128]{3,2,1,0:T(8,128)S(1)}, u32[]{:S(2)}) copy-start(f32[5,2,128,128]{3,2,1,0:T(8,128)S(1)} %collective-permute-done.1.up_ref) | copy-start | bytes 1966084
  41.6 17.6 %collective-permute-start.2 = (f32[1,3,128,128]{3,2,1,0:T(8,128)}, f32[1,3,128,128]{3,2,1,0:T(8,128)S(1)}, u32[]{:S(2)}, u32[]{:S(2)}) collective-permute-start(f32[1,3,128,128]{3,2,1,0:T(8,128)} %get-tuple-element.21), channel_id=1, source_target_pairs={{0,1},{1,2},{2,3},{3,4},{4,5},{5,6},{6,7},{7,0},{8,9},{9,10},{10,1... | collective-permute-start | bytes 589832 | tf_op jit(solution)/shard_map/ppermute | solution.py:16
  42.8 16.4 %collective-permute-start.3 = (f32[1,3,128,128]{3,2,1,0:T(8,128)}, f32[1,3,128,128]{3,2,1,0:T(8,128)S(1)}, u32[]{:S(2)}, u32[]{:S(2)}) collective-permute-start(f32[1,3,128,128]{3,2,1,0:T(8,128)} %get-tuple-element.22), channel_id=1, source_target_pairs={{0,7},{1,0},{2,1},{3,2},{4,3},{5,4},{6,5},{7,6},{8,15},{9,8},{10,9... | collective-permute-start | bytes 589832 | tf_op jit(solution)/shard_map/ppermute | solution.py:16
  59.2 14.0 %copy-start.4 = (f32[1,3,128,128]{3,2,1,0:T(8,128)S(1)}, f32[1,3,128,128]{3,2,1,0:T(8,128)}, u32[]{:S(2)}) copy-start(f32[1,3,128,128]{3,2,1,0:T(8,128)} %get-tuple-element.29) | copy-start | bytes 589828
  59.2 19.0 %copy-start = (f32[1,3,128,128]{3,2,1,0:T(8,128)S(1)}, f32[1,3,128,128]{3,2,1,0:T(8,128)}, u32[]{:S(2)}) copy-start(f32[1,3,128,128]{3,2,1,0:T(8,128)} %get-tuple-element.18) | copy-start | bytes 589828
  59.2 19.0 %copy-start.1 = (f32[1,3,128,128]{3,2,1,0:T(8,128)S(1)}, f32[1,3,128,128]{3,2,1,0:T(8,128)}, u32[]{:S(2)}) copy-start(f32[1,3,128,128]{3,2,1,0:T(8,128)} %get-tuple-element.20) | copy-start | bytes 589828
  59.2 20.6 %collective-permute-start.4 = (f32[1,3,128,128]{3,2,1,0:T(8,128)}, f32[1,3,128,128]{3,2,1,0:T(8,128)S(1)}, u32[]{:S(2)}, u32[]{:S(2)}) collective-permute-start(f32[1,3,128,128]{3,2,1,0:T(8,128)} %get-tuple-element.26), channel_id=1, source_target_pairs={{0,1},{1,2},{2,3},{3,4},{4,5},{5,6},{6,7},{7,0},{8,9},{9,10},{10,1... | collective-permute-start | bytes 589832 | tf_op jit(solution)/shard_map/ppermute | solution.py:16
  72.7 7.6 %collective-permute-start.5 = (f32[1,3,128,128]{3,2,1,0:T(8,128)}, f32[1,3,128,128]{3,2,1,0:T(8,128)S(1)}, u32[]{:S(2)}, u32[]{:S(2)}) collective-permute-start(f32[1,3,128,128]{3,2,1,0:T(8,128)} %get-tuple-element.27), channel_id=1, source_target_pairs={{0,1},{1,2},{2,3},{3,4},{4,5},{5,6},{6,7},{7,0},{8,9},{9,10},{10,1... | collective-permute-start | bytes 589832 | tf_op jit(solution)/shard_map/ppermute | solution.py:16
  73.1 7.8 %collective-permute-start.6 = (f32[1,3,128,128]{3,2,1,0:T(8,128)S(1)}, f32[1,3,128,128]{3,2,1,0:T(8,128)S(1)}, u32[]{:S(2)}, u32[]{:S(2)}) collective-permute-start(f32[1,3,128,128]{3,2,1,0:T(8,128)S(1)} %copy-done.4), channel_id=1, source_target_pairs={{0,7},{1,0},{2,1},{3,2},{4,3},{5,4},{6,5},{7,6},{8,15},{9,8},{10,9... | collective-permute-start | bytes 589832 | tf_op jit(solution)/shard_map/ppermute | solution.py:16
  76.9 5.3 %collective-permute-start.7 = (f32[1,3,128,128]{3,2,1,0:T(8,128)}, f32[1,3,128,128]{3,2,1,0:T(8,128)S(1)}, u32[]{:S(2)}, u32[]{:S(2)}) collective-permute-start(f32[1,3,128,128]{3,2,1,0:T(8,128)} %get-tuple-element.30), channel_id=1, source_target_pairs={{0,7},{1,0},{2,1},{3,2},{4,3},{5,4},{6,5},{7,6},{8,15},{9,8},{10,9... | collective-permute-start | bytes 589832 | tf_op jit(solution)/shard_map/ppermute | solution.py:16

commit v8 on v6

--- a/solution.py
+++ b/solution.py
@@ -38,7 +38,9 @@
     y_ref, acc_ref, p3_ref,
 ):
     g = pl.program_id(0)
-    rows = pl.num_programs(0)
+    steps = pl.num_programs(0)
+    per_step = a_ref.shape[0]
+    rows = steps * per_step
     bs = a_ref.shape[2]
     slot_base = rows * coupling_slots
     owner_base = slot_base + rows * coupling_slots * interp_slots
@@ -63,21 +65,26 @@
         fill(mid_ref, RIM, rows)
         fill(up_ref, RIM + rows, RIM)
 
-    y_ref[...] = jnp.zeros_like(y_ref)
-    for a in range(coupling_slots):
-        row = idx_ref[g * coupling_slots + a]
-        prod = jnp.dot(stack_lhs(a_ref[0, a]), p3_ref[row], preferred_element_type=jnp.float32)
-        for p in range(interp_slots):
-            slot = idx_ref[slot_base + (g * coupling_slots + a) * interp_slots + p]
-            y_ref[slot] += prod[:, p * bs : (p + 1) * bs]
-    pt = stack_lhs(jnp.concatenate([mid_ref[g, q].T for q in range(interp_slots)], axis=0))
-    owners = [idx_ref[owner_base + g * interp_slots + q] for q in range(interp_slots)]
-    for c in range(region):
-        res = jnp.dot(pt, stack_rhs(y_ref[c]), preferred_element_type=jnp.float32)
-        for q in range(interp_slots):
-            acc_ref[owners[q], c] += res[q * bs : (q + 1) * bs]
-
-    @pl.when(g == rows - 1)
+    def row_step(i, carry):
+        gi = g * per_step + i
+        y_ref[...] = jnp.zeros_like(y_ref)
+        for a in range(coupling_slots):
+            row = idx_ref[gi * coupling_slots + a]
+            prod = jnp.dot(stack_lhs(a_ref[i, a]), p3_ref[row], preferred_element_type=jnp.float32)
+            for p in range(interp_slots):
+                slot = idx_ref[slot_base + (gi * coupling_slots + a) * interp_slots + p]
+                y_ref[slot] += prod[:, p * bs : (p + 1) * bs]
+        pt = stack_lhs(jnp.concatenate([mid_ref[gi, q].T for q in range(interp_slots)], axis=0))
+        owners = [idx_ref[owner_base + gi * interp_slots + q] for q in range(interp_slots)]
+        for c in range(region):
+            res = jnp.dot(pt, stack_rhs(y_ref[c]), preferred_element_type=jnp.float32)
+            for q in range(interp_slots):
+                acc_ref[owners[q], c] += res[q * bs : (q + 1) * bs]
+        return carry
+
+    lax.fori_loop(0, per_step, row_step, 0)
+
+    @pl.when(g == steps - 1)
     def _():
         lo_ref[...] = acc_ref[:blocks]
         own_ref[...] = acc_ref[blocks : 2 * blocks]
@@ -134,6 +141,7 @@
     relative = jnp.remainder(targets // blocks - t + 1, tiles)
     owner = jnp.clip(relative * blocks + targets % blocks, 0, 3 * blocks - 1)
 
+    per_step = next(d for d in (4, 2, 1) if rows % d == 0)
     kernel = functools.partial(triple_kernel, coupling_slots, interp_slots, blocks, region)
     part = jax.ShapeDtypeStruct((blocks, region, bs, bs), jnp.float32)
     part_spec = pl.BlockSpec((blocks, region, bs, bs), lambda g, *_: (0, 0, 0, 0))
@@ -145,9 +153,9 @@
         out_shape=(part, part, part),
         grid_spec=pltpu.PrefetchScalarGridSpec(
             num_scalar_prefetch=1,
-            grid=(rows,),
+            grid=(rows // per_step,),
             in_specs=[
-                pl.BlockSpec((1, coupling_slots, bs, bs), lambda g, *_: (g, 0, 0, 0)),
+                pl.BlockSpec((per_step, coupling_slots, bs, bs), lambda g, *_: (g, 0, 0, 0)),
                 pl.BlockSpec(low.shape, lambda g, *_: (0, 0, 0, 0)),
                 pl.BlockSpec(p_tiles.shape, lambda g, *_: (0, 0, 0, 0)),
                 pl.BlockSpec(up.shape, lambda g, *_: (0, 0, 0, 0)),

time: 68.5 us -> 68.1 us (level)
  no operation moved by 1% of the time
where the time goes in v8:
time: 68.1 us; the launch traced here: 67.8 us
  waiting for transfers between devices  23.9 us (35%)
  Pallas kernels  23.5 us (35%)
  starting transfers between devices  10.7 us (16%)
  local copies, waits for them, and re-layouts  6.14 us (9%)
  other arithmetic  3.41 us (5%)
    pallas_call x1, Pallas kernels, shards(): pl.pallas_call(kernel, out_shape=(part, part, part), grid_spec=pltpu.Pref...  23.5 us
    ppermute x2, waiting for transfers between devices, passed_along(): return lax.ppermute(value, axis, pairs)  15.4 us
    ppermute x1, starting transfers between devices, shards(): lax.ppermute(halo(rows - RIM), 'slab', [(i, i + 1) for i in range(slabs -...  4.54 us
    ppermute x1, waiting for transfers between devices, shards(): up = lax.ppermute(halo(0), 'slab', [(i + 1, i) for i in range(slabs - 1)])  4.52 us
    ppermute x2, starting transfers between devices, passed_along(): return lax.ppermute(value, axis, pairs)  4.25 us
    ppermute x1, waiting for transfers between devices, shards(): lax.ppermute(halo(rows - RIM), 'slab', [(i, i + 1) for i in range(slabs -...  4.01 us
    gather x3, local copies, waits for them, and re-layouts, pick(): tiles_picked = part[r_idx, idx]  2.9 us
    ppermute x1, starting transfers between devices, shards(): up = lax.ppermute(halo(0), 'slab', [(i + 1, i) for i in range(slabs - 1)])  1.92 us
  transfers between devices with their start and end apart: 4, of which 4 were waited for; matrix products, arithmetic and copies ran while one was open for 6% of the time, Pallas kernels for 0%

profile of v8, /device:TPU:1, one launch (start us, length us, event | category | flops | bytes accessed | tf_op | source)
XLA Modules:
  0.0 67.8 jit_solution(5181689826894649883)
XLA Ops:
  0.0 1.3 %fusion.19 = (f32[4,2,128,128]{3,2,1,0:T(8,128)S(1)}, f32[4,2,128,128]{3,2,1,0:T(8,128)S(1)}) fusion(f32[16,2,128,128]{3,2,1,0:T(8,128)} %mid_ref.1), kind=kLoop, calls=%fused_computation.71 | loop fusion | bytes 2097152 | tf_op jit(solution)/shard_map/slice | solution.py:110
  1.3 0.1 slice_convert_fusion.1
  1.4 0.1 copy.27
  1.5 0.1 reshape.64
  1.6 4.5 %collective-permute-start = (f32[5,2,128,128]{3,2,1,0:T(8,128)S(1)}, f32[5,2,128,128]{3,2,1,0:T(8,128)S(1)}, u32[]{:S(2)}, u32[]{:S(2)}) collective-permute-start(f32[5,2,128,128]{3,2,1,0:T(8,128)S(1)} %select_maximum_fusion.1), channel_id=1, source_target_pairs={{0,8},{8,16},{16,24},{1,9},{9,17},{17,25},{2,10},{10,18},{18,26},{... | collective-permute-start | bytes 1966088 | tf_op jit(solution)/shard_map/ppermute | solution.py:112
  6.2 0.1 copy.28
  6.3 0.1 reshape.65
  6.4 1.9 %collective-permute-start.1 = (f32[5,2,128,128]{3,2,1,0:T(8,128)S(1)}, f32[5,2,128,128]{3,2,1,0:T(8,128)S(1)}, u32[]{:S(2)}, u32[]{:S(2)}) collective-permute-start(f32[5,2,128,128]{3,2,1,0:T(8,128)S(1)} %select_maximum_fusion), channel_id=1, source_target_pairs={{8,0},{16,8},{24,16},{9,1},{17,9},{25,17},{10,2},{18,10},{26,18},{... | collective-permute-start | bytes 1966088 | tf_op jit(solution)/shard_map/ppermute | solution.py:113
  8.4 0.1 copy.29
  8.5 0.1 copy.30
  8.6 0.1 reshape.69
  8.7 0.1 copy.26
  8.7 0.1 reshape.63
  8.8 0.1 copy.31
  8.9 0.1 reshape.66
  9.1 0.6 and_bitcast_fusion.1
  9.7 4.0 %collective-permute-done.low_ref = f32[5,2,128,128]{3,2,1,0:T(8,128)S(1)} collective-permute-done((f32[5,2,128,128]{3,2,1,0:T(8,128)S(1)}, f32[5,2,128,128]{3,2,1,0:T(8,128)S(1)}, u32[]{:S(2)}, u32[]{:S(2)}) %collective-permute-start) | collective-permute-done | bytes 655392 | tf_op jit(solution)/shard_map/ppermute | solution.py:112
  13.7 0.1 convert_element_type.25
  13.8 4.5 %collective-permute-done.1.up_ref = f32[5,2,128,128]{3,2,1,0:T(8,128)S(1)} collective-permute-done((f32[5,2,128,128]{3,2,1,0:T(8,128)S(1)}, f32[5,2,128,128]{3,2,1,0:T(8,128)S(1)}, u32[]{:S(2)}, u32[]{:S(2)}) %collective-permute-start.1) | collective-permute-done | bytes 655392 | tf_op jit(solution)/shard_map/ppermute | solution.py:113
  18.4 0.1 convert_element_type.28
  18.4 0.6 gather_fusion
  19.1 0.1 gather.15
  19.3 0.6 pad_add_fusion.1.idx_ref
  19.9 23.5 %shard_map.55 = (f32[1,9,128,128]{3,2,1,0:T(8,128)}, f32[1,9,128,128]{3,2,1,0:T(8,128)}, f32[1,9,128,128]{3,2,1,0:T(8,128)}) custom-call(s32[416]{0:T(512)} %pad_add_fusion.1.idx_ref, f32[16,8,128,128]{3,2,1,0:T(8,128)} %a_ref.1, f32[5,2,128,128]{3,2,1,0:T(8,128)} %copy-done, f32[16,2,128,128]{3,2,1,0:T(8,128)} %mid_ref.1, f32[5,2,128,128]{3,2,1,0:T(8,128)} %copy-done.1), custom_call_target="tpu_custom_call" | custom-call | tf_op jit(solution)/shard_map/pallas_call | solution.py:151
  43.4 1.2 %collective-permute-start.2 = (f32[1,9,128,128]{3,2,1,0:T(8,128)}, f32[1,9,128,128]{3,2,1,0:T(8,128)S(1)}, u32[]{:S(2)}, u32[]{:S(2)}) collective-permute-start(f32[1,9,128,128]{3,2,1,0:T(8,128)} %get-tuple-element.9), channel_id=1, source_target_pairs={{0,1},{1,2},{2,3},{3,4},{4,5},{5,6},{6,7},{7,0},{8,9},{9,10},{10,1... | collective-permute-start | bytes 1769480 | tf_op jit(solution)/shard_map/ppermute | solution.py:16
  44.6 3.0 %collective-permute-start.3 = (f32[1,9,128,128]{3,2,1,0:T(8,128)}, f32[1,9,128,128]{3,2,1,0:T(8,128)S(1)}, u32[]{:S(2)}, u32[]{:S(2)}) collective-permute-start(f32[1,9,128,128]{3,2,1,0:T(8,128)} %get-tuple-element.10), channel_id=1, source_target_pairs={{0,7},{1,0},{2,1},{3,2},{4,3},{5,4},{6,5},{7,6},{8,15},{9,8},{10,9... | collective-permute-start | bytes 1769480 | tf_op jit(solution)/shard_map/ppermute | solution.py:16
  47.7 1.7 %gather_fusion.1 = f32[15,128,128]{2,1,0:T(8,128)S(1)} fusion(f32[1,9,128,128]{3,2,1,0:T(8,128)} %get-tuple-element.8, s32[15]{0:T(128)S(1)} %or_bitcast_fusion.2), kind=kCustom, calls=%fused_computation.1 | custom fusion | bytes 1966200 | tf_op jit(solution)/shard_map/gather | solution.py:187
  49.4 13.9 %collective-permute-done.2 = f32[1,9,128,128]{3,2,1,0:T(8,128)S(1)} collective-permute-done((f32[1,9,128,128]{3,2,1,0:T(8,128)}, f32[1,9,128,128]{3,2,1,0:T(8,128)S(1)}, u32[]{:S(2)}, u32[]{:S(2)}) %collective-permute-start.2) | collective-permute-done | bytes 589856 | tf_op jit(solution)/shard_map/ppermute | solution.py:16
  63.3 0.6 gather_fusion.2
  63.9 1.5 %collective-permute-done.3 = f32[1,9,128,128]{3,2,1,0:T(8,128)S(1)} collective-permute-done((f32[1,9,128,128]{3,2,1,0:T(8,128)}, f32[1,9,128,128]{3,2,1,0:T(8,128)S(1)}, u32[]{:S(2)}, u32[]{:S(2)}) %collective-permute-start.3) | collective-permute-done | bytes 589856 | tf_op jit(solution)/shard_map/ppermute | solution.py:16
  65.3 0.6 gather_fusion.3
  66.0 1.9 %fusion = f32[1,15,128,128]{3,2,1,0:T(8,128)} fusion(f32[15,128,128]{2,1,0:T(8,128)S(1)} %gather_fusion.3, f32[15,128,128]{2,1,0:T(8,128)S(1)} %gather_fusion.2, f32[15,128,128]{2,1,0:T(8,128)S(1)} %gather_fusion.1, pred[15]{0:T(512)(128)(4,1)} %get-tuple-element.24, pred[15]{0:T(512)(128)(4,1)S(1)} %get-tuple-element.23, pred[15]{0:T(512)(128)(4,1)S(1)} %get-tuple-element.11), kind=kLoop, calls=%fused_computation.5 | loop fusion | flops 1228800 | bytes 3932205 | tf_op jit(solution)/shard_map/add | solution.py:190
  (28 shorter events, 0.3 us)
Async XLA Ops:
  0.0 1.3 %copy-start.2 = (s32[16,2]{0,1:T(2,128)S(1)}, s32[16,2]{0,1:T(2,128)}, u32[]{:S(2)}) copy-start(s32[16,2]{0,1:T(2,128)} %param.8) | copy-start | bytes 388
  0.0 8.5 %copy-start.3 = (s32[16,8]{0,1:T(8,128)S(1)}, s32[16,8]{0,1:T(8,128)}, u32[]{:S(2)}) copy-start(s32[16,8]{0,1:T(8,128)} %param.6) | copy-start | bytes 1540
  0.0 9.0 %copy-start.4 = (s32[1,15]{1,0:T(1,128)S(1)}, s32[1,15]{1,0:T(1,128)}, u32[]{:S(2)}) copy-start(s32[1,15]{1,0:T(1,128)} %param.9) | copy-start | bytes 184
  1.6 12.1 %collective-permute-start = (f32[5,2,128,128]{3,2,1,0:T(8,128)S(1)}, f32[5,2,128,128]{3,2,1,0:T(8,128)S(1)}, u32[]{:S(2)}, u32[]{:S(2)}) collective-permute-start(f32[5,2,128,128]{3,2,1,0:T(8,128)S(1)} %select_maximum_fusion.1), channel_id=1, source_target_pairs={{0,8},{8,16},{16,24},{1,9},{9,17},{17,25},{2,10},{10,18},{18,26},{... | collective-permute-start | bytes 1966088 | tf_op jit(solution)/shard_map/ppermute | solution.py:112
  6.4 11.9 %collective-permute-start.1 = (f32[5,2,128,128]{3,2,1,0:T(8,128)S(1)}, f32[5,2,128,128]{3,2,1,0:T(8,128)S(1)}, u32[]{:S(2)}, u32[]{:S(2)}) collective-permute-start(f32[5,2,128,128]{3,2,1,0:T(8,128)S(1)} %select_maximum_fusion), channel_id=1, source_target_pairs={{8,0},{16,8},{24,16},{9,1},{17,9},{25,17},{10,2},{18,10},{26,18},{... | collective-permute-start | bytes 1966088 | tf_op jit(solution)/shard_map/ppermute | solution.py:113
  13.7 6.2 %copy-start = (f32[5,2,128,128]{3,2,1,0:T(8,128)}, f32[5,2,128,128]{3,2,1,0:T(8,128)S(1)}, u32[]{:S(2)}) copy-start(f32[5,2,128,128]{3,2,1,0:T(8,128)S(1)} %collective-permute-done.low_ref) | copy-start | bytes 1966084
  18.3 1.5 %copy-start.1 = (f32[5,2,128,128]{3,2,1,0:T(8,128)}, f32[5,2,128,128]{3,2,1,0:T(8,128)S(1)}, u32[]{:S(2)}) copy-start(f32[5,2,128,128]{3,2,1,0:T(8,128)S(1)} %collective-permute-done.1.up_ref) | copy-start | bytes 1966084
  43.4 19.9 %collective-permute-start.2 = (f32[1,9,128,128]{3,2,1,0:T(8,128)}, f32[1,9,128,128]{3,2,1,0:T(8,128)S(1)}, u32[]{:S(2)}, u32[]{:S(2)}) collective-permute-start(f32[1,9,128,128]{3,2,1,0:T(8,128)} %get-tuple-element.9), channel_id=1, source_target_pairs={{0,1},{1,2},{2,3},{3,4},{4,5},{5,6},{6,7},{7,0},{8,9},{9,10},{10,1... | collective-permute-start | bytes 1769480 | tf_op jit(solution)/shard_map/ppermute | solution.py:16
  44.6 20.7 %collective-permute-start.3 = (f32[1,9,128,128]{3,2,1,0:T(8,128)}, f32[1,9,128,128]{3,2,1,0:T(8,128)S(1)}, u32[]{:S(2)}, u32[]{:S(2)}) collective-permute-start(f32[1,9,128,128]{3,2,1,0:T(8,128)} %get-tuple-element.10), channel_id=1, source_target_pairs={{0,7},{1,0},{2,1},{3,2},{4,3},{5,4},{6,5},{7,6},{8,15},{9,8},{10,9... | collective-permute-start | bytes 1769480 | tf_op jit(solution)/shard_map/ppermute | solution.py:16

commit v9 on v8

--- a/solution.py
+++ b/solution.py
@@ -35,7 +35,7 @@
 def triple_kernel(
     coupling_slots, interp_slots, blocks, region,
     idx_ref, a_ref, low_ref, mid_ref, up_ref, lo_ref, own_ref, hi_ref,
-    y_ref, acc_ref, p3_ref,
+    y_ref, acc_ref, pt3_ref, p3_ref,
 ):
     g = pl.program_id(0)
     steps = pl.num_programs(0)
@@ -49,46 +49,59 @@
     def _():
         acc_ref[...] = jnp.zeros_like(acc_ref)
 
-        def fill(src, offset, count):
+        def fill(src, offset, count, stage_two):
             def body(r, carry):
                 for p in range(interp_slots):
-                    hi, lo = split(src[r, p])
-                    cols = slice(p * bs, (p + 1) * bs)
-                    p3_ref[offset + r, 0:bs, cols] = hi
-                    p3_ref[offset + r, bs : 2 * bs, cols] = lo
-                    p3_ref[offset + r, 2 * bs : 3 * bs, cols] = hi
+                    rows_p = slice(p * bs, (p + 1) * bs)
+                    th, tl = split(src[r, p].T)
+                    pt3_ref[offset + r, rows_p, 0:bs] = th
+                    pt3_ref[offset + r, rows_p, bs : 2 * bs] = th
+                    pt3_ref[offset + r, rows_p, 2 * bs : 3 * bs] = tl
+                    if stage_two:
+                        hi, lo = split(src[r, p])
+                        p3_ref[r, 0:bs, rows_p] = hi
+                        p3_ref[r, bs : 2 * bs, rows_p] = lo
+                        p3_ref[r, 2 * bs : 3 * bs, rows_p] = hi
                 return carry
 
             lax.fori_loop(0, count, body, 0)
 
-        fill(low_ref, 0, RIM)
-        fill(mid_ref, RIM, rows)
-        fill(up_ref, RIM + rows, RIM)
+        fill(low_ref, 0, RIM, False)
+        fill(mid_ref, RIM, rows, True)
+        fill(up_ref, RIM + rows, RIM, False)
 
     def row_step(i, carry):
         gi = g * per_step + i
         y_ref[...] = jnp.zeros_like(y_ref)
         for a in range(coupling_slots):
             row = idx_ref[gi * coupling_slots + a]
-            prod = jnp.dot(stack_lhs(a_ref[i, a]), p3_ref[row], preferred_element_type=jnp.float32)
+            ah, al = split(a_ref[i, a])
+            a3 = jnp.concatenate([ah, al, ah], axis=1)
+            prod_t = lax.dot_general(
+                pt3_ref[row], a3, (((1,), (1,)), ((), ())), preferred_element_type=jnp.float32
+            )
             for p in range(interp_slots):
                 slot = idx_ref[slot_base + (gi * coupling_slots + a) * interp_slots + p]
-                y_ref[slot] += prod[:, p * bs : (p + 1) * bs]
-        pt = stack_lhs(jnp.concatenate([mid_ref[gi, q].T for q in range(interp_slots)], axis=0))
+                y_ref[slot] += prod_t[p * bs : (p + 1) * bs]
         owners = [idx_ref[owner_base + gi * interp_slots + q] for q in range(interp_slots)]
+        pieces = []
         for c in range(region):
-            res = jnp.dot(pt, stack_rhs(y_ref[c]), preferred_element_type=jnp.float32)
+            yh, yl = split(y_ref[c])
+            pieces.append(jnp.concatenate([yh, yh, yl], axis=1))
+        res = jnp.dot(jnp.concatenate(pieces, axis=0), p3_ref[gi], preferred_element_type=jnp.float32)
+        for c in range(region):
             for q in range(interp_slots):
-                acc_ref[owners[q], c] += res[q * bs : (q + 1) * bs]
+                acc_ref[owners[q], c] += res[c * bs : (c + 1) * bs, q * bs : (q + 1) * bs]
         return carry
 
     lax.fori_loop(0, per_step, row_step, 0)
 
     @pl.when(g == steps - 1)
     def _():
-        lo_ref[...] = acc_ref[:blocks]
-        own_ref[...] = acc_ref[blocks : 2 * blocks]
-        hi_ref[...] = acc_ref[2 * blocks :]
+        for o, out in enumerate((lo_ref, own_ref, hi_ref)):
+            for w in range(blocks):
+                for c in range(region):
+                    out[w, c] = acc_ref[o * blocks + w, c].T
 
 
 def shards(a_tiles, a_cols, p_tiles, p_cols, c_cols):
@@ -164,7 +177,8 @@
             scratch_shapes=[
                 pltpu.VMEM((region, bs, bs), jnp.float32),
                 pltpu.VMEM((3 * blocks, region, bs, bs), jnp.float32),
-                pltpu.VMEM((ext_rows, 3 * bs, interp_slots * bs), jnp.bfloat16),
+                pltpu.VMEM((ext_rows, interp_slots * bs, 3 * bs), jnp.bfloat16),
+                pltpu.VMEM((rows, 3 * bs, interp_slots * bs), jnp.bfloat16),
             ],
         ),
         compiler_params=pltpu.CompilerParams(dimension_semantics=("arbitrary",)),

time: 68.1 us -> 68.9 us (1.012)
  Pallas kernels: 23.5 us -> 24.4 us
    pallas_call x1, Pallas kernels: 23.5 us -> 24.4 us  [shards(): pl.pallas_call(kernel, out_shape=(part, part, part), grid_spec=pltpu.Pref...]
where the time goes in v9:
time: 68.9 us; the launch traced here: 68.7 us
  Pallas kernels  24.4 us (35%)
  waiting for transfers between devices  23.9 us (35%)
  starting transfers between devices  10.7 us (16%)
  local copies, waits for them, and re-layouts  6.14 us (9%)
  other arithmetic  3.41 us (5%)
    pallas_call x1, Pallas kernels, shards(): pl.pallas_call(kernel, out_shape=(part, part, part), grid_spec=pltpu.Pref...  24.4 us
    ppermute x2, waiting for transfers between devices, passed_along(): return lax.ppermute(value, axis, pairs)  15.3 us
    ppermute x1, starting transfers between devices, shards(): lax.ppermute(halo(rows - RIM), 'slab', [(i, i + 1) for i in range(slabs -...  4.54 us
    ppermute x1, waiting for transfers between devices, shards(): up = lax.ppermute(halo(0), 'slab', [(i + 1, i) for i in range(slabs - 1)])  4.52 us
    ppermute x2, starting transfers between devices, passed_along(): return lax.ppermute(value, axis, pairs)  4.25 us
    ppermute x1, waiting for transfers between devices, shards(): lax.ppermute(halo(rows - RIM), 'slab', [(i, i + 1) for i in range(slabs -...  4.01 us
    gather x3, local copies, waits for them, and re-layouts, pick(): tiles_picked = part[r_idx, idx]  2.9 us
    ppermute x1, starting transfers between devices, shards(): up = lax.ppermute(halo(0), 'slab', [(i + 1, i) for i in range(slabs - 1)])  1.92 us
  transfers between devices with their start and end apart: 4, of which 4 were waited for; matrix products, arithmetic and copies ran while one was open for 6% of the time, Pallas kernels for 0%

profile of v9, /device:TPU:1, one launch (start us, length us, event | category | flops | bytes accessed | tf_op | source)
XLA Modules:
  0.0 68.7 jit_solution(5041882377290152086)
XLA Ops:
  0.0 1.3 %fusion.19 = (f32[4,2,128,128]{3,2,1,0:T(8,128)S(1)}, f32[4,2,128,128]{3,2,1,0:T(8,128)S(1)}) fusion(f32[16,2,128,128]{3,2,1,0:T(8,128)} %mid_ref.1), kind=kLoop, calls=%fused_computation.71 | loop fusion | bytes 2097152 | tf_op jit(solution)/shard_map/slice | solution.py:123
  1.3 0.1 slice_convert_fusion.1
  1.4 0.1 copy.27
  1.5 0.1 reshape.64
  1.6 4.5 %collective-permute-start = (f32[5,2,128,128]{3,2,1,0:T(8,128)S(1)}, f32[5,2,128,128]{3,2,1,0:T(8,128)S(1)}, u32[]{:S(2)}, u32[]{:S(2)}) collective-permute-start(f32[5,2,128,128]{3,2,1,0:T(8,128)S(1)} %select_maximum_fusion.1), channel_id=1, source_target_pairs={{0,8},{8,16},{16,24},{1,9},{9,17},{17,25},{2,10},{10,18},{18,26},{... | collective-permute-start | bytes 1966088 | tf_op jit(solution)/shard_map/ppermute | solution.py:125
  6.2 0.1 copy.28
  6.3 0.1 reshape.65
  6.4 1.9 %collective-permute-start.1 = (f32[5,2,128,128]{3,2,1,0:T(8,128)S(1)}, f32[5,2,128,128]{3,2,1,0:T(8,128)S(1)}, u32[]{:S(2)}, u32[]{:S(2)}) collective-permute-start(f32[5,2,128,128]{3,2,1,0:T(8,128)S(1)} %select_maximum_fusion), channel_id=1, source_target_pairs={{8,0},{16,8},{24,16},{9,1},{17,9},{25,17},{10,2},{18,10},{26,18},{... | collective-permute-start | bytes 1966088 | tf_op jit(solution)/shard_map/ppermute | solution.py:126
  8.4 0.1 copy.29
  8.5 0.1 copy.30
  8.6 0.1 reshape.69
  8.7 0.1 copy.26
  8.7 0.1 reshape.63
  8.8 0.1 copy.31
  8.9 0.1 reshape.66
  9.1 0.6 and_bitcast_fusion.1
  9.7 4.0 %collective-permute-done.low_ref = f32[5,2,128,128]{3,2,1,0:T(8,128)S(1)} collective-permute-done((f32[5,2,128,128]{3,2,1,0:T(8,128)S(1)}, f32[5,2,128,128]{3,2,1,0:T(8,128)S(1)}, u32[]{:S(2)}, u32[]{:S(2)}) %collective-permute-start) | collective-permute-done | bytes 655392 | tf_op jit(solution)/shard_map/ppermute | solution.py:125
  13.7 0.1 convert_element_type.25
  13.8 4.5 %collective-permute-done.1.up_ref = f32[5,2,128,128]{3,2,1,0:T(8,128)S(1)} collective-permute-done((f32[5,2,128,128]{3,2,1,0:T(8,128)S(1)}, f32[5,2,128,128]{3,2,1,0:T(8,128)S(1)}, u32[]{:S(2)}, u32[]{:S(2)}) %collective-permute-start.1) | collective-permute-done | bytes 655392 | tf_op jit(solution)/shard_map/ppermute | solution.py:126
  18.4 0.1 convert_element_type.28
  18.4 0.6 gather_fusion
  19.1 0.1 gather.15
  19.3 0.6 pad_add_fusion.1.idx_ref
  19.9 24.4 %shard_map.55 = (f32[1,9,128,128]{3,2,1,0:T(8,128)}, f32[1,9,128,128]{3,2,1,0:T(8,128)}, f32[1,9,128,128]{3,2,1,0:T(8,128)}) custom-call(s32[416]{0:T(512)} %pad_add_fusion.1.idx_ref, f32[16,8,128,128]{3,2,1,0:T(8,128)} %a_ref.1, f32[5,2,128,128]{3,2,1,0:T(8,128)} %copy-done, f32[16,2,128,128]{3,2,1,0:T(8,128)} %mid_ref.1, f32[5,2,128,128]{3,2,1,0:T(8,128)} %copy-done.1), custom_call_target="tpu_custom_call" | custom-call | tf_op jit(solution)/shard_map/pallas_call | solution.py:164
  44.2 1.2 %collective-permute-start.2 = (f32[1,9,128,128]{3,2,1,0:T(8,128)}, f32[1,9,128,128]{3,2,1,0:T(8,128)S(1)}, u32[]{:S(2)}, u32[]{:S(2)}) collective-permute-start(f32[1,9,128,128]{3,2,1,0:T(8,128)} %get-tuple-element.9), channel_id=1, source_target_pairs={{0,1},{1,2},{2,3},{3,4},{4,5},{5,6},{6,7},{7,0},{8,9},{9,10},{10,1... | collective-permute-start | bytes 1769480 | tf_op jit(solution)/shard_map/ppermute | solution.py:16
  45.4 3.0 %collective-permute-start.3 = (f32[1,9,128,128]{3,2,1,0:T(8,128)}, f32[1,9,128,128]{3,2,1,0:T(8,128)S(1)}, u32[]{:S(2)}, u32[]{:S(2)}) collective-permute-start(f32[1,9,128,128]{3,2,1,0:T(8,128)} %get-tuple-element.10), channel_id=1, source_target_pairs={{0,7},{1,0},{2,1},{3,2},{4,3},{5,4},{6,5},{7,6},{8,15},{9,8},{10,9... | collective-permute-start | bytes 1769480 | tf_op jit(solution)/shard_map/ppermute | solution.py:16
  48.5 1.7 %gather_fusion.1 = f32[15,128,128]{2,1,0:T(8,128)S(1)} fusion(f32[1,9,128,128]{3,2,1,0:T(8,128)} %get-tuple-element.8, s32[15]{0:T(128)S(1)} %or_bitcast_fusion.2), kind=kCustom, calls=%fused_computation.1 | custom fusion | bytes 1966200 | tf_op jit(solution)/shard_map/gather | solution.py:201
  50.2 13.9 %collective-permute-done.2 = f32[1,9,128,128]{3,2,1,0:T(8,128)S(1)} collective-permute-done((f32[1,9,128,128]{3,2,1,0:T(8,128)}, f32[1,9,128,128]{3,2,1,0:T(8,128)S(1)}, u32[]{:S(2)}, u32[]{:S(2)}) %collective-permute-start.2) | collective-permute-done | bytes 589856 | tf_op jit(solution)/shard_map/ppermute | solution.py:16
  64.1 0.6 gather_fusion.2
  64.7 1.5 %collective-permute-done.3 = f32[1,9,128,128]{3,2,1,0:T(8,128)S(1)} collective-permute-done((f32[1,9,128,128]{3,2,1,0:T(8,128)}, f32[1,9,128,128]{3,2,1,0:T(8,128)S(1)}, u32[]{:S(2)}, u32[]{:S(2)}) %collective-permute-start.3) | collective-permute-done | bytes 589856 | tf_op jit(solution)/shard_map/ppermute | solution.py:16
  66.2 0.6 gather_fusion.3
  66.8 1.9 %fusion = f32[1,15,128,128]{3,2,1,0:T(8,128)} fusion(f32[15,128,128]{2,1,0:T(8,128)S(1)} %gather_fusion.3, f32[15,128,128]{2,1,0:T(8,128)S(1)} %gather_fusion.2, f32[15,128,128]{2,1,0:T(8,128)S(1)} %gather_fusion.1, pred[15]{0:T(512)(128)(4,1)} %get-tuple-element.24, pred[15]{0:T(512)(128)(4,1)S(1)} %get-tuple-element.23, pred[15]{0:T(512)(128)(4,1)S(1)} %get-tuple-element.11), kind=kLoop, calls=%fused_computation.5 | loop fusion | flops 1228800 | bytes 3932205 | tf_op jit(solution)/shard_map/add | solution.py:204
  (28 shorter events, 0.3 us)
Async XLA Ops:
  0.0 1.3 %copy-start.2 = (s32[16,2]{0,1:T(2,128)S(1)}, s32[16,2]{0,1:T(2,128)}, u32[]{:S(2)}) copy-start(s32[16,2]{0,1:T(2,128)} %param.8) | copy-start | bytes 388
  0.0 8.5 %copy-start.3 = (s32[16,8]{0,1:T(8,128)S(1)}, s32[16,8]{0,1:T(8,128)}, u32[]{:S(2)}) copy-start(s32[16,8]{0,1:T(8,128)} %param.6) | copy-start | bytes 1540
  0.0 9.0 %copy-start.4 = (s32[1,15]{1,0:T(1,128)S(1)}, s32[1,15]{1,0:T(1,128)}, u32[]{:S(2)}) copy-start(s32[1,15]{1,0:T(1,128)} %param.9) | copy-start | bytes 184
  1.6 12.1 %collective-permute-start = (f32[5,2,128,128]{3,2,1,0:T(8,128)S(1)}, f32[5,2,128,128]{3,2,1,0:T(8,128)S(1)}, u32[]{:S(2)}, u32[]{:S(2)}) collective-permute-start(f32[5,2,128,128]{3,2,1,0:T(8,128)S(1)} %select_maximum_fusion.1), channel_id=1, source_target_pairs={{0,8},{8,16},{16,24},{1,9},{9,17},{17,25},{2,10},{10,18},{18,26},{... | collective-permute-start | bytes 1966088 | tf_op jit(solution)/shard_map/ppermute | solution.py:125
  6.4 11.9 %collective-permute-start.1 = (f32[5,2,128,128]{3,2,1,0:T(8,128)S(1)}, f32[5,2,128,128]{3,2,1,0:T(8,128)S(1)}, u32[]{:S(2)}, u32[]{:S(2)}) collective-permute-start(f32[5,2,128,128]{3,2,1,0:T(8,128)S(1)} %select_maximum_fusion), channel_id=1, source_target_pairs={{8,0},{16,8},{24,16},{9,1},{17,9},{25,17},{10,2},{18,10},{26,18},{... | collective-permute-start | bytes 1966088 | tf_op jit(solution)/shard_map/ppermute | solution.py:126
  13.7 6.2 %copy-start = (f32[5,2,128,128]{3,2,1,0:T(8,128)}, f32[5,2,128,128]{3,2,1,0:T(8,128)S(1)}, u32[]{:S(2)}) copy-start(f32[5,2,128,128]{3,2,1,0:T(8,128)S(1)} %collective-permute-done.low_ref) | copy-start | bytes 1966084
  18.3 1.5 %copy-start.1 = (f32[5,2,128,128]{3,2,1,0:T(8,128)}, f32[5,2,128,128]{3,2,1,0:T(8,128)S(1)}, u32[]{:S(2)}) copy-start(f32[5,2,128,128]{3,2,1,0:T(8,128)S(1)} %collective-permute-done.1.up_ref) | copy-start | bytes 1966084
  44.2 19.9 %collective-permute-start.2 = (f32[1,9,128,128]{3,2,1,0:T(8,128)}, f32[1,9,128,128]{3,2,1,0:T(8,128)S(1)}, u32[]{:S(2)}, u32[]{:S(2)}) collective-permute-start(f32[1,9,128,128]{3,2,1,0:T(8,128)} %get-tuple-element.9), channel_id=1, source_target_pairs={{0,1},{1,2},{2,3},{3,4},{4,5},{5,6},{6,7},{7,0},{8,9},{9,10},{10,1... | collective-permute-start | bytes 1769480 | tf_op jit(solution)/shard_map/ppermute | solution.py:16
  45.4 20.7 %collective-permute-start.3 = (f32[1,9,128,128]{3,2,1,0:T(8,128)}, f32[1,9,128,128]{3,2,1,0:T(8,128)S(1)}, u32[]{:S(2)}, u32[]{:S(2)}) collective-permute-start(f32[1,9,128,128]{3,2,1,0:T(8,128)} %get-tuple-element.10), channel_id=1, source_target_pairs={{0,7},{1,0},{2,1},{3,2},{4,3},{5,4},{6,5},{7,6},{8,15},{9,8},{10,9... | collective-permute-start | bytes 1769480 | tf_op jit(solution)/shard_map/ppermute | solution.py:16

commit v10 on v8

--- a/solution.py
+++ b/solution.py
@@ -34,7 +34,7 @@
 
 def triple_kernel(
     coupling_slots, interp_slots, blocks, region,
-    idx_ref, a_ref, low_ref, mid_ref, up_ref, lo_ref, own_ref, hi_ref,
+    idx_ref, a_ref, al_ref, low_ref, mid_ref, up_ref, lo_ref, own_ref, hi_ref,
     y_ref, acc_ref, p3_ref,
 ):
     g = pl.program_id(0)
@@ -70,7 +70,9 @@
         y_ref[...] = jnp.zeros_like(y_ref)
         for a in range(coupling_slots):
             row = idx_ref[gi * coupling_slots + a]
-            prod = jnp.dot(stack_lhs(a_ref[i, a]), p3_ref[row], preferred_element_type=jnp.float32)
+            ah = a_ref[i, a]
+            lhs = jnp.concatenate([ah, ah, al_ref[i, a]], axis=1)
+            prod = jnp.dot(lhs, p3_ref[row], preferred_element_type=jnp.float32)
             for p in range(interp_slots):
                 slot = idx_ref[slot_base + (gi * coupling_slots + a) * interp_slots + p]
                 y_ref[slot] += prod[:, p * bs : (p + 1) * bs]
@@ -142,6 +144,9 @@
     owner = jnp.clip(relative * blocks + targets % blocks, 0, 3 * blocks - 1)
 
     per_step = next(d for d in (4, 2, 1) if rows % d == 0)
+    a_round = lax.reduce_precision(a_tiles, exponent_bits=8, mantissa_bits=7)
+    a_hi = a_round.astype(jnp.bfloat16)
+    a_lo = (a_tiles - a_round).astype(jnp.bfloat16)
     kernel = functools.partial(triple_kernel, coupling_slots, interp_slots, blocks, region)
     part = jax.ShapeDtypeStruct((blocks, region, bs, bs), jnp.float32)
     part_spec = pl.BlockSpec((blocks, region, bs, bs), lambda g, *_: (0, 0, 0, 0))
@@ -156,6 +161,7 @@
             grid=(rows // per_step,),
             in_specs=[
                 pl.BlockSpec((per_step, coupling_slots, bs, bs), lambda g, *_: (g, 0, 0, 0)),
+                pl.BlockSpec((per_step, coupling_slots, bs, bs), lambda g, *_: (g, 0, 0, 0)),
                 pl.BlockSpec(low.shape, lambda g, *_: (0, 0, 0, 0)),
                 pl.BlockSpec(p_tiles.shape, lambda g, *_: (0, 0, 0, 0)),
                 pl.BlockSpec(up.shape, lambda g, *_: (0, 0, 0, 0)),
@@ -168,7 +174,7 @@
             ],
         ),
         compiler_params=pltpu.CompilerParams(dimension_semantics=("arbitrary",)),
-    )(table, a_tiles, low, p_tiles, up)
+    )(table, a_hi, a_lo, low, p_tiles, up)
 
     from_lower = passed_along(to_upper, "tile", 1)
     from_upper = passed_along(to_lower, "tile", -1)

time: 68.1 us -> 75.2 us (1.10)
  other arithmetic: 3.41 us -> 13.1 us
  waiting for transfers between devices: 23.9 us -> 21.4 us
    convert_element_type x0 -> x1, other arithmetic: none -> 9.01 us  [shards(): a_lo = (a_tiles - a_round).astype(jnp.bfloat16)]
    ppermute x2, waiting for transfers between devices: 15.4 us -> 21.4 us  [passed_along(): return lax.ppermute(value, axis, pairs)]
    ppermute x1, waiting for transfers between devices: 4.52 us -> 0.01 us  [shards(): up = lax.ppermute(halo(0), 'slab', [(i + 1, i) for i in range(slabs - 1)])]
    ppermute x1, waiting for transfers between devices: 4.01 us -> 0.01 us  [shards(): lax.ppermute(halo(rows - RIM), 'slab', [(i, i + 1) for i in range(slabs -...]
    convert_element_type x1, other arithmetic: 0.07 us -> 0.83 us  [halo(): p_cols[first:first + RIM].astype(jnp.float32)]
  transfers between devices with their start and end apart: 4 -> 4, of which waited for: 4 -> 2; matrix products, arithmetic and copies ran while one was open for 6% -> 17% of each run, Pallas kernels for 0% -> 0%
where the time goes in v10:
time: 75.2 us; the launch traced here: 74.9 us
  Pallas kernels  23.4 us (31%)
  waiting for transfers between devices  21.4 us (28%)
  other arithmetic  13.1 us (17%)
  starting transfers between devices  10.7 us (14%)
  local copies, waits for them, and re-layouts  6.14 us (8%)
    pallas_call x1, Pallas kernels, shards(): pl.pallas_call(kernel, out_shape=(part, part, part), grid_spec=pltpu.Pref...  23.4 us
    ppermute x2, waiting for transfers between devices, passed_along(): return lax.ppermute(value, axis, pairs)  21.4 us
    convert_element_type x1, other arithmetic, shards(): a_lo = (a_tiles - a_round).astype(jnp.bfloat16)  9.01 us
    ppermute x1, starting transfers between devices, shards(): lax.ppermute(halo(rows - RIM), 'slab', [(i, i + 1) for i in range(slabs -...  4.54 us
    ppermute x2, starting transfers between devices, passed_along(): return lax.ppermute(value, axis, pairs)  4.25 us
    gather x3, local copies, waits for them, and re-layouts, pick(): tiles_picked = part[r_idx, idx]  2.9 us
    ppermute x1, starting transfers between devices, shards(): up = lax.ppermute(halo(0), 'slab', [(i + 1, i) for i in range(slabs - 1)])  1.92 us
    add x1, other arithmetic, shards(): pick(own_part, c_dt) + pick(from_lower, c_dt + 1)  1.88 us
  transfers between devices with their start and end apart: 4, of which 2 were waited for; matrix products, arithmetic and copies ran while one was open for 17% of the time, Pallas kernels for 0%

profile of v10, /device:TPU:1, one launch (start us, length us, event | category | flops | bytes accessed | tf_op | source)
XLA Modules:
  0.0 74.9 jit_solution(10824906078445632349)
XLA Ops:
  0.0 1.3 %fusion.20 = (f32[4,2,128,128]{3,2,1,0:T(8,128)S(1)}, f32[4,2,128,128]{3,2,1,0:T(8,128)S(1)}) fusion(f32[16,2,128,128]{3,2,1,0:T(8,128)} %mid_ref.1), kind=kLoop, calls=%fused_computation.74 | loop fusion | bytes 2097152 | tf_op jit(solution)/shard_map/slice | solution.py:112
  1.3 0.8 %slice_convert_fusion.1 = (f32[4,2]{0,1:T(2,128)S(1)}, f32[4,2]{0,1:T(2,128)S(1)}) fusion(s32[16,2]{0,1:T(2,128)} %param.8), kind=kLoop, calls=%fused_computation.57 | loop fusion | flops 16 | bytes 128 | tf_op jit(solution)/shard_map/convert_element_type | solution.py:110
  2.2 0.1 copy.27
  2.2 0.1 reshape.64
  2.4 4.5 %collective-permute-start = (f32[5,2,128,128]{3,2,1,0:T(8,128)S(1)}, f32[5,2,128,128]{3,2,1,0:T(8,128)S(1)}, u32[]{:S(2)}, u32[]{:S(2)}) collective-permute-start(f32[5,2,128,128]{3,2,1,0:T(8,128)S(1)} %select_maximum_fusion.1), channel_id=1, source_target_pairs={{0,8},{8,16},{16,24},{1,9},{9,17},{17,25},{2,10},{10,18},{18,26},{... | collective-permute-start | bytes 1966088 | tf_op jit(solution)/shard_map/ppermute | solution.py:114
  6.9 0.1 copy.28
  7.0 0.1 reshape.65
  7.2 1.9 %collective-permute-start.1 = (f32[5,2,128,128]{3,2,1,0:T(8,128)S(1)}, f32[5,2,128,128]{3,2,1,0:T(8,128)S(1)}, u32[]{:S(2)}, u32[]{:S(2)}) collective-permute-start(f32[5,2,128,128]{3,2,1,0:T(8,128)S(1)} %select_maximum_fusion), channel_id=1, source_target_pairs={{8,0},{16,8},{24,16},{9,1},{17,9},{25,17},{10,2},{18,10},{26,18},{... | collective-permute-start | bytes 1966088 | tf_op jit(solution)/shard_map/ppermute | solution.py:115
  9.2 0.6 and_bitcast_fusion.1
  9.8 0.1 copy.30
  9.9 0.1 reshape.69
  10.0 0.1 copy.29
  10.1 0.1 copy.26
  10.2 0.1 reshape.63
  10.3 0.1 copy.31
  10.3 0.1 reshape.66
  10.4 9.0 %fusion = (bf16[16,8,128,128]{3,2,1,0:T(8,128)(2,1)}, bf16[16,8,128,128]{3,2,1,0:T(8,128)(2,1)}) fusion(f32[16,8,128,128]{3,2,1,0:T(8,128)} %param.5), kind=kLoop, calls=%fused_computation.6 | loop fusion | flops 8388608 | bytes 16777216 | tf_op jit(solution)/shard_map/convert_element_type | solution.py:149
  19.5 0.1 convert_element_type.31
  19.6 0.0 collective-permute-done.1.up_ref
  19.6 0.1 convert_element_type.34
  19.7 0.6 gather_fusion
  20.3 0.1 gather.15
  20.5 0.5 pad_add_fusion.1.idx_ref
  21.0 23.4 %shard_map.55 = (f32[1,9,128,128]{3,2,1,0:T(8,128)}, f32[1,9,128,128]{3,2,1,0:T(8,128)}, f32[1,9,128,128]{3,2,1,0:T(8,128)}) custom-call(s32[416]{0:T(512)} %pad_add_fusion.1.idx_ref, bf16[16,8,128,128]{3,2,1,0:T(8,128)(2,1)} %get-tuple-element.18.a_ref, bf16[16,8,128,128]{3,2,1,0:T(8,128)(2,1)} %get-tuple-element.17.al_ref, f32[5,2,128,128]{3,2,1,0:T(8,128)} %copy-done, ...), custom_call_target="tpu_custom_call" | custom-call | tf_op jit(solution)/shard_map/pallas_call | solution.py:156
  44.4 1.2 %collective-permute-start.2 = (f32[1,9,128,128]{3,2,1,0:T(8,128)}, f32[1,9,128,128]{3,2,1,0:T(8,128)S(1)}, u32[]{:S(2)}, u32[]{:S(2)}) collective-permute-start(f32[1,9,128,128]{3,2,1,0:T(8,128)} %get-tuple-element.9), channel_id=1, source_target_pairs={{0,1},{1,2},{2,3},{3,4},{4,5},{5,6},{6,7},{7,0},{8,9},{9,10},{10,1... | collective-permute-start | bytes 1769480 | tf_op jit(solution)/shard_map/ppermute | solution.py:16
  45.6 3.0 %collective-permute-start.3 = (f32[1,9,128,128]{3,2,1,0:T(8,128)}, f32[1,9,128,128]{3,2,1,0:T(8,128)S(1)}, u32[]{:S(2)}, u32[]{:S(2)}) collective-permute-start(f32[1,9,128,128]{3,2,1,0:T(8,128)} %get-tuple-element.10), channel_id=1, source_target_pairs={{0,7},{1,0},{2,1},{3,2},{4,3},{5,4},{6,5},{7,6},{8,15},{9,8},{10,9... | collective-permute-start | bytes 1769480 | tf_op jit(solution)/shard_map/ppermute | solution.py:16
  48.7 1.7 %gather_fusion.1 = f32[15,128,128]{2,1,0:T(8,128)S(1)} fusion(f32[1,9,128,128]{3,2,1,0:T(8,128)} %get-tuple-element.8, s32[15]{0:T(128)S(1)} %or_bitcast_fusion.2), kind=kCustom, calls=%fused_computation.1 | custom fusion | bytes 1966200 | tf_op jit(solution)/shard_map/gather | solution.py:193
  50.4 19.9 %collective-permute-done.2 = f32[1,9,128,128]{3,2,1,0:T(8,128)S(1)} collective-permute-done((f32[1,9,128,128]{3,2,1,0:T(8,128)}, f32[1,9,128,128]{3,2,1,0:T(8,128)S(1)}, u32[]{:S(2)}, u32[]{:S(2)}) %collective-permute-start.2) | collective-permute-done | bytes 589856 | tf_op jit(solution)/shard_map/ppermute | solution.py:16
  70.3 0.6 gather_fusion.2
  70.9 1.5 %collective-permute-done.3 = f32[1,9,128,128]{3,2,1,0:T(8,128)S(1)} collective-permute-done((f32[1,9,128,128]{3,2,1,0:T(8,128)}, f32[1,9,128,128]{3,2,1,0:T(8,128)S(1)}, u32[]{:S(2)}, u32[]{:S(2)}) %collective-permute-start.3) | collective-permute-done | bytes 589856 | tf_op jit(solution)/shard_map/ppermute | solution.py:16
  72.4 0.6 gather_fusion.3
  73.0 1.9 %fusion.1 = f32[1,15,128,128]{3,2,1,0:T(8,128)} fusion(f32[15,128,128]{2,1,0:T(8,128)S(1)} %gather_fusion.3, f32[15,128,128]{2,1,0:T(8,128)S(1)} %gather_fusion.2, f32[15,128,128]{2,1,0:T(8,128)S(1)} %gather_fusion.1, pred[15]{0:T(512)(128)(4,1)} %get-tuple-element.26, pred[15]{0:T(512)(128)(4,1)S(1)} %get-tuple-element.25, pred[15]{0:T(512)(128)(4,1)S(1)} %get-tuple-element.11), kind=kLoop, calls=%fused_computation.8 | loop fusion | flops 1228800 | bytes 3932205 | tf_op jit(solution)/shard_map/add | solution.py:196
  (29 shorter events, 0.3 us)
Async XLA Ops:
  0.0 9.1 %copy-start.2 = (s32[16,2]{0,1:T(2,128)S(1)}, s32[16,2]{0,1:T(2,128)}, u32[]{:S(2)}) copy-start(s32[16,2]{0,1:T(2,128)} %param.8) | copy-start | bytes 388
  0.0 9.1 %copy-start.4 = (s32[1,15]{1,0:T(1,128)S(1)}, s32[1,15]{1,0:T(1,128)}, u32[]{:S(2)}) copy-start(s32[1,15]{1,0:T(1,128)} %param.9) | copy-start | bytes 184
  0.0 9.8 %copy-start.3 = (s32[16,8]{0,1:T(8,128)S(1)}, s32[16,8]{0,1:T(8,128)}, u32[]{:S(2)}) copy-start(s32[16,8]{0,1:T(8,128)} %param.6) | copy-start | bytes 1540
  2.4 17.1 %collective-permute-start = (f32[5,2,128,128]{3,2,1,0:T(8,128)S(1)}, f32[5,2,128,128]{3,2,1,0:T(8,128)S(1)}, u32[]{:S(2)}, u32[]{:S(2)}) collective-permute-start(f32[5,2,128,128]{3,2,1,0:T(8,128)S(1)} %select_maximum_fusion.1), channel_id=1, source_target_pairs={{0,8},{8,16},{16,24},{1,9},{9,17},{17,25},{2,10},{10,18},{18,26},{... | collective-permute-start | bytes 1966088 | tf_op jit(solution)/shard_map/ppermute | solution.py:114
  7.2 12.4 %collective-permute-start.1 = (f32[5,2,128,128]{3,2,1,0:T(8,128)S(1)}, f32[5,2,128,128]{3,2,1,0:T(8,128)S(1)}, u32[]{:S(2)}, u32[]{:S(2)}) collective-permute-start(f32[5,2,128,128]{3,2,1,0:T(8,128)S(1)} %select_maximum_fusion), channel_id=1, source_target_pairs={{8,0},{16,8},{24,16},{9,1},{17,9},{25,17},{10,2},{18,10},{26,18},{... | collective-permute-start | bytes 1966088 | tf_op jit(solution)/shard_map/ppermute | solution.py:115
  19.4 1.6 %copy-start = (f32[5,2,128,128]{3,2,1,0:T(8,128)}, f32[5,2,128,128]{3,2,1,0:T(8,128)S(1)}, u32[]{:S(2)}) copy-start(f32[5,2,128,128]{3,2,1,0:T(8,128)S(1)} %collective-permute-done.low_ref) | copy-start | bytes 1966084
  19.6 1.5 %copy-start.1 = (f32[5,2,128,128]{3,2,1,0:T(8,128)}, f32[5,2,128,128]{3,2,1,0:T(8,128)S(1)}, u32[]{:S(2)}) copy-start(f32[5,2,128,128]{3,2,1,0:T(8,128)S(1)} %collective-permute-done.1.up_ref) | copy-start | bytes 1966084
  44.4 25.9 %collective-permute-start.2 = (f32[1,9,128,128]{3,2,1,0:T(8,128)}, f32[1,9,128,128]{3,2,1,0:T(8,128)S(1)}, u32[]{:S(2)}, u32[]{:S(2)}) collective-permute-start(f32[1,9,128,128]{3,2,1,0:T(8,128)} %get-tuple-element.9), channel_id=1, source_target_pairs={{0,1},{1,2},{2,3},{3,4},{4,5},{5,6},{6,7},{7,0},{8,9},{9,10},{10,1... | collective-permute-start | bytes 1769480 | tf_op jit(solution)/shard_map/ppermute | solution.py:16
  45.6 26.8 %collective-permute-start.3 = (f32[1,9,128,128]{3,2,1,0:T(8,128)}, f32[1,9,128,128]{3,2,1,0:T(8,128)S(1)}, u32[]{:S(2)}, u32[]{:S(2)}) collective-permute-start(f32[1,9,128,128]{3,2,1,0:T(8,128)} %get-tuple-element.10), channel_id=1, source_target_pairs={{0,7},{1,0},{2,1},{3,2},{4,3},{5,4},{6,5},{7,6},{8,15},{9,8},{10,9... | collective-permute-start | bytes 1769480 | tf_op jit(solution)/shard_map/ppermute | solution.py:16

commit v11 on v8

--- a/solution.py
+++ b/solution.py
@@ -187,7 +187,8 @@
         tiles_picked = part[r_idx, idx]
         return jnp.where(valid[:, :, None, None], tiles_picked, 0.0)
 
-    return pick(own_part, c_dt) + pick(from_lower, c_dt + 1) + pick(from_upper, c_dt - 1)
+    early = lax.optimization_barrier(pick(own_part, c_dt) + pick(from_lower, c_dt + 1))
+    return early + pick(from_upper, c_dt - 1)
 
 
 def solution(mesh):

time: 68.1 us -> 67.4 us (0.990)
  waiting for transfers between devices: 23.9 us -> 23 us
    add x0 -> x1, other arithmetic: none -> 1.11 us  [shards(): return early + pick(from_upper, c_dt - 1)]
    add x1, other arithmetic: 1.89 us -> 0.85 us  [shards(): pick(own_part, c_dt) + pick(from_lower, c_dt + 1)]
    ppermute x2, waiting for transfers between devices: 15.4 us -> 14.5 us  [passed_along(): return lax.ppermute(value, axis, pairs)]
  transfers between devices with their start and end apart: 4 -> 4, of which waited for: 4 -> 4; matrix products, arithmetic and copies ran while one was open for 6% -> 7% of each run, Pallas kernels for 0% -> 0%
where the time goes in v11:
time: 67.4 us; the launch traced here: 67.1 us
  Pallas kernels  23.5 us (35%)
  waiting for transfers between devices  23 us (34%)
  starting transfers between devices  10.8 us (16%)
  local copies, waits for them, and re-layouts  6.14 us (9%)
  other arithmetic  3.49 us (5%)
    pallas_call x1, Pallas kernels, shards(): pl.pallas_call(kernel, out_shape=(part, part, part), grid_spec=pltpu.Pref...  23.5 us
    ppermute x2, waiting for transfers between devices, passed_along(): return lax.ppermute(value, axis, pairs)  14.5 us
    ppermute x1, starting transfers between devices, shards(): lax.ppermute(halo(rows - RIM), 'slab', [(i, i + 1) for i in range(slabs -...  4.54 us
    ppermute x1, waiting for transfers between devices, shards(): up = lax.ppermute(halo(0), 'slab', [(i + 1, i) for i in range(slabs - 1)])  4.52 us
    ppermute x2, starting transfers between devices, passed_along(): return lax.ppermute(value, axis, pairs)  4.31 us
    ppermute x1, waiting for transfers between devices, shards(): lax.ppermute(halo(rows - RIM), 'slab', [(i, i + 1) for i in range(slabs -...  4.01 us
    gather x3, local copies, waits for them, and re-layouts, pick(): tiles_picked = part[r_idx, idx]  2.9 us
    ppermute x1, starting transfers between devices, shards(): up = lax.ppermute(halo(0), 'slab', [(i + 1, i) for i in range(slabs - 1)])  1.92 us
  transfers between devices with their start and end apart: 4, of which 4 were waited for; matrix products, arithmetic and copies ran while one was open for 7% of the time, Pallas kernels for 0%

profile of v11, /device:TPU:1, one launch (start us, length us, event | category | flops | bytes accessed | tf_op | source)
XLA Modules:
  0.0 67.1 jit_solution(12984230322095960211)
XLA Ops:
  0.0 1.3 %fusion.19 = (f32[4,2,128,128]{3,2,1,0:T(8,128)S(1)}, f32[4,2,128,128]{3,2,1,0:T(8,128)S(1)}) fusion(f32[16,2,128,128]{3,2,1,0:T(8,128)} %mid_ref.1), kind=kLoop, calls=%fused_computation.71 | loop fusion | bytes 2097152 | tf_op jit(solution)/shard_map/slice | solution.py:110
  1.3 0.1 slice_convert_fusion.1
  1.4 0.1 copy.27
  1.5 0.1 reshape.60
  1.6 4.5 %collective-permute-start = (f32[5,2,128,128]{3,2,1,0:T(8,128)S(1)}, f32[5,2,128,128]{3,2,1,0:T(8,128)S(1)}, u32[]{:S(2)}, u32[]{:S(2)}) collective-permute-start(f32[5,2,128,128]{3,2,1,0:T(8,128)S(1)} %select_maximum_fusion.1), channel_id=1, source_target_pairs={{0,8},{8,16},{16,24},{1,9},{9,17},{17,25},{2,10},{10,18},{18,26},{... | collective-permute-start | bytes 1966088 | tf_op jit(solution)/shard_map/ppermute | solution.py:112
  6.2 0.1 copy.28
  6.3 0.1 reshape.61
  6.4 1.9 %collective-permute-start.1 = (f32[5,2,128,128]{3,2,1,0:T(8,128)S(1)}, f32[5,2,128,128]{3,2,1,0:T(8,128)S(1)}, u32[]{:S(2)}, u32[]{:S(2)}) collective-permute-start(f32[5,2,128,128]{3,2,1,0:T(8,128)S(1)} %select_maximum_fusion), channel_id=1, source_target_pairs={{8,0},{16,8},{24,16},{9,1},{17,9},{25,17},{10,2},{18,10},{26,18},{... | collective-permute-start | bytes 1966088 | tf_op jit(solution)/shard_map/ppermute | solution.py:113
  8.4 0.1 copy.29
  8.5 0.1 copy.30
  8.6 0.1 reshape.65
  8.7 0.1 reshape.59
  8.8 0.1 copy.31
  8.9 0.1 reshape.62
  9.1 0.6 and_bitcast_fusion.2
  9.7 4.0 %collective-permute-done.low_ref = f32[5,2,128,128]{3,2,1,0:T(8,128)S(1)} collective-permute-done((f32[5,2,128,128]{3,2,1,0:T(8,128)S(1)}, f32[5,2,128,128]{3,2,1,0:T(8,128)S(1)}, u32[]{:S(2)}, u32[]{:S(2)}) %collective-permute-start) | collective-permute-done | bytes 655392 | tf_op jit(solution)/shard_map/ppermute | solution.py:112
  13.7 0.1 convert_element_type.25
  13.8 4.5 %collective-permute-done.1.up_ref = f32[5,2,128,128]{3,2,1,0:T(8,128)S(1)} collective-permute-done((f32[5,2,128,128]{3,2,1,0:T(8,128)S(1)}, f32[5,2,128,128]{3,2,1,0:T(8,128)S(1)}, u32[]{:S(2)}, u32[]{:S(2)}) %collective-permute-start.1) | collective-permute-done | bytes 655392 | tf_op jit(solution)/shard_map/ppermute | solution.py:113
  18.4 0.1 convert_element_type.28
  18.4 0.6 gather_fusion
  19.1 0.1 gather.15
  19.3 0.6 pad_add_fusion.1.idx_ref
  19.9 23.5 %shard_map.55 = (f32[1,9,128,128]{3,2,1,0:T(8,128)}, f32[1,9,128,128]{3,2,1,0:T(8,128)}, f32[1,9,128,128]{3,2,1,0:T(8,128)}) custom-call(s32[416]{0:T(512)} %pad_add_fusion.1.idx_ref, f32[16,8,128,128]{3,2,1,0:T(8,128)} %a_ref.1, f32[5,2,128,128]{3,2,1,0:T(8,128)} %copy-done, f32[16,2,128,128]{3,2,1,0:T(8,128)} %mid_ref.1, f32[5,2,128,128]{3,2,1,0:T(8,128)} %copy-done.1), custom_call_target="tpu_custom_call" | custom-call | tf_op jit(solution)/shard_map/pallas_call | solution.py:151
  43.4 1.2 %collective-permute-start.2 = (f32[1,9,128,128]{3,2,1,0:T(8,128)}, f32[1,9,128,128]{3,2,1,0:T(8,128)S(1)}, u32[]{:S(2)}, u32[]{:S(2)}) collective-permute-start(f32[1,9,128,128]{3,2,1,0:T(8,128)} %get-tuple-element.9), channel_id=1, source_target_pairs={{0,1},{1,2},{2,3},{3,4},{4,5},{5,6},{6,7},{7,0},{8,9},{9,10},{10,1... | collective-permute-start | bytes 1769480 | tf_op jit(solution)/shard_map/ppermute | solution.py:16
  44.6 3.1 %collective-permute-start.3 = (f32[1,9,128,128]{3,2,1,0:T(8,128)}, f32[1,9,128,128]{3,2,1,0:T(8,128)S(1)}, u32[]{:S(2)}, u32[]{:S(2)}) collective-permute-start(f32[1,9,128,128]{3,2,1,0:T(8,128)} %get-tuple-element.10), channel_id=1, source_target_pairs={{0,7},{1,0},{2,1},{3,2},{4,3},{5,4},{6,5},{7,6},{8,15},{9,8},{10,9... | collective-permute-start | bytes 1769480 | tf_op jit(solution)/shard_map/ppermute | solution.py:16
  47.7 1.7 %gather_fusion.1 = f32[15,128,128]{2,1,0:T(8,128)S(1)} fusion(f32[1,9,128,128]{3,2,1,0:T(8,128)} %get-tuple-element.8, s32[15]{0:T(128)S(1)} %or_bitcast_fusion.2), kind=kCustom, calls=%fused_computation.1 | custom fusion | bytes 1966200 | tf_op jit(solution)/shard_map/gather | solution.py:187
  49.4 13.8 %collective-permute-done.2 = f32[1,9,128,128]{3,2,1,0:T(8,128)S(1)} collective-permute-done((f32[1,9,128,128]{3,2,1,0:T(8,128)}, f32[1,9,128,128]{3,2,1,0:T(8,128)S(1)}, u32[]{:S(2)}, u32[]{:S(2)}) %collective-permute-start.2) | collective-permute-done | bytes 589856 | tf_op jit(solution)/shard_map/ppermute | solution.py:16
  63.3 0.6 gather_fusion.2
  63.9 0.9 %fusion.1 = f32[1,15,128,128]{3,2,1,0:T(8,128)S(1)} fusion(f32[15,128,128]{2,1,0:T(8,128)S(1)} %gather_fusion.2, f32[15,128,128]{2,1,0:T(8,128)S(1)} %gather_fusion.1, pred[15]{0:T(512)(128)(4,1)} %get-tuple-element.24, pred[15]{0:T(512)(128)(4,1)S(1)} %get-tuple-element.23), kind=kLoop, calls=%fused_computation.7 | loop fusion | flops 737280 | bytes 2949150 | tf_op jit(solution)/shard_map/add | solution.py:190
  64.7 0.7 collective-permute-done.3
  65.4 0.6 gather_fusion.3
  66.0 1.1 %fusion = f32[1,15,128,128]{3,2,1,0:T(8,128)} fusion(f32[1,15,128,128]{3,2,1,0:T(8,128)S(1)} %fusion.1, f32[15,128,128]{2,1,0:T(8,128)S(1)} %gather_fusion.3, pred[15]{0:T(512)(128)(4,1)S(1)} %get-tuple-element.11), kind=kLoop, calls=%fused_computation.5 | loop fusion | flops 491520 | bytes 2949135 | tf_op jit(solution)/shard_map/add | solution.py:191
  (29 shorter events, 0.4 us)
Async XLA Ops:
  0.0 1.3 %copy-start.2 = (s32[16,2]{0,1:T(2,128)S(1)}, s32[16,2]{0,1:T(2,128)}, u32[]{:S(2)}) copy-start(s32[16,2]{0,1:T(2,128)} %param.8) | copy-start | bytes 388
  0.0 8.5 %copy-start.3 = (s32[16,8]{0,1:T(8,128)S(1)}, s32[16,8]{0,1:T(8,128)}, u32[]{:S(2)}) copy-start(s32[16,8]{0,1:T(8,128)} %param.6) | copy-start | bytes 1540
  0.0 9.0 %copy-start.4 = (s32[1,15]{1,0:T(1,128)S(1)}, s32[1,15]{1,0:T(1,128)}, u32[]{:S(2)}) copy-start(s32[1,15]{1,0:T(1,128)} %param.9) | copy-start | bytes 184
  1.6 12.1 %collective-permute-start = (f32[5,2,128,128]{3,2,1,0:T(8,128)S(1)}, f32[5,2,128,128]{3,2,1,0:T(8,128)S(1)}, u32[]{:S(2)}, u32[]{:S(2)}) collective-permute-start(f32[5,2,128,128]{3,2,1,0:T(8,128)S(1)} %select_maximum_fusion.1), channel_id=1, source_target_pairs={{0,8},{8,16},{16,24},{1,9},{9,17},{17,25},{2,10},{10,18},{18,26},{... | collective-permute-start | bytes 1966088 | tf_op jit(solution)/shard_map/ppermute | solution.py:112
  6.4 11.9 %collective-permute-start.1 = (f32[5,2,128,128]{3,2,1,0:T(8,128)S(1)}, f32[5,2,128,128]{3,2,1,0:T(8,128)S(1)}, u32[]{:S(2)}, u32[]{:S(2)}) collective-permute-start(f32[5,2,128,128]{3,2,1,0:T(8,128)S(1)} %select_maximum_fusion), channel_id=1, source_target_pairs={{8,0},{16,8},{24,16},{9,1},{17,9},{25,17},{10,2},{18,10},{26,18},{... | collective-permute-start | bytes 1966088 | tf_op jit(solution)/shard_map/ppermute | solution.py:113
  13.7 6.2 %copy-start = (f32[5,2,128,128]{3,2,1,0:T(8,128)}, f32[5,2,128,128]{3,2,1,0:T(8,128)S(1)}, u32[]{:S(2)}) copy-start(f32[5,2,128,128]{3,2,1,0:T(8,128)S(1)} %collective-permute-done.low_ref) | copy-start | bytes 1966084
  18.3 1.5 %copy-start.1 = (f32[5,2,128,128]{3,2,1,0:T(8,128)}, f32[5,2,128,128]{3,2,1,0:T(8,128)S(1)}, u32[]{:S(2)}) copy-start(f32[5,2,128,128]{3,2,1,0:T(8,128)S(1)} %collective-permute-done.1.up_ref) | copy-start | bytes 1966084
  43.4 19.9 %collective-permute-start.2 = (f32[1,9,128,128]{3,2,1,0:T(8,128)}, f32[1,9,128,128]{3,2,1,0:T(8,128)S(1)}, u32[]{:S(2)}, u32[]{:S(2)}) collective-permute-start(f32[1,9,128,128]{3,2,1,0:T(8,128)} %get-tuple-element.9), channel_id=1, source_target_pairs={{0,1},{1,2},{2,3},{3,4},{4,5},{5,6},{6,7},{7,0},{8,9},{9,10},{10,1... | collective-permute-start | bytes 1769480 | tf_op jit(solution)/shard_map/ppermute | solution.py:16
  44.6 20.8 %collective-permute-start.3 = (f32[1,9,128,128]{3,2,1,0:T(8,128)}, f32[1,9,128,128]{3,2,1,0:T(8,128)S(1)}, u32[]{:S(2)}, u32[]{:S(2)}) collective-permute-start(f32[1,9,128,128]{3,2,1,0:T(8,128)} %get-tuple-element.10), channel_id=1, source_target_pairs={{0,7},{1,0},{2,1},{3,2},{4,3},{5,4},{6,5},{7,6},{8,15},{9,8},{10,9... | collective-permute-start | bytes 1769480 | tf_op jit(solution)/shard_map/ppermute | solution.py:16

commit v12 on v11

--- a/solution.py
+++ b/solution.py
@@ -104,18 +104,14 @@
 
     ext_rows = rows + 2 * RIM
 
-    def halo(first):
-        keys = p_cols[first : first + RIM].astype(jnp.float32).reshape(1, 1, 1, RIM * interp_slots)
-        key_tile = jnp.pad(keys, ((0, 0), (0, interp_slots - 1), (0, bs - 1), (0, bs - RIM * interp_slots)))
-        return jnp.concatenate([p_tiles[first : first + RIM], key_tile], axis=0)
-
-    low = lax.ppermute(halo(rows - RIM), "slab", [(i, i + 1) for i in range(slabs - 1)])
-    up = lax.ppermute(halo(0), "slab", [(i + 1, i) for i in range(slabs - 1)])
-
-    def halo_keys(block):
-        return block[RIM, 0, 0, : RIM * interp_slots].astype(jnp.int32).reshape(RIM, interp_slots)
-
-    ext_keys = jnp.concatenate([halo_keys(low), p_cols, halo_keys(up)], axis=0)
+    up_pairs = [(i, i + 1) for i in range(slabs - 1)]
+    down_pairs = [(i + 1, i) for i in range(slabs - 1)]
+    low = lax.ppermute(p_tiles[rows - RIM :], "slab", up_pairs)
+    up = lax.ppermute(p_tiles[:RIM], "slab", down_pairs)
+    low_keys = lax.ppermute(p_cols[rows - RIM :], "slab", up_pairs)
+    up_keys = lax.ppermute(p_cols[:RIM], "slab", down_pairs)
+
+    ext_keys = jnp.concatenate([low_keys, p_cols, up_keys], axis=0)
 
     own_base = device * rows
     lower_base = (device - tiles) * rows + rows - RIM

time: 67.4 us -> 72.3 us (1.073)
  starting transfers between devices: 10.8 us -> 16.3 us
  waiting for transfers between devices: 23 us -> 21.6 us
  local copies, waits for them, and re-layouts: 6.14 us -> 7.23 us
    ppermute x2 -> x4, starting transfers between devices: 6.46 us -> 12 us  [the longest x1 4.53 us: shards(): low_keys = lax.ppermute(p_cols[rows - RIM:], 'slab', up_pairs)]
    ppermute x2 -> x4, waiting for transfers between devices: 8.53 us -> 5.79 us  [the longest x1 4.39 us: shards(): up = lax.ppermute(p_tiles[:RIM], 'slab', down_pairs)]
    ppermute x2, waiting for transfers between devices: 14.5 us -> 15.8 us  [passed_along(): return lax.ppermute(value, axis, pairs)]
    slice x1 -> x2, local copies, waits for them, and re-layouts: 1.31 us -> 2.13 us  [the longest x1 1.28 us: shards(): up = lax.ppermute(p_tiles[:RIM], 'slab', down_pairs)]
  transfers between devices with their start and end apart: 4 -> 6, of which waited for: 4 -> 4; matrix products, arithmetic and copies ran while one was open for 7% -> 10% of each run, Pallas kernels for 0% -> 0%
where the time goes in v12:
time: 72.3 us; the launch traced here: 72 us
  Pallas kernels  23.4 us (32%)
  waiting for transfers between devices  21.6 us (30%)
  starting transfers between devices  16.3 us (23%)
  local copies, waits for them, and re-layouts  7.23 us (10%)
  other arithmetic  3.25 us (4%)
    pallas_call x1, Pallas kernels, shards(): pl.pallas_call(kernel, out_shape=(part, part, part), grid_spec=pltpu.Pref...  23.4 us
    ppermute x2, waiting for transfers between devices, passed_along(): return lax.ppermute(value, axis, pairs)  15.8 us
    ppermute x1, starting transfers between devices, shards(): low_keys = lax.ppermute(p_cols[rows - RIM:], 'slab', up_pairs)  4.53 us
    ppermute x1, waiting for transfers between devices, shards(): up = lax.ppermute(p_tiles[:RIM], 'slab', down_pairs)  4.39 us
    ppermute x2, starting transfers between devices, passed_along(): return lax.ppermute(value, axis, pairs)  4.31 us
    ppermute x1, starting transfers between devices, shards(): low = lax.ppermute(p_tiles[rows - RIM:], 'slab', up_pairs)  3.64 us
    gather x3, local copies, waits for them, and re-layouts, pick(): tiles_picked = part[r_idx, idx]  2.9 us
    ppermute x1, starting transfers between devices, shards(): up_keys = lax.ppermute(p_cols[:RIM], 'slab', down_pairs)  1.92 us
  transfers between devices with their start and end apart: 6, of which 4 were waited for; matrix products, arithmetic and copies ran while one was open for 10% of the time, Pallas kernels for 0%

profile of v12, /device:TPU:1, one launch (start us, length us, event | category | flops | bytes accessed | tf_op | source)
XLA Modules:
  0.0 72.0 jit_solution(11917896582890068475)
XLA Ops:
  0.0 0.9 %fusion.18 = (s32[4,2]{0,1:T(2,128)S(1)}, s32[4,2]{0,1:T(2,128)S(1)}) fusion(s32[16,2]{0,1:T(2,128)} %param.8), kind=kLoop, calls=%fused_computation.63 | loop fusion | bytes 128 | tf_op jit(solution)/shard_map/slice | solution.py:111
  0.9 4.5 %collective-permute-start = (s32[4,2]{0,1:T(2,128)S(1)}, s32[4,2]{0,1:T(2,128)S(1)}, u32[]{:S(2)}, u32[]{:S(2)}) collective-permute-start(s32[4,2]{0,1:T(2,128)S(1)} %get-tuple-element.21), channel_id=1, source_target_pairs={{0,8},{8,16},{16,24},{1,9},{9,17},{17,25},{2,10},{10,18},{18,26},{... | collective-permute-start | bytes 104 | tf_op jit(solution)/shard_map/ppermute | solution.py:111
  5.4 1.9 %collective-permute-start.1 = (s32[4,2]{0,1:T(2,128)S(1)}, s32[4,2]{0,1:T(2,128)S(1)}, u32[]{:S(2)}, u32[]{:S(2)}) collective-permute-start(s32[4,2]{0,1:T(2,128)S(1)} %get-tuple-element.22), channel_id=1, source_target_pairs={{8,0},{16,8},{24,16},{9,1},{17,9},{25,17},{10,2},{18,10},{26,18},{... | collective-permute-start | bytes 104 | tf_op jit(solution)/shard_map/ppermute | solution.py:112
  7.3 1.3 %fusion.17 = (f32[4,2,128,128]{3,2,1,0:T(8,128)S(1)}, f32[4,2,128,128]{3,2,1,0:T(8,128)S(1)}) fusion(f32[16,2,128,128]{3,2,1,0:T(8,128)} %mid_ref.1), kind=kLoop, calls=%fused_computation.62 | loop fusion | bytes 2097152 | tf_op jit(solution)/shard_map/slice | solution.py:110
  8.6 3.6 %collective-permute-start.2 = (f32[4,2,128,128]{3,2,1,0:T(8,128)S(1)}, f32[4,2,128,128]{3,2,1,0:T(8,128)S(1)}, u32[]{:S(2)}, u32[]{:S(2)}) collective-permute-start(f32[4,2,128,128]{3,2,1,0:T(8,128)S(1)} %get-tuple-element.18), channel_id=1, source_target_pairs={{0,8},{8,16},{16,24},{1,9},{9,17},{17,25},{2,10},{10,18},{18,26},{... | collective-permute-start | bytes 1572872 | tf_op jit(solution)/shard_map/ppermute | solution.py:109
  12.3 1.9 %collective-permute-start.3 = (f32[4,2,128,128]{3,2,1,0:T(8,128)S(1)}, f32[4,2,128,128]{3,2,1,0:T(8,128)S(1)}, u32[]{:S(2)}, u32[]{:S(2)}) collective-permute-start(f32[4,2,128,128]{3,2,1,0:T(8,128)S(1)} %get-tuple-element.17), channel_id=1, source_target_pairs={{8,0},{16,8},{24,16},{9,1},{17,9},{25,17},{10,2},{18,10},{26,18},{... | collective-permute-start | bytes 1572872 | tf_op jit(solution)/shard_map/ppermute | solution.py:110
  14.3 0.6 and_bitcast_fusion.2
  14.9 0.1 copy.19
  14.9 0.1 reshape.51
  15.0 0.1 copy.18
  15.1 0.1 reshape.47
  15.2 0.1 copy.21
  15.3 0.1 reshape.48
  15.4 0.0 collective-permute-done.1
  15.4 0.1 pad_add_fusion.1
  15.5 0.1 copy.20
  15.6 0.6 gather_fusion
  16.2 0.1 gather.15
  16.4 0.6 pad_add_fusion.idx_ref
  17.0 1.4 %collective-permute-done.2.low_ref = f32[4,2,128,128]{3,2,1,0:T(8,128)S(1)} collective-permute-done((f32[4,2,128,128]{3,2,1,0:T(8,128)S(1)}, f32[4,2,128,128]{3,2,1,0:T(8,128)S(1)}, u32[]{:S(2)}, u32[]{:S(2)}) %collective-permute-start.2) | collective-permute-done | bytes 524320 | tf_op jit(solution)/shard_map/ppermute | solution.py:109
  18.4 4.4 %collective-permute-done.3.up_ref = f32[4,2,128,128]{3,2,1,0:T(8,128)S(1)} collective-permute-done((f32[4,2,128,128]{3,2,1,0:T(8,128)S(1)}, f32[4,2,128,128]{3,2,1,0:T(8,128)S(1)}, u32[]{:S(2)}, u32[]{:S(2)}) %collective-permute-start.3) | collective-permute-done | bytes 524320 | tf_op jit(solution)/shard_map/ppermute | solution.py:110
  22.8 0.8 %copy-done.1 = f32[4,2,128,128]{3,2,1,0:T(8,128)} copy-done((f32[4,2,128,128]{3,2,1,0:T(8,128)}, f32[4,2,128,128]{3,2,1,0:T(8,128)S(1)}, u32[]{:S(2)}) %copy-start.1) | copy-done | bytes 524312
  23.6 23.4 %shard_map.55 = (f32[1,9,128,128]{3,2,1,0:T(8,128)}, f32[1,9,128,128]{3,2,1,0:T(8,128)}, f32[1,9,128,128]{3,2,1,0:T(8,128)}) custom-call(s32[416]{0:T(512)} %pad_add_fusion.idx_ref, f32[16,8,128,128]{3,2,1,0:T(8,128)} %a_ref.1, f32[4,2,128,128]{3,2,1,0:T(8,128)} %copy-done, f32[16,2,128,128]{3,2,1,0:T(8,128)} %mid_ref.1, f32[4,2,128,128]{3,2,1,0:T(8,128)} %copy-done.1), custom_call_target="tpu_custom_call" | custom-call | tf_op jit(solution)/shard_map/pallas_call | solution.py:147
  47.0 1.2 %collective-permute-start.4 = (f32[1,9,128,128]{3,2,1,0:T(8,128)}, f32[1,9,128,128]{3,2,1,0:T(8,128)S(1)}, u32[]{:S(2)}, u32[]{:S(2)}) collective-permute-start(f32[1,9,128,128]{3,2,1,0:T(8,128)} %get-tuple-element.9), channel_id=1, source_target_pairs={{0,1},{1,2},{2,3},{3,4},{4,5},{5,6},{6,7},{7,0},{8,9},{9,10},{10,1... | collective-permute-start | bytes 1769480 | tf_op jit(solution)/shard_map/ppermute | solution.py:16
  48.2 3.1 %collective-permute-start.5 = (f32[1,9,128,128]{3,2,1,0:T(8,128)}, f32[1,9,128,128]{3,2,1,0:T(8,128)S(1)}, u32[]{:S(2)}, u32[]{:S(2)}) collective-permute-start(f32[1,9,128,128]{3,2,1,0:T(8,128)} %get-tuple-element.10), channel_id=1, source_target_pairs={{0,7},{1,0},{2,1},{3,2},{4,3},{5,4},{6,5},{7,6},{8,15},{9,8},{10,9... | collective-permute-start | bytes 1769480 | tf_op jit(solution)/shard_map/ppermute | solution.py:16
  51.3 1.7 %gather_fusion.1 = f32[15,128,128]{2,1,0:T(8,128)S(1)} fusion(f32[1,9,128,128]{3,2,1,0:T(8,128)} %get-tuple-element.8, s32[15]{0:T(128)S(1)} %or_bitcast_fusion.2), kind=kCustom, calls=%fused_computation.1 | custom fusion | bytes 1966200 | tf_op jit(solution)/shard_map/gather | solution.py:183
  53.0 15.1 %collective-permute-done.4 = f32[1,9,128,128]{3,2,1,0:T(8,128)S(1)} collective-permute-done((f32[1,9,128,128]{3,2,1,0:T(8,128)}, f32[1,9,128,128]{3,2,1,0:T(8,128)S(1)}, u32[]{:S(2)}, u32[]{:S(2)}) %collective-permute-start.4) | collective-permute-done | bytes 589856 | tf_op jit(solution)/shard_map/ppermute | solution.py:16
  68.1 0.6 gather_fusion.2
  68.7 0.8 %fusion.1 = f32[1,15,128,128]{3,2,1,0:T(8,128)S(1)} fusion(f32[15,128,128]{2,1,0:T(8,128)S(1)} %gather_fusion.2, f32[15,128,128]{2,1,0:T(8,128)S(1)} %gather_fusion.1, pred[15]{0:T(512)(128)(4,1)} %get-tuple-element.24, pred[15]{0:T(512)(128)(4,1)S(1)} %get-tuple-element.23), kind=kLoop, calls=%fused_computation.7 | loop fusion | flops 737280 | bytes 2949150 | tf_op jit(solution)/shard_map/add | solution.py:186
  69.5 0.7 collective-permute-done.5
  70.2 0.6 gather_fusion.3
  70.9 1.1 %fusion = f32[1,15,128,128]{3,2,1,0:T(8,128)} fusion(f32[1,15,128,128]{3,2,1,0:T(8,128)S(1)} %fusion.1, f32[15,128,128]{2,1,0:T(8,128)S(1)} %gather_fusion.3, pred[15]{0:T(512)(128)(4,1)S(1)} %get-tuple-element.11), kind=kLoop, calls=%fused_computation.5 | loop fusion | flops 491520 | bytes 2949135 | tf_op jit(solution)/shard_map/add | solution.py:187
  (23 shorter events, 0.2 us)
Async XLA Ops:
  0.0 14.2 %copy-start.2 = (s32[16,2]{0,1:T(2,128)S(1)}, s32[16,2]{0,1:T(2,128)}, u32[]{:S(2)}) copy-start(s32[16,2]{0,1:T(2,128)} %param.8) | copy-start | bytes 388
  0.0 14.2 %copy-start.4 = (s32[1,15]{1,0:T(1,128)S(1)}, s32[1,15]{1,0:T(1,128)}, u32[]{:S(2)}) copy-start(s32[1,15]{1,0:T(1,128)} %param.9) | copy-start | bytes 184
  0.0 14.8 %copy-start.3 = (s32[16,8]{0,1:T(8,128)S(1)}, s32[16,8]{0,1:T(8,128)}, u32[]{:S(2)}) copy-start(s32[16,8]{0,1:T(8,128)} %param.6) | copy-start | bytes 1540
  0.9 14.6 %collective-permute-start = (s32[4,2]{0,1:T(2,128)S(1)}, s32[4,2]{0,1:T(2,128)S(1)}, u32[]{:S(2)}, u32[]{:S(2)}) collective-permute-start(s32[4,2]{0,1:T(2,128)S(1)} %get-tuple-element.21), channel_id=1, source_target_pairs={{0,8},{8,16},{16,24},{1,9},{9,17},{17,25},{2,10},{10,18},{18,26},{... | collective-permute-start | bytes 104 | tf_op jit(solution)/shard_map/ppermute | solution.py:111
  5.4 10.0 %collective-permute-start.1 = (s32[4,2]{0,1:T(2,128)S(1)}, s32[4,2]{0,1:T(2,128)S(1)}, u32[]{:S(2)}, u32[]{:S(2)}) collective-permute-start(s32[4,2]{0,1:T(2,128)S(1)} %get-tuple-element.22), channel_id=1, source_target_pairs={{8,0},{16,8},{24,16},{9,1},{17,9},{25,17},{10,2},{18,10},{26,18},{... | collective-permute-start | bytes 104 | tf_op jit(solution)/shard_map/ppermute | solution.py:112
  8.6 9.8 %collective-permute-start.2 = (f32[4,2,128,128]{3,2,1,0:T(8,128)S(1)}, f32[4,2,128,128]{3,2,1,0:T(8,128)S(1)}, u32[]{:S(2)}, u32[]{:S(2)}) collective-permute-start(f32[4,2,128,128]{3,2,1,0:T(8,128)S(1)} %get-tuple-element.18), channel_id=1, source_target_pairs={{0,8},{8,16},{16,24},{1,9},{9,17},{17,25},{2,10},{10,18},{18,26},{... | collective-permute-start | bytes 1572872 | tf_op jit(solution)/shard_map/ppermute | solution.py:109
  12.3 10.5 %collective-permute-start.3 = (f32[4,2,128,128]{3,2,1,0:T(8,128)S(1)}, f32[4,2,128,128]{3,2,1,0:T(8,128)S(1)}, u32[]{:S(2)}, u32[]{:S(2)}) collective-permute-start(f32[4,2,128,128]{3,2,1,0:T(8,128)S(1)} %get-tuple-element.17), channel_id=1, source_target_pairs={{8,0},{16,8},{24,16},{9,1},{17,9},{25,17},{10,2},{18,10},{26,18},{... | collective-permute-start | bytes 1572872 | tf_op jit(solution)/shard_map/ppermute | solution.py:110
  18.4 4.4 %copy-start = (f32[4,2,128,128]{3,2,1,0:T(8,128)}, f32[4,2,128,128]{3,2,1,0:T(8,128)S(1)}, u32[]{:S(2)}) copy-start(f32[4,2,128,128]{3,2,1,0:T(8,128)S(1)} %collective-permute-done.2.low_ref) | copy-start | bytes 1572868
  22.8 0.8 %copy-start.1 = (f32[4,2,128,128]{3,2,1,0:T(8,128)}, f32[4,2,128,128]{3,2,1,0:T(8,128)S(1)}, u32[]{:S(2)}) copy-start(f32[4,2,128,128]{3,2,1,0:T(8,128)S(1)} %collective-permute-done.3.up_ref) | copy-start | bytes 1572868
  47.0 21.1 %collective-permute-start.4 = (f32[1,9,128,128]{3,2,1,0:T(8,128)}, f32[1,9,128,128]{3,2,1,0:T(8,128)S(1)}, u32[]{:S(2)}, u32[]{:S(2)}) collective-permute-start(f32[1,9,128,128]{3,2,1,0:T(8,128)} %get-tuple-element.9), channel_id=1, source_target_pairs={{0,1},{1,2},{2,3},{3,4},{4,5},{5,6},{6,7},{7,0},{8,9},{9,10},{10,1... | collective-permute-start | bytes 1769480 | tf_op jit(solution)/shard_map/ppermute | solution.py:16
  48.2 22.0 %collective-permute-start.5 = (f32[1,9,128,128]{3,2,1,0:T(8,128)}, f32[1,9,128,128]{3,2,1,0:T(8,128)S(1)}, u32[]{:S(2)}, u32[]{:S(2)}) collective-permute-start(f32[1,9,128,128]{3,2,1,0:T(8,128)} %get-tuple-element.10), channel_id=1, source_target_pairs={{0,7},{1,0},{2,1},{3,2},{4,3},{5,4},{6,5},{7,6},{8,15},{9,8},{10,9... | collective-permute-start | bytes 1769480 | tf_op jit(solution)/shard_map/ppermute | solution.py:16

commit v13 on v11

--- a/solution.py
+++ b/solution.py
@@ -8,6 +8,7 @@
 from jax.sharding import PartitionSpec as P
 
 RIM = 4
+HIGH = lax.Precision.HIGH
 
 
 def passed_along(value, axis, steps):
@@ -52,11 +53,7 @@
         def fill(src, offset, count):
             def body(r, carry):
                 for p in range(interp_slots):
-                    hi, lo = split(src[r, p])
-                    cols = slice(p * bs, (p + 1) * bs)
-                    p3_ref[offset + r, 0:bs, cols] = hi
-                    p3_ref[offset + r, bs : 2 * bs, cols] = lo
-                    p3_ref[offset + r, 2 * bs : 3 * bs, cols] = hi
+                    p3_ref[offset + r, :, p * bs : (p + 1) * bs] = src[r, p]
                 return carry
 
             lax.fori_loop(0, count, body, 0)
@@ -70,14 +67,14 @@
         y_ref[...] = jnp.zeros_like(y_ref)
         for a in range(coupling_slots):
             row = idx_ref[gi * coupling_slots + a]
-            prod = jnp.dot(stack_lhs(a_ref[i, a]), p3_ref[row], preferred_element_type=jnp.float32)
+            prod = jnp.dot(a_ref[i, a], p3_ref[row], precision=HIGH, preferred_element_type=jnp.float32)
             for p in range(interp_slots):
                 slot = idx_ref[slot_base + (gi * coupling_slots + a) * interp_slots + p]
                 y_ref[slot] += prod[:, p * bs : (p + 1) * bs]
-        pt = stack_lhs(jnp.concatenate([mid_ref[gi, q].T for q in range(interp_slots)], axis=0))
+        pt = jnp.concatenate([mid_ref[gi, q].T for q in range(interp_slots)], axis=0)
         owners = [idx_ref[owner_base + gi * interp_slots + q] for q in range(interp_slots)]
         for c in range(region):
-            res = jnp.dot(pt, stack_rhs(y_ref[c]), preferred_element_type=jnp.float32)
+            res = jnp.dot(pt, y_ref[c], precision=HIGH, preferred_element_type=jnp.float32)
             for q in range(interp_slots):
                 acc_ref[owners[q], c] += res[q * bs : (q + 1) * bs]
         return carry
@@ -164,7 +161,7 @@
             scratch_shapes=[
                 pltpu.VMEM((region, bs, bs), jnp.float32),
                 pltpu.VMEM((3 * blocks, region, bs, bs), jnp.float32),
-                pltpu.VMEM((ext_rows, 3 * bs, interp_slots * bs), jnp.bfloat16),
+                pltpu.VMEM((ext_rows, bs, interp_slots * bs), jnp.float32),
             ],
         ),
         compiler_params=pltpu.CompilerParams(dimension_semantics=("arbitrary",)),

time: 67.4 us -> 69.8 us (1.036)
  Pallas kernels: 23.5 us -> 25.9 us
    pallas_call x1, Pallas kernels: 23.5 us -> 25.9 us  [shards(): pl.pallas_call(kernel, out_shape=(part, part, part), grid_spec=pltpu.Pref...]
where the time goes in v13:
time: 69.8 us; the launch traced here: 69.5 us
  Pallas kernels  25.9 us (37%)
  waiting for transfers between devices  23.1 us (33%)
  starting transfers between devices  10.8 us (15%)
  local copies, waits for them, and re-layouts  6.14 us (9%)
  other arithmetic  3.49 us (5%)
    pallas_call x1, Pallas kernels, shards(): pl.pallas_call(kernel, out_shape=(part, part, part), grid_spec=pltpu.Pref...  25.9 us
    ppermute x2, waiting for transfers between devices, passed_along(): return lax.ppermute(value, axis, pairs)  14.5 us
    ppermute x1, starting transfers between devices, shards(): lax.ppermute(halo(rows - RIM), 'slab', [(i, i + 1) for i in range(slabs -...  4.54 us
    ppermute x1, waiting for transfers between devices, shards(): up = lax.ppermute(halo(0), 'slab', [(i + 1, i) for i in range(slabs - 1)])  4.52 us
    ppermute x2, starting transfers between devices, passed_along(): return lax.ppermute(value, axis, pairs)  4.3 us
    ppermute x1, waiting for transfers between devices, shards(): lax.ppermute(halo(rows - RIM), 'slab', [(i, i + 1) for i in range(slabs -...  4.01 us
    gather x3, local copies, waits for them, and re-layouts, pick(): tiles_picked = part[r_idx, idx]  2.9 us
    ppermute x1, starting transfers between devices, shards(): up = lax.ppermute(halo(0), 'slab', [(i + 1, i) for i in range(slabs - 1)])  1.92 us
  transfers between devices with their start and end apart: 4, of which 4 were waited for; matrix products, arithmetic and copies ran while one was open for 7% of the time, Pallas kernels for 0%

profile of v13, /device:TPU:1, one launch (start us, length us, event | category | flops | bytes accessed | tf_op | source)
XLA Modules:
  0.0 69.5 jit_solution(457099108956030060)
XLA Ops:
  0.0 1.3 %fusion.19 = (f32[4,2,128,128]{3,2,1,0:T(8,128)S(1)}, f32[4,2,128,128]{3,2,1,0:T(8,128)S(1)}) fusion(f32[16,2,128,128]{3,2,1,0:T(8,128)} %mid_ref.1), kind=kLoop, calls=%fused_computation.71 | loop fusion | bytes 2097152 | tf_op jit(solution)/shard_map/slice | solution.py:107
  1.3 0.1 slice_convert_fusion.1
  1.4 0.1 copy.27
  1.5 0.1 reshape.60
  1.6 4.5 %collective-permute-start = (f32[5,2,128,128]{3,2,1,0:T(8,128)S(1)}, f32[5,2,128,128]{3,2,1,0:T(8,128)S(1)}, u32[]{:S(2)}, u32[]{:S(2)}) collective-permute-start(f32[5,2,128,128]{3,2,1,0:T(8,128)S(1)} %select_maximum_fusion.1), channel_id=1, source_target_pairs={{0,8},{8,16},{16,24},{1,9},{9,17},{17,25},{2,10},{10,18},{18,26},{... | collective-permute-start | bytes 1966088 | tf_op jit(solution)/shard_map/ppermute | solution.py:109
  6.2 0.1 copy.28
  6.3 0.1 reshape.61
  6.4 1.9 %collective-permute-start.1 = (f32[5,2,128,128]{3,2,1,0:T(8,128)S(1)}, f32[5,2,128,128]{3,2,1,0:T(8,128)S(1)}, u32[]{:S(2)}, u32[]{:S(2)}) collective-permute-start(f32[5,2,128,128]{3,2,1,0:T(8,128)S(1)} %select_maximum_fusion), channel_id=1, source_target_pairs={{8,0},{16,8},{24,16},{9,1},{17,9},{25,17},{10,2},{18,10},{26,18},{... | collective-permute-start | bytes 1966088 | tf_op jit(solution)/shard_map/ppermute | solution.py:110
  8.4 0.1 copy.29
  8.5 0.1 copy.30
  8.6 0.1 reshape.65
  8.7 0.1 reshape.59
  8.8 0.1 copy.31
  8.9 0.1 reshape.62
  9.1 0.6 and_bitcast_fusion.2
  9.7 4.0 %collective-permute-done.low_ref = f32[5,2,128,128]{3,2,1,0:T(8,128)S(1)} collective-permute-done((f32[5,2,128,128]{3,2,1,0:T(8,128)S(1)}, f32[5,2,128,128]{3,2,1,0:T(8,128)S(1)}, u32[]{:S(2)}, u32[]{:S(2)}) %collective-permute-start) | collective-permute-done | bytes 655392 | tf_op jit(solution)/shard_map/ppermute | solution.py:109
  13.7 0.1 convert_element_type.25
  13.8 4.5 %collective-permute-done.1.up_ref = f32[5,2,128,128]{3,2,1,0:T(8,128)S(1)} collective-permute-done((f32[5,2,128,128]{3,2,1,0:T(8,128)S(1)}, f32[5,2,128,128]{3,2,1,0:T(8,128)S(1)}, u32[]{:S(2)}, u32[]{:S(2)}) %collective-permute-start.1) | collective-permute-done | bytes 655392 | tf_op jit(solution)/shard_map/ppermute | solution.py:110
  18.4 0.1 convert_element_type.28
  18.4 0.6 gather_fusion
  19.1 0.1 gather.15
  19.3 0.6 pad_add_fusion.1.idx_ref
  19.9 25.9 %shard_map.55 = (f32[1,9,128,128]{3,2,1,0:T(8,128)}, f32[1,9,128,128]{3,2,1,0:T(8,128)}, f32[1,9,128,128]{3,2,1,0:T(8,128)}) custom-call(s32[416]{0:T(512)} %pad_add_fusion.1.idx_ref, f32[16,8,128,128]{3,2,1,0:T(8,128)} %a_ref.1, f32[5,2,128,128]{3,2,1,0:T(8,128)} %copy-done, f32[16,2,128,128]{3,2,1,0:T(8,128)} %mid_ref.1, f32[5,2,128,128]{3,2,1,0:T(8,128)} %copy-done.1), custom_call_target="tpu_custom_call" | custom-call | tf_op jit(solution)/shard_map/pallas_call | solution.py:148
  45.8 1.2 %collective-permute-start.2 = (f32[1,9,128,128]{3,2,1,0:T(8,128)}, f32[1,9,128,128]{3,2,1,0:T(8,128)S(1)}, u32[]{:S(2)}, u32[]{:S(2)}) collective-permute-start(f32[1,9,128,128]{3,2,1,0:T(8,128)} %get-tuple-element.9), channel_id=1, source_target_pairs={{0,1},{1,2},{2,3},{3,4},{4,5},{5,6},{6,7},{7,0},{8,9},{9,10},{10,1... | collective-permute-start | bytes 1769480 | tf_op jit(solution)/shard_map/ppermute | solution.py:17
  47.0 3.1 %collective-permute-start.3 = (f32[1,9,128,128]{3,2,1,0:T(8,128)}, f32[1,9,128,128]{3,2,1,0:T(8,128)S(1)}, u32[]{:S(2)}, u32[]{:S(2)}) collective-permute-start(f32[1,9,128,128]{3,2,1,0:T(8,128)} %get-tuple-element.10), channel_id=1, source_target_pairs={{0,7},{1,0},{2,1},{3,2},{4,3},{5,4},{6,5},{7,6},{8,15},{9,8},{10,9... | collective-permute-start | bytes 1769480 | tf_op jit(solution)/shard_map/ppermute | solution.py:17
  50.1 1.7 %gather_fusion.1 = f32[15,128,128]{2,1,0:T(8,128)S(1)} fusion(f32[1,9,128,128]{3,2,1,0:T(8,128)} %get-tuple-element.8, s32[15]{0:T(128)S(1)} %or_bitcast_fusion.2), kind=kCustom, calls=%fused_computation.1 | custom fusion | bytes 1966200 | tf_op jit(solution)/shard_map/gather | solution.py:184
  51.8 13.9 %collective-permute-done.2 = f32[1,9,128,128]{3,2,1,0:T(8,128)S(1)} collective-permute-done((f32[1,9,128,128]{3,2,1,0:T(8,128)}, f32[1,9,128,128]{3,2,1,0:T(8,128)S(1)}, u32[]{:S(2)}, u32[]{:S(2)}) %collective-permute-start.2) | collective-permute-done | bytes 589856 | tf_op jit(solution)/shard_map/ppermute | solution.py:17
  65.6 0.6 gather_fusion.2
  66.3 0.9 %fusion.1 = f32[1,15,128,128]{3,2,1,0:T(8,128)S(1)} fusion(f32[15,128,128]{2,1,0:T(8,128)S(1)} %gather_fusion.2, f32[15,128,128]{2,1,0:T(8,128)S(1)} %gather_fusion.1, pred[15]{0:T(512)(128)(4,1)} %get-tuple-element.24, pred[15]{0:T(512)(128)(4,1)S(1)} %get-tuple-element.23), kind=kLoop, calls=%fused_computation.7 | loop fusion | flops 737280 | bytes 2949150 | tf_op jit(solution)/shard_map/add | solution.py:187
  67.1 0.7 collective-permute-done.3
  67.8 0.6 gather_fusion.3
  68.4 1.1 %fusion = f32[1,15,128,128]{3,2,1,0:T(8,128)} fusion(f32[1,15,128,128]{3,2,1,0:T(8,128)S(1)} %fusion.1, f32[15,128,128]{2,1,0:T(8,128)S(1)} %gather_fusion.3, pred[15]{0:T(512)(128)(4,1)S(1)} %get-tuple-element.11), kind=kLoop, calls=%fused_computation.5 | loop fusion | flops 491520 | bytes 2949135 | tf_op jit(solution)/shard_map/add | solution.py:188
  (29 shorter events, 0.4 us)
Async XLA Ops:
  0.0 1.3 %copy-start.2 = (s32[16,2]{0,1:T(2,128)S(1)}, s32[16,2]{0,1:T(2,128)}, u32[]{:S(2)}) copy-start(s32[16,2]{0,1:T(2,128)} %param.8) | copy-start | bytes 388
  0.0 8.5 %copy-start.3 = (s32[16,8]{0,1:T(8,128)S(1)}, s32[16,8]{0,1:T(8,128)}, u32[]{:S(2)}) copy-start(s32[16,8]{0,1:T(8,128)} %param.6) | copy-start | bytes 1540
  0.0 9.0 %copy-start.4 = (s32[1,15]{1,0:T(1,128)S(1)}, s32[1,15]{1,0:T(1,128)}, u32[]{:S(2)}) copy-start(s32[1,15]{1,0:T(1,128)} %param.9) | copy-start | bytes 184
  1.6 12.1 %collective-permute-start = (f32[5,2,128,128]{3,2,1,0:T(8,128)S(1)}, f32[5,2,128,128]{3,2,1,0:T(8,128)S(1)}, u32[]{:S(2)}, u32[]{:S(2)}) collective-permute-start(f32[5,2,128,128]{3,2,1,0:T(8,128)S(1)} %select_maximum_fusion.1), channel_id=1, source_target_pairs={{0,8},{8,16},{16,24},{1,9},{9,17},{17,25},{2,10},{10,18},{18,26},{... | collective-permute-start | bytes 1966088 | tf_op jit(solution)/shard_map/ppermute | solution.py:109
  6.4 11.9 %collective-permute-start.1 = (f32[5,2,128,128]{3,2,1,0:T(8,128)S(1)}, f32[5,2,128,128]{3,2,1,0:T(8,128)S(1)}, u32[]{:S(2)}, u32[]{:S(2)}) collective-permute-start(f32[5,2,128,128]{3,2,1,0:T(8,128)S(1)} %select_maximum_fusion), channel_id=1, source_target_pairs={{8,0},{16,8},{24,16},{9,1},{17,9},{25,17},{10,2},{18,10},{26,18},{... | collective-permute-start | bytes 1966088 | tf_op jit(solution)/shard_map/ppermute | solution.py:110
  13.7 6.2 %copy-start = (f32[5,2,128,128]{3,2,1,0:T(8,128)}, f32[5,2,128,128]{3,2,1,0:T(8,128)S(1)}, u32[]{:S(2)}) copy-start(f32[5,2,128,128]{3,2,1,0:T(8,128)S(1)} %collective-permute-done.low_ref) | copy-start | bytes 1966084
  18.3 1.5 %copy-start.1 = (f32[5,2,128,128]{3,2,1,0:T(8,128)}, f32[5,2,128,128]{3,2,1,0:T(8,128)S(1)}, u32[]{:S(2)}) copy-start(f32[5,2,128,128]{3,2,1,0:T(8,128)S(1)} %collective-permute-done.1.up_ref) | copy-start | bytes 1966084
  45.8 19.9 %collective-permute-start.2 = (f32[1,9,128,128]{3,2,1,0:T(8,128)}, f32[1,9,128,128]{3,2,1,0:T(8,128)S(1)}, u32[]{:S(2)}, u32[]{:S(2)}) collective-permute-start(f32[1,9,128,128]{3,2,1,0:T(8,128)} %get-tuple-element.9), channel_id=1, source_target_pairs={{0,1},{1,2},{2,3},{3,4},{4,5},{5,6},{6,7},{7,0},{8,9},{9,10},{10,1... | collective-permute-start | bytes 1769480 | tf_op jit(solution)/shard_map/ppermute | solution.py:17
  47.0 20.8 %collective-permute-start.3 = (f32[1,9,128,128]{3,2,1,0:T(8,128)}, f32[1,9,128,128]{3,2,1,0:T(8,128)S(1)}, u32[]{:S(2)}, u32[]{:S(2)}) collective-permute-start(f32[1,9,128,128]{3,2,1,0:T(8,128)} %get-tuple-element.10), channel_id=1, source_target_pairs={{0,7},{1,0},{2,1},{3,2},{4,3},{5,4},{6,5},{7,6},{8,15},{9,8},{10,9... | collective-permute-start | bytes 1769480 | tf_op jit(solution)/shard_map/ppermute | solution.py:17

commit v14 on v11

--- a/solution.py
+++ b/solution.py
@@ -52,7 +52,12 @@
         def fill(src, offset, count):
             def body(r, carry):
                 for p in range(interp_slots):
-                    hi, lo = split(src[r, p])
+                    if len(src.shape) == 2:
+                        start = pl.multiple_of((r * interp_slots + p) * bs, bs)
+                        tile = src[pl.ds(start, bs), :]
+                    else:
+                        tile = src[r, p]
+                    hi, lo = split(tile)
                     cols = slice(p * bs, (p + 1) * bs)
                     p3_ref[offset + r, 0:bs, cols] = hi
                     p3_ref[offset + r, bs : 2 * bs, cols] = lo
@@ -104,16 +109,19 @@
 
     ext_rows = rows + 2 * RIM
 
+    key_count = RIM * interp_slots
+
     def halo(first):
-        keys = p_cols[first : first + RIM].astype(jnp.float32).reshape(1, 1, 1, RIM * interp_slots)
-        key_tile = jnp.pad(keys, ((0, 0), (0, interp_slots - 1), (0, bs - 1), (0, bs - RIM * interp_slots)))
-        return jnp.concatenate([p_tiles[first : first + RIM], key_tile], axis=0)
+        keys = p_cols[first : first + RIM].astype(jnp.float32).reshape(1, key_count)
+        key_rows = jnp.pad(keys, ((0, 7), (0, bs - key_count)))
+        flat = p_tiles[first : first + RIM].reshape(RIM * interp_slots * bs, bs)
+        return jnp.concatenate([flat, key_rows], axis=0)
 
     low = lax.ppermute(halo(rows - RIM), "slab", [(i, i + 1) for i in range(slabs - 1)])
     up = lax.ppermute(halo(0), "slab", [(i + 1, i) for i in range(slabs - 1)])
 
     def halo_keys(block):
-        return block[RIM, 0, 0, : RIM * interp_slots].astype(jnp.int32).reshape(RIM, interp_slots)
+        return block[key_count * bs, :key_count].astype(jnp.int32).reshape(RIM, interp_slots)
 
     ext_keys = jnp.concatenate([halo_keys(low), p_cols, halo_keys(up)], axis=0)
 
@@ -156,9 +164,9 @@
             grid=(rows // per_step,),
             in_specs=[
                 pl.BlockSpec((per_step, coupling_slots, bs, bs), lambda g, *_: (g, 0, 0, 0)),
-                pl.BlockSpec(low.shape, lambda g, *_: (0, 0, 0, 0)),
+                pl.BlockSpec(low.shape, lambda g, *_: (0, 0)),
                 pl.BlockSpec(p_tiles.shape, lambda g, *_: (0, 0, 0, 0)),
-                pl.BlockSpec(up.shape, lambda g, *_: (0, 0, 0, 0)),
+                pl.BlockSpec(up.shape, lambda g, *_: (0, 0)),
             ],
             out_specs=(part_spec, part_spec, part_spec),
             scratch_shapes=[

time: 67.4 us -> 67.1 us (level)
    ppermute x1, waiting for transfers between devices: 4.01 us -> 2.72 us  [shards(): lax.ppermute(halo(rows - RIM), 'slab', [(i, i + 1) for i in range(slabs -...]
    ppermute x2, waiting for transfers between devices: 14.5 us -> 15.8 us  [passed_along(): return lax.ppermute(value, axis, pairs)]
where the time goes in v14:
time: 67.1 us; the launch traced here: 66.8 us
  Pallas kernels  23.4 us (35%)
  waiting for transfers between devices  23 us (34%)
  starting transfers between devices  10.8 us (16%)
  local copies, waits for them, and re-layouts  6.14 us (9%)
  other arithmetic  3.35 us (5%)
    pallas_call x1, Pallas kernels, shards(): pl.pallas_call(kernel, out_shape=(part, part, part), grid_spec=pltpu.Pref...  23.4 us
    ppermute x2, waiting for transfers between devices, passed_along(): return lax.ppermute(value, axis, pairs)  15.8 us
    ppermute x1, starting transfers between devices, shards(): lax.ppermute(halo(rows - RIM), 'slab', [(i, i + 1) for i in range(slabs -...  4.54 us
    ppermute x1, waiting for transfers between devices, shards(): up = lax.ppermute(halo(0), 'slab', [(i + 1, i) for i in range(slabs - 1)])  4.51 us
    ppermute x2, starting transfers between devices, passed_along(): return lax.ppermute(value, axis, pairs)  4.31 us
    gather x3, local copies, waits for them, and re-layouts, pick(): tiles_picked = part[r_idx, idx]  2.9 us
    ppermute x1, waiting for transfers between devices, shards(): lax.ppermute(halo(rows - RIM), 'slab', [(i, i + 1) for i in range(slabs -...  2.72 us
    ppermute x1, starting transfers between devices, shards(): up = lax.ppermute(halo(0), 'slab', [(i + 1, i) for i in range(slabs - 1)])  1.92 us
  transfers between devices with their start and end apart: 4, of which 4 were waited for; matrix products, arithmetic and copies ran while one was open for 7% of the time, Pallas kernels for 0%

profile of v14, /device:TPU:1, one launch (start us, length us, event | category | flops | bytes accessed | tf_op | source)
XLA Modules:
  0.0 66.8 jit_solution(7648176706467874400)
XLA Ops:
  0.0 1.3 %fusion.19 = (f32[4,2,128,128]{3,2,1,0:T(8,128)S(1)}, f32[4,2,128,128]{3,2,1,0:T(8,128)S(1)}) fusion(f32[16,2,128,128]{3,2,1,0:T(8,128)} %mid_ref.1), kind=kLoop, calls=%fused_computation.71 | loop fusion | bytes 2097152 | tf_op jit(solution)/shard_map/slice | solution.py:117
  1.3 0.1 slice_convert_fusion.1
  1.4 0.1 copy.27
  1.5 0.1 reshape.67
  1.6 4.5 %collective-permute-start = (f32[1032,128]{1,0:T(8,128)S(1)}, f32[1032,128]{1,0:T(8,128)S(1)}, u32[]{:S(2)}, u32[]{:S(2)}) collective-permute-start(f32[1032,128]{1,0:T(8,128)S(1)} %select_maximum_fusion.1), channel_id=1, source_target_pairs={{0,8},{8,16},{16,24},{1,9},{9,17},{17,25},{2,10},{10,18},{18,26},{... | collective-permute-start | bytes 1585160 | tf_op jit(solution)/shard_map/ppermute | solution.py:120
  6.2 0.1 copy.28
  6.3 0.1 reshape.69
  6.4 1.9 %collective-permute-start.1 = (f32[1032,128]{1,0:T(8,128)S(1)}, f32[1032,128]{1,0:T(8,128)S(1)}, u32[]{:S(2)}, u32[]{:S(2)}) collective-permute-start(f32[1032,128]{1,0:T(8,128)S(1)} %select_maximum_fusion), channel_id=1, source_target_pairs={{8,0},{16,8},{24,16},{9,1},{17,9},{25,17},{10,2},{18,10},{26,18},{... | collective-permute-start | bytes 1585160 | tf_op jit(solution)/shard_map/ppermute | solution.py:121
  8.3 0.1 copy.29
  8.5 0.1 copy.30
  8.5 0.1 reshape.73
  8.7 0.1 reshape.65
  8.8 0.1 copy.31
  8.9 0.1 reshape.70
  9.1 0.5 and_bitcast_fusion.2
  9.6 2.7 %collective-permute-done.low_ref = f32[1032,128]{1,0:T(8,128)S(1)} collective-permute-done((f32[1032,128]{1,0:T(8,128)S(1)}, f32[1032,128]{1,0:T(8,128)S(1)}, u32[]{:S(2)}, u32[]{:S(2)}) %collective-permute-start) | collective-permute-done | bytes 528416 | tf_op jit(solution)/shard_map/ppermute | solution.py:120
  12.4 0.1 convert_element_type.25
  12.4 4.5 %collective-permute-done.1.up_ref = f32[1032,128]{1,0:T(8,128)S(1)} collective-permute-done((f32[1032,128]{1,0:T(8,128)S(1)}, f32[1032,128]{1,0:T(8,128)S(1)}, u32[]{:S(2)}, u32[]{:S(2)}) %collective-permute-start.1) | collective-permute-done | bytes 528416 | tf_op jit(solution)/shard_map/ppermute | solution.py:121
  17.0 0.1 convert_element_type.28
  17.1 0.6 gather_fusion
  17.7 0.1 gather.15
  17.9 0.6 pad_add_fusion.1.idx_ref
  18.5 23.4 %shard_map.55 = (f32[1,9,128,128]{3,2,1,0:T(8,128)}, f32[1,9,128,128]{3,2,1,0:T(8,128)}, f32[1,9,128,128]{3,2,1,0:T(8,128)}) custom-call(s32[416]{0:T(512)} %pad_add_fusion.1.idx_ref, f32[16,8,128,128]{3,2,1,0:T(8,128)} %a_ref.1, f32[1032,128]{1,0:T(8,128)} %copy-done, f32[16,2,128,128]{3,2,1,0:T(8,128)} %mid_ref.1, f32[1032,128]{1,0:T(8,128)} %copy-done.1), custom_call_target="tpu_custom_call" | custom-call | tf_op jit(solution)/shard_map/pallas_call | solution.py:159
  41.9 1.2 %collective-permute-start.2 = (f32[1,9,128,128]{3,2,1,0:T(8,128)}, f32[1,9,128,128]{3,2,1,0:T(8,128)S(1)}, u32[]{:S(2)}, u32[]{:S(2)}) collective-permute-start(f32[1,9,128,128]{3,2,1,0:T(8,128)} %get-tuple-element.9), channel_id=1, source_target_pairs={{0,1},{1,2},{2,3},{3,4},{4,5},{5,6},{6,7},{7,0},{8,9},{9,10},{10,1... | collective-permute-start | bytes 1769480 | tf_op jit(solution)/shard_map/ppermute | solution.py:16
  43.1 3.1 %collective-permute-start.3 = (f32[1,9,128,128]{3,2,1,0:T(8,128)}, f32[1,9,128,128]{3,2,1,0:T(8,128)S(1)}, u32[]{:S(2)}, u32[]{:S(2)}) collective-permute-start(f32[1,9,128,128]{3,2,1,0:T(8,128)} %get-tuple-element.10), channel_id=1, source_target_pairs={{0,7},{1,0},{2,1},{3,2},{4,3},{5,4},{6,5},{7,6},{8,15},{9,8},{10,9... | collective-permute-start | bytes 1769480 | tf_op jit(solution)/shard_map/ppermute | solution.py:16
  46.3 1.7 %gather_fusion.1 = f32[15,128,128]{2,1,0:T(8,128)S(1)} fusion(f32[1,9,128,128]{3,2,1,0:T(8,128)} %get-tuple-element.8, s32[15]{0:T(128)S(1)} %or_bitcast_fusion.2), kind=kCustom, calls=%fused_computation.1 | custom fusion | bytes 1966200 | tf_op jit(solution)/shard_map/gather | solution.py:195
  47.9 15.0 %collective-permute-done.2 = f32[1,9,128,128]{3,2,1,0:T(8,128)S(1)} collective-permute-done((f32[1,9,128,128]{3,2,1,0:T(8,128)}, f32[1,9,128,128]{3,2,1,0:T(8,128)S(1)}, u32[]{:S(2)}, u32[]{:S(2)}) %collective-permute-start.2) | collective-permute-done | bytes 589856 | tf_op jit(solution)/shard_map/ppermute | solution.py:16
  63.0 0.6 gather_fusion.2
  63.6 0.8 %fusion.1 = f32[1,15,128,128]{3,2,1,0:T(8,128)S(1)} fusion(f32[15,128,128]{2,1,0:T(8,128)S(1)} %gather_fusion.2, f32[15,128,128]{2,1,0:T(8,128)S(1)} %gather_fusion.1, pred[15]{0:T(512)(128)(4,1)} %get-tuple-element.24, pred[15]{0:T(512)(128)(4,1)S(1)} %get-tuple-element.23), kind=kLoop, calls=%fused_computation.7 | loop fusion | flops 737280 | bytes 2949150 | tf_op jit(solution)/shard_map/add | solution.py:198
  64.4 0.7 %collective-permute-done.3 = f32[1,9,128,128]{3,2,1,0:T(8,128)S(1)} collective-permute-done((f32[1,9,128,128]{3,2,1,0:T(8,128)}, f32[1,9,128,128]{3,2,1,0:T(8,128)S(1)}, u32[]{:S(2)}, u32[]{:S(2)}) %collective-permute-start.3) | collective-permute-done | bytes 589856 | tf_op jit(solution)/shard_map/ppermute | solution.py:16
  65.1 0.6 gather_fusion.3
  65.7 1.1 %fusion = f32[1,15,128,128]{3,2,1,0:T(8,128)} fusion(f32[1,15,128,128]{3,2,1,0:T(8,128)S(1)} %fusion.1, f32[15,128,128]{2,1,0:T(8,128)S(1)} %gather_fusion.3, pred[15]{0:T(512)(128)(4,1)S(1)} %get-tuple-element.11), kind=kLoop, calls=%fused_computation.5 | loop fusion | flops 491520 | bytes 2949135 | tf_op jit(solution)/shard_map/add | solution.py:199
  (29 shorter events, 0.4 us)
Async XLA Ops:
  0.0 1.3 %copy-start.2 = (s32[16,2]{0,1:T(2,128)S(1)}, s32[16,2]{0,1:T(2,128)}, u32[]{:S(2)}) copy-start(s32[16,2]{0,1:T(2,128)} %param.8) | copy-start | bytes 388
  0.0 8.4 %copy-start.3 = (s32[16,8]{0,1:T(8,128)S(1)}, s32[16,8]{0,1:T(8,128)}, u32[]{:S(2)}) copy-start(s32[16,8]{0,1:T(8,128)} %param.6) | copy-start | bytes 1540
  0.0 9.0 %copy-start.4 = (s32[1,15]{1,0:T(1,128)S(1)}, s32[1,15]{1,0:T(1,128)}, u32[]{:S(2)}) copy-start(s32[1,15]{1,0:T(1,128)} %param.9) | copy-start | bytes 184
  1.6 10.7 %collective-permute-start = (f32[1032,128]{1,0:T(8,128)S(1)}, f32[1032,128]{1,0:T(8,128)S(1)}, u32[]{:S(2)}, u32[]{:S(2)}) collective-permute-start(f32[1032,128]{1,0:T(8,128)S(1)} %select_maximum_fusion.1), channel_id=1, source_target_pairs={{0,8},{8,16},{16,24},{1,9},{9,17},{17,25},{2,10},{10,18},{18,26},{... | collective-permute-start | bytes 1585160 | tf_op jit(solution)/shard_map/ppermute | solution.py:120
  6.4 10.5 %collective-permute-start.1 = (f32[1032,128]{1,0:T(8,128)S(1)}, f32[1032,128]{1,0:T(8,128)S(1)}, u32[]{:S(2)}, u32[]{:S(2)}) collective-permute-start(f32[1032,128]{1,0:T(8,128)S(1)} %select_maximum_fusion), channel_id=1, source_target_pairs={{8,0},{16,8},{24,16},{9,1},{17,9},{25,17},{10,2},{18,10},{26,18},{... | collective-permute-start | bytes 1585160 | tf_op jit(solution)/shard_map/ppermute | solution.py:121
  12.3 6.1 %copy-start = (f32[1032,128]{1,0:T(8,128)}, f32[1032,128]{1,0:T(8,128)S(1)}, u32[]{:S(2)}) copy-start(f32[1032,128]{1,0:T(8,128)S(1)} %collective-permute-done.low_ref) | copy-start | bytes 1585156
  16.9 1.5 %copy-start.1 = (f32[1032,128]{1,0:T(8,128)}, f32[1032,128]{1,0:T(8,128)S(1)}, u32[]{:S(2)}) copy-start(f32[1032,128]{1,0:T(8,128)S(1)} %collective-permute-done.1.up_ref) | copy-start | bytes 1585156
  41.9 21.1 %collective-permute-start.2 = (f32[1,9,128,128]{3,2,1,0:T(8,128)}, f32[1,9,128,128]{3,2,1,0:T(8,128)S(1)}, u32[]{:S(2)}, u32[]{:S(2)}) collective-permute-start(f32[1,9,128,128]{3,2,1,0:T(8,128)} %get-tuple-element.9), channel_id=1, source_target_pairs={{0,1},{1,2},{2,3},{3,4},{4,5},{5,6},{6,7},{7,0},{8,9},{9,10},{10,1... | collective-permute-start | bytes 1769480 | tf_op jit(solution)/shard_map/ppermute | solution.py:16
  43.1 22.0 %collective-permute-start.3 = (f32[1,9,128,128]{3,2,1,0:T(8,128)}, f32[1,9,128,128]{3,2,1,0:T(8,128)S(1)}, u32[]{:S(2)}, u32[]{:S(2)}) collective-permute-start(f32[1,9,128,128]{3,2,1,0:T(8,128)} %get-tuple-element.10), channel_id=1, source_target_pairs={{0,7},{1,0},{2,1},{3,2},{4,3},{5,4},{6,5},{7,6},{8,15},{9,8},{10,9... | collective-permute-start | bytes 1769480 | tf_op jit(solution)/shard_map/ppermute | solution.py:16

commit v15 on v14

--- a/solution.py
+++ b/solution.py
@@ -149,7 +149,7 @@
     relative = jnp.remainder(targets // blocks - t + 1, tiles)
     owner = jnp.clip(relative * blocks + targets % blocks, 0, 3 * blocks - 1)
 
-    per_step = next(d for d in (4, 2, 1) if rows % d == 0)
+    per_step = next(d for d in (2, 1) if rows % d == 0)
     kernel = functools.partial(triple_kernel, coupling_slots, interp_slots, blocks, region)
     part = jax.ShapeDtypeStruct((blocks, region, bs, bs), jnp.float32)
     part_spec = pl.BlockSpec((blocks, region, bs, bs), lambda g, *_: (0, 0, 0, 0))

time: 67.1 us -> 66.9 us (level)
  no operation moved by 1% of the time
where the time goes in v15:
time: 66.9 us; the launch traced here: 66.7 us
  Pallas kernels  23.3 us (35%)
  waiting for transfers between devices  23 us (34%)
  starting transfers between devices  10.8 us (16%)
  local copies, waits for them, and re-layouts  6.14 us (9%)
  other arithmetic  3.35 us (5%)
    pallas_call x1, Pallas kernels, shards(): pl.pallas_call(kernel, out_shape=(part, part, part), grid_spec=pltpu.Pref...  23.3 us
    ppermute x2, waiting for transfers between devices, passed_along(): return lax.ppermute(value, axis, pairs)  15.8 us
    ppermute x1, starting transfers between devices, shards(): lax.ppermute(halo(rows - RIM), 'slab', [(i, i + 1) for i in range(slabs -...  4.54 us
    ppermute x1, waiting for transfers between devices, shards(): up = lax.ppermute(halo(0), 'slab', [(i + 1, i) for i in range(slabs - 1)])  4.51 us
    ppermute x2, starting transfers between devices, passed_along(): return lax.ppermute(value, axis, pairs)  4.31 us
    gather x3, local copies, waits for them, and re-layouts, pick(): tiles_picked = part[r_idx, idx]  2.9 us
    ppermute x1, waiting for transfers between devices, shards(): lax.ppermute(halo(rows - RIM), 'slab', [(i, i + 1) for i in range(slabs -...  2.72 us
    ppermute x1, starting transfers between devices, shards(): up = lax.ppermute(halo(0), 'slab', [(i + 1, i) for i in range(slabs - 1)])  1.92 us
  transfers between devices with their start and end apart: 4, of which 4 were waited for; matrix products, arithmetic and copies ran while one was open for 7% of the time, Pallas kernels for 0%

profile of v15, /device:TPU:1, one launch (start us, length us, event | category | flops | bytes accessed | tf_op | source)
XLA Modules:
  0.0 66.7 jit_solution(6119957804717199050)
XLA Ops:
  0.0 1.3 %fusion.19 = (f32[4,2,128,128]{3,2,1,0:T(8,128)S(1)}, f32[4,2,128,128]{3,2,1,0:T(8,128)S(1)}) fusion(f32[16,2,128,128]{3,2,1,0:T(8,128)} %mid_ref.1), kind=kLoop, calls=%fused_computation.71 | loop fusion | bytes 2097152 | tf_op jit(solution)/shard_map/slice | solution.py:117
  1.3 0.1 slice_convert_fusion.1
  1.4 0.1 copy.27
  1.5 0.1 reshape.67
  1.6 4.5 %collective-permute-start = (f32[1032,128]{1,0:T(8,128)S(1)}, f32[1032,128]{1,0:T(8,128)S(1)}, u32[]{:S(2)}, u32[]{:S(2)}) collective-permute-start(f32[1032,128]{1,0:T(8,128)S(1)} %select_maximum_fusion.1), channel_id=1, source_target_pairs={{0,8},{8,16},{16,24},{1,9},{9,17},{17,25},{2,10},{10,18},{18,26},{... | collective-permute-start | bytes 1585160 | tf_op jit(solution)/shard_map/ppermute | solution.py:120
  6.2 0.1 copy.28
  6.3 0.1 reshape.69
  6.4 1.9 %collective-permute-start.1 = (f32[1032,128]{1,0:T(8,128)S(1)}, f32[1032,128]{1,0:T(8,128)S(1)}, u32[]{:S(2)}, u32[]{:S(2)}) collective-permute-start(f32[1032,128]{1,0:T(8,128)S(1)} %select_maximum_fusion), channel_id=1, source_target_pairs={{8,0},{16,8},{24,16},{9,1},{17,9},{25,17},{10,2},{18,10},{26,18},{... | collective-permute-start | bytes 1585160 | tf_op jit(solution)/shard_map/ppermute | solution.py:121
  8.3 0.1 copy.29
  8.5 0.1 copy.30
  8.5 0.1 reshape.73
  8.7 0.1 reshape.65
  8.8 0.1 copy.31
  8.9 0.1 reshape.70
  9.1 0.5 and_bitcast_fusion.2
  9.6 2.7 %collective-permute-done.low_ref = f32[1032,128]{1,0:T(8,128)S(1)} collective-permute-done((f32[1032,128]{1,0:T(8,128)S(1)}, f32[1032,128]{1,0:T(8,128)S(1)}, u32[]{:S(2)}, u32[]{:S(2)}) %collective-permute-start) | collective-permute-done | bytes 528416 | tf_op jit(solution)/shard_map/ppermute | solution.py:120
  12.4 0.1 convert_element_type.25
  12.4 4.5 %collective-permute-done.1.up_ref = f32[1032,128]{1,0:T(8,128)S(1)} collective-permute-done((f32[1032,128]{1,0:T(8,128)S(1)}, f32[1032,128]{1,0:T(8,128)S(1)}, u32[]{:S(2)}, u32[]{:S(2)}) %collective-permute-start.1) | collective-permute-done | bytes 528416 | tf_op jit(solution)/shard_map/ppermute | solution.py:121
  17.0 0.1 convert_element_type.28
  17.1 0.6 gather_fusion
  17.7 0.1 gather.15
  17.9 0.6 pad_add_fusion.1.idx_ref
  18.5 23.3 %shard_map.55 = (f32[1,9,128,128]{3,2,1,0:T(8,128)}, f32[1,9,128,128]{3,2,1,0:T(8,128)}, f32[1,9,128,128]{3,2,1,0:T(8,128)}) custom-call(s32[416]{0:T(512)} %pad_add_fusion.1.idx_ref, f32[16,8,128,128]{3,2,1,0:T(8,128)} %a_ref.1, f32[1032,128]{1,0:T(8,128)} %copy-done, f32[16,2,128,128]{3,2,1,0:T(8,128)} %mid_ref.1, f32[1032,128]{1,0:T(8,128)} %copy-done.1), custom_call_target="tpu_custom_call" | custom-call | tf_op jit(solution)/shard_map/pallas_call | solution.py:159
  41.7 1.2 %collective-permute-start.2 = (f32[1,9,128,128]{3,2,1,0:T(8,128)}, f32[1,9,128,128]{3,2,1,0:T(8,128)S(1)}, u32[]{:S(2)}, u32[]{:S(2)}) collective-permute-start(f32[1,9,128,128]{3,2,1,0:T(8,128)} %get-tuple-element.9), channel_id=1, source_target_pairs={{0,1},{1,2},{2,3},{3,4},{4,5},{5,6},{6,7},{7,0},{8,9},{9,10},{10,1... | collective-permute-start | bytes 1769480 | tf_op jit(solution)/shard_map/ppermute | solution.py:16
  43.0 3.1 %collective-permute-start.3 = (f32[1,9,128,128]{3,2,1,0:T(8,128)}, f32[1,9,128,128]{3,2,1,0:T(8,128)S(1)}, u32[]{:S(2)}, u32[]{:S(2)}) collective-permute-start(f32[1,9,128,128]{3,2,1,0:T(8,128)} %get-tuple-element.10), channel_id=1, source_target_pairs={{0,7},{1,0},{2,1},{3,2},{4,3},{5,4},{6,5},{7,6},{8,15},{9,8},{10,9... | collective-permute-start | bytes 1769480 | tf_op jit(solution)/shard_map/ppermute | solution.py:16
  46.1 1.7 %gather_fusion.1 = f32[15,128,128]{2,1,0:T(8,128)S(1)} fusion(f32[1,9,128,128]{3,2,1,0:T(8,128)} %get-tuple-element.8, s32[15]{0:T(128)S(1)} %or_bitcast_fusion.2), kind=kCustom, calls=%fused_computation.1 | custom fusion | bytes 1966200 | tf_op jit(solution)/shard_map/gather | solution.py:195
  47.8 15.0 %collective-permute-done.2 = f32[1,9,128,128]{3,2,1,0:T(8,128)S(1)} collective-permute-done((f32[1,9,128,128]{3,2,1,0:T(8,128)}, f32[1,9,128,128]{3,2,1,0:T(8,128)S(1)}, u32[]{:S(2)}, u32[]{:S(2)}) %collective-permute-start.2) | collective-permute-done | bytes 589856 | tf_op jit(solution)/shard_map/ppermute | solution.py:16
  62.8 0.6 gather_fusion.2
  63.4 0.8 %fusion.1 = f32[1,15,128,128]{3,2,1,0:T(8,128)S(1)} fusion(f32[15,128,128]{2,1,0:T(8,128)S(1)} %gather_fusion.2, f32[15,128,128]{2,1,0:T(8,128)S(1)} %gather_fusion.1, pred[15]{0:T(512)(128)(4,1)} %get-tuple-element.24, pred[15]{0:T(512)(128)(4,1)S(1)} %get-tuple-element.23), kind=kLoop, calls=%fused_computation.7 | loop fusion | flops 737280 | bytes 2949150 | tf_op jit(solution)/shard_map/add | solution.py:198
  64.2 0.7 %collective-permute-done.3 = f32[1,9,128,128]{3,2,1,0:T(8,128)S(1)} collective-permute-done((f32[1,9,128,128]{3,2,1,0:T(8,128)}, f32[1,9,128,128]{3,2,1,0:T(8,128)S(1)}, u32[]{:S(2)}, u32[]{:S(2)}) %collective-permute-start.3) | collective-permute-done | bytes 589856 | tf_op jit(solution)/shard_map/ppermute | solution.py:16
  64.9 0.6 gather_fusion.3
  65.6 1.1 %fusion = f32[1,15,128,128]{3,2,1,0:T(8,128)} fusion(f32[1,15,128,128]{3,2,1,0:T(8,128)S(1)} %fusion.1, f32[15,128,128]{2,1,0:T(8,128)S(1)} %gather_fusion.3, pred[15]{0:T(512)(128)(4,1)S(1)} %get-tuple-element.11), kind=kLoop, calls=%fused_computation.5 | loop fusion | flops 491520 | bytes 2949135 | tf_op jit(solution)/shard_map/add | solution.py:199
  (29 shorter events, 0.4 us)
Async XLA Ops:
  0.0 1.3 %copy-start.2 = (s32[16,2]{0,1:T(2,128)S(1)}, s32[16,2]{0,1:T(2,128)}, u32[]{:S(2)}) copy-start(s32[16,2]{0,1:T(2,128)} %param.8) | copy-start | bytes 388
  0.0 8.4 %copy-start.3 = (s32[16,8]{0,1:T(8,128)S(1)}, s32[16,8]{0,1:T(8,128)}, u32[]{:S(2)}) copy-start(s32[16,8]{0,1:T(8,128)} %param.6) | copy-start | bytes 1540
  0.0 9.0 %copy-start.4 = (s32[1,15]{1,0:T(1,128)S(1)}, s32[1,15]{1,0:T(1,128)}, u32[]{:S(2)}) copy-start(s32[1,15]{1,0:T(1,128)} %param.9) | copy-start | bytes 184
  1.6 10.7 %collective-permute-start = (f32[1032,128]{1,0:T(8,128)S(1)}, f32[1032,128]{1,0:T(8,128)S(1)}, u32[]{:S(2)}, u32[]{:S(2)}) collective-permute-start(f32[1032,128]{1,0:T(8,128)S(1)} %select_maximum_fusion.1), channel_id=1, source_target_pairs={{0,8},{8,16},{16,24},{1,9},{9,17},{17,25},{2,10},{10,18},{18,26},{... | collective-permute-start | bytes 1585160 | tf_op jit(solution)/shard_map/ppermute | solution.py:120
  6.4 10.5 %collective-permute-start.1 = (f32[1032,128]{1,0:T(8,128)S(1)}, f32[1032,128]{1,0:T(8,128)S(1)}, u32[]{:S(2)}, u32[]{:S(2)}) collective-permute-start(f32[1032,128]{1,0:T(8,128)S(1)} %select_maximum_fusion), channel_id=1, source_target_pairs={{8,0},{16,8},{24,16},{9,1},{17,9},{25,17},{10,2},{18,10},{26,18},{... | collective-permute-start | bytes 1585160 | tf_op jit(solution)/shard_map/ppermute | solution.py:121
  12.3 6.1 %copy-start = (f32[1032,128]{1,0:T(8,128)}, f32[1032,128]{1,0:T(8,128)S(1)}, u32[]{:S(2)}) copy-start(f32[1032,128]{1,0:T(8,128)S(1)} %collective-permute-done.low_ref) | copy-start | bytes 1585156
  16.9 1.5 %copy-start.1 = (f32[1032,128]{1,0:T(8,128)}, f32[1032,128]{1,0:T(8,128)S(1)}, u32[]{:S(2)}) copy-start(f32[1032,128]{1,0:T(8,128)S(1)} %collective-permute-done.1.up_ref) | copy-start | bytes 1585156
  41.7 21.1 %collective-permute-start.2 = (f32[1,9,128,128]{3,2,1,0:T(8,128)}, f32[1,9,128,128]{3,2,1,0:T(8,128)S(1)}, u32[]{:S(2)}, u32[]{:S(2)}) collective-permute-start(f32[1,9,128,128]{3,2,1,0:T(8,128)} %get-tuple-element.9), channel_id=1, source_target_pairs={{0,1},{1,2},{2,3},{3,4},{4,5},{5,6},{6,7},{7,0},{8,9},{9,10},{10,1... | collective-permute-start | bytes 1769480 | tf_op jit(solution)/shard_map/ppermute | solution.py:16
  43.0 22.0 %collective-permute-start.3 = (f32[1,9,128,128]{3,2,1,0:T(8,128)}, f32[1,9,128,128]{3,2,1,0:T(8,128)S(1)}, u32[]{:S(2)}, u32[]{:S(2)}) collective-permute-start(f32[1,9,128,128]{3,2,1,0:T(8,128)} %get-tuple-element.10), channel_id=1, source_target_pairs={{0,7},{1,0},{2,1},{3,2},{4,3},{5,4},{6,5},{7,6},{8,15},{9,8},{10,9... | collective-permute-start | bytes 1769480 | tf_op jit(solution)/shard_map/ppermute | solution.py:16

commit v16 on v15

--- a/solution.py
+++ b/solution.py
@@ -34,7 +34,7 @@
 
 def triple_kernel(
     coupling_slots, interp_slots, blocks, region,
-    idx_ref, a_ref, low_ref, mid_ref, up_ref, lo_ref, own_ref, hi_ref,
+    idx_ref, rowslot_ref, a_ref, low_ref, mid_ref, up_ref, lo_ref, own_ref, hi_ref,
     y_ref, acc_ref, p3_ref,
 ):
     g = pl.program_id(0)
@@ -43,7 +43,7 @@
     rows = steps * per_step
     bs = a_ref.shape[2]
     slot_base = rows * coupling_slots
-    owner_base = slot_base + rows * coupling_slots * interp_slots
+    owner_base = slot_base
 
     @pl.when(g == 0)
     def _():
@@ -77,7 +77,7 @@
             row = idx_ref[gi * coupling_slots + a]
             prod = jnp.dot(stack_lhs(a_ref[i, a]), p3_ref[row], preferred_element_type=jnp.float32)
             for p in range(interp_slots):
-                slot = idx_ref[slot_base + (gi * coupling_slots + a) * interp_slots + p]
+                slot = rowslot_ref[row * interp_slots + p]
                 y_ref[slot] += prod[:, p * bs : (p + 1) * bs]
         pt = stack_lhs(jnp.concatenate([mid_ref[gi, q].T for q in range(interp_slots)], axis=0))
         owners = [idx_ref[owner_base + gi * interp_slots + q] for q in range(interp_slots)]
@@ -121,9 +121,9 @@
     up = lax.ppermute(halo(0), "slab", [(i + 1, i) for i in range(slabs - 1)])
 
     def halo_keys(block):
-        return block[key_count * bs, :key_count].astype(jnp.int32).reshape(RIM, interp_slots)
-
-    ext_keys = jnp.concatenate([halo_keys(low), p_cols, halo_keys(up)], axis=0)
+        return block[key_count * bs, :key_count].astype(jnp.int32)
+
+    ext_keys = jnp.concatenate([halo_keys(low), p_cols.reshape(-1), halo_keys(up)])
 
     own_base = device * rows
     lower_base = (device - tiles) * rows + rows - RIM
@@ -138,12 +138,12 @@
         ),
     )
     local_index = jnp.clip(local_index, 0, ext_rows - 1)
-    keys = ext_keys[local_index]
+    keys = ext_keys
     k_slab = keys // (tiles * blocks)
     k_tile = (keys // blocks) % tiles
     k_dt = (k_tile - t + 1) % tiles - 1
     slot = ((k_slab - s + 1) * 3 + (k_dt + 1)) * blocks + keys % blocks
-    slot = jnp.clip(slot, 0, region - 1)
+    slot = jnp.clip(slot, 0, region - 1).astype(jnp.int32)
 
     targets = p_cols - s * tiles * blocks
     relative = jnp.remainder(targets // blocks - t + 1, tiles)
@@ -154,13 +154,13 @@
     part = jax.ShapeDtypeStruct((blocks, region, bs, bs), jnp.float32)
     part_spec = pl.BlockSpec((blocks, region, bs, bs), lambda g, *_: (0, 0, 0, 0))
     table = jnp.concatenate(
-        [local_index.reshape(-1), slot.reshape(-1), owner.reshape(-1)]
+        [local_index.reshape(-1), owner.reshape(-1)]
     ).astype(jnp.int32)
     to_lower, own_part, to_upper = pl.pallas_call(
         kernel,
         out_shape=(part, part, part),
         grid_spec=pltpu.PrefetchScalarGridSpec(
-            num_scalar_prefetch=1,
+            num_scalar_prefetch=2,
             grid=(rows // per_step,),
             in_specs=[
                 pl.BlockSpec((per_step, coupling_slots, bs, bs), lambda g, *_: (g, 0, 0, 0)),
@@ -176,7 +176,7 @@
             ],
         ),
         compiler_params=pltpu.CompilerParams(dimension_semantics=("arbitrary",)),
-    )(table, a_tiles, low, p_tiles, up)
+    )(table, slot, a_tiles, low, p_tiles, up)
 
     from_lower = passed_along(to_upper, "tile", 1)
     from_upper = passed_along(to_lower, "tile", -1)

time: 66.9 us -> 66.2 us (0.990)
  local copies, waits for them, and re-layouts: 6.14 us -> 5.18 us
  waiting for transfers between devices: 23 us -> 22.1 us
    ppermute x2, waiting for transfers between devices: 15.8 us -> 17.7 us  [passed_along(): return lax.ppermute(value, axis, pairs)]
    ppermute x1, waiting for transfers between devices: 4.51 us -> 3.01 us  [shards(): up = lax.ppermute(halo(0), 'slab', [(i + 1, i) for i in range(slabs - 1)])]
    ppermute x1, waiting for transfers between devices: 2.72 us -> 1.4 us  [shards(): lax.ppermute(halo(rows - RIM), 'slab', [(i, i + 1) for i in range(slabs -...]
    gather x2 -> x0, local copies, waits for them, and re-layouts: 0.78 us -> none  [shards(): keys = ext_keys[local_index]]
    min x1 -> x2, other arithmetic: 0.02 us -> 0.72 us  [the longest x1 0.72 us: shards(): slot = jnp.clip(slot, 0, region - 1).astype(jnp.int32)]
  transfers between devices with their start and end apart: 4 -> 4, of which waited for: 4 -> 4; matrix products, arithmetic and copies ran while one was open for 7% -> 8% of each run, Pallas kernels for 0% -> 0%
where the time goes in v16:
time: 66.2 us; the launch traced here: 66 us
  Pallas kernels  23.8 us (36%)
  waiting for transfers between devices  22.1 us (33%)
  starting transfers between devices  10.8 us (16%)
  local copies, waits for them, and re-layouts  5.18 us (8%)
  other arithmetic  3.97 us (6%)
    pallas_call x1, Pallas kernels, shards(): pl.pallas_call(kernel, out_shape=(part, part, part), grid_spec=pltpu.Pref...  23.8 us
    ppermute x2, waiting for transfers between devices, passed_along(): return lax.ppermute(value, axis, pairs)  17.7 us
    ppermute x1, starting transfers between devices, shards(): lax.ppermute(halo(rows - RIM), 'slab', [(i, i + 1) for i in range(slabs -...  4.49 us
    ppermute x2, starting transfers between devices, passed_along(): return lax.ppermute(value, axis, pairs)  4.32 us
    ppermute x1, waiting for transfers between devices, shards(): up = lax.ppermute(halo(0), 'slab', [(i + 1, i) for i in range(slabs - 1)])  3.01 us
    gather x3, local copies, waits for them, and re-layouts, pick(): tiles_picked = part[r_idx, idx]  2.9 us
    ppermute x1, starting transfers between devices, shards(): up = lax.ppermute(halo(0), 'slab', [(i + 1, i) for i in range(slabs - 1)])  1.97 us
    ppermute x1, waiting for transfers between devices, shards(): lax.ppermute(halo(rows - RIM), 'slab', [(i, i + 1) for i in range(slabs -...  1.4 us
  transfers between devices with their start and end apart: 4, of which 4 were waited for; matrix products, arithmetic and copies ran while one was open for 8% of the time, Pallas kernels for 0%

profile of v16, /device:TPU:1, one launch (start us, length us, event | category | flops | bytes accessed | tf_op | source)
XLA Modules:
  0.0 66.0 jit_solution(13129336733672729043)
XLA Ops:
  0.0 1.3 %fusion.20 = (f32[4,2,128,128]{3,2,1,0:T(8,128)S(1)}, f32[4,2,128,128]{3,2,1,0:T(8,128)S(1)}) fusion(f32[16,2,128,128]{3,2,1,0:T(8,128)} %mid_ref.1), kind=kLoop, calls=%fused_computation.69 | loop fusion | bytes 2097152 | tf_op jit(solution)/shard_map/slice | solution.py:117
  1.3 0.1 slice_convert_fusion.1
  1.4 0.1 copy.15
  1.5 0.1 reshape.68
  1.6 2.0 %collective-permute-start.1 = (f32[1032,128]{1,0:T(8,128)S(1)}, f32[1032,128]{1,0:T(8,128)S(1)}, u32[]{:S(2)}, u32[]{:S(2)}) collective-permute-start(f32[1032,128]{1,0:T(8,128)S(1)} %select_maximum_fusion), channel_id=1, source_target_pairs={{8,0},{16,8},{24,16},{9,1},{17,9},{25,17},{10,2},{18,10},{26,18},{... | collective-permute-start | bytes 1585160 | tf_op jit(solution)/shard_map/ppermute | solution.py:121
  3.6 0.1 copy.13
  3.7 0.1 reshape.65
  3.8 4.5 %collective-permute-start = (f32[1032,128]{1,0:T(8,128)S(1)}, f32[1032,128]{1,0:T(8,128)S(1)}, u32[]{:S(2)}, u32[]{:S(2)}) collective-permute-start(f32[1032,128]{1,0:T(8,128)S(1)} %select_maximum_fusion.1), channel_id=1, source_target_pairs={{0,8},{8,16},{16,24},{1,9},{9,17},{17,25},{2,10},{10,18},{18,26},{... | collective-permute-start | bytes 1585160 | tf_op jit(solution)/shard_map/ppermute | solution.py:120
  8.4 0.1 copy.14
  8.4 0.0 copy-done.3
  8.5 0.1 copy.11
  8.5 0.1 reshape.62
  8.6 0.1 copy.12
  8.7 0.1 reshape.63
  8.8 0.1 reshape.66
  8.9 0.0 copy-done.4
  9.0 0.5 and_bitcast_fusion.2
  9.5 0.5 pad_add_fusion.idx_ref
  10.1 3.0 %collective-permute-done.1.up_ref = f32[1032,128]{1,0:T(8,128)S(1)} collective-permute-done((f32[1032,128]{1,0:T(8,128)S(1)}, f32[1032,128]{1,0:T(8,128)S(1)}, u32[]{:S(2)}, u32[]{:S(2)}) %collective-permute-start.1) | collective-permute-done | bytes 528416 | tf_op jit(solution)/shard_map/ppermute | solution.py:121
  13.1 1.4 %collective-permute-done.low_ref = f32[1032,128]{1,0:T(8,128)S(1)} collective-permute-done((f32[1032,128]{1,0:T(8,128)S(1)}, f32[1032,128]{1,0:T(8,128)S(1)}, u32[]{:S(2)}, u32[]{:S(2)}) %collective-permute-start) | collective-permute-done | bytes 528416 | tf_op jit(solution)/shard_map/ppermute | solution.py:120
  14.5 0.7 %fusion.18.rowslot_ref = s32[48]{0:T(128)} fusion(s32[8]{0:T(128)S(1)} %fusion.16, s32[32]{0:T(128)S(1)} %reshape.66, s32[8]{0:T(128)S(1)} %fusion.17, s32[]{:T(128)S(6)} %axis_index.22, s32[]{:T(128)S(6)} %axis_index.25), kind=kLoop, calls=%fused_computation.68 | loop fusion | flops 1872 | bytes 392 | tf_op jit(solution)/shard_map/jit(clip)/min | solution.py:146
  15.2 0.1 copy-done.1
  15.3 23.8 %shard_map.55 = (f32[1,9,128,128]{3,2,1,0:T(8,128)}, f32[1,9,128,128]{3,2,1,0:T(8,128)}, f32[1,9,128,128]{3,2,1,0:T(8,128)}) custom-call(s32[160]{0:T(256)} %pad_add_fusion.idx_ref, s32[48]{0:T(128)} %fusion.18.rowslot_ref, f32[16,8,128,128]{3,2,1,0:T(8,128)} %a_ref.1, f32[1032,128]{1,0:T(8,128)} %copy-done.1, f32[16,2,128,128]{3,2,1,0:T(8,128)} %mid_ref.1, ...), custom_call_target="tpu_custom_call" | custom-call | tf_op jit(solution)/shard_map/pallas_call | solution.py:159
  39.1 1.2 %collective-permute-start.2 = (f32[1,9,128,128]{3,2,1,0:T(8,128)}, f32[1,9,128,128]{3,2,1,0:T(8,128)S(1)}, u32[]{:S(2)}, u32[]{:S(2)}) collective-permute-start(f32[1,9,128,128]{3,2,1,0:T(8,128)} %get-tuple-element.9), channel_id=1, source_target_pairs={{0,1},{1,2},{2,3},{3,4},{4,5},{5,6},{6,7},{7,0},{8,9},{9,10},{10,1... | collective-permute-start | bytes 1769480 | tf_op jit(solution)/shard_map/ppermute | solution.py:16
  40.4 3.1 %collective-permute-start.3 = (f32[1,9,128,128]{3,2,1,0:T(8,128)}, f32[1,9,128,128]{3,2,1,0:T(8,128)S(1)}, u32[]{:S(2)}, u32[]{:S(2)}) collective-permute-start(f32[1,9,128,128]{3,2,1,0:T(8,128)} %get-tuple-element.10), channel_id=1, source_target_pairs={{0,7},{1,0},{2,1},{3,2},{4,3},{5,4},{6,5},{7,6},{8,15},{9,8},{10,9... | collective-permute-start | bytes 1769480 | tf_op jit(solution)/shard_map/ppermute | solution.py:16
  43.5 1.7 %gather_fusion = f32[15,128,128]{2,1,0:T(8,128)S(1)} fusion(f32[1,9,128,128]{3,2,1,0:T(8,128)} %get-tuple-element.8, s32[15]{0:T(128)S(1)} %or_bitcast_fusion.2), kind=kCustom, calls=%fused_computation | custom fusion | bytes 1966200 | tf_op jit(solution)/shard_map/gather | solution.py:195
  45.2 16.9 %collective-permute-done.2 = f32[1,9,128,128]{3,2,1,0:T(8,128)S(1)} collective-permute-done((f32[1,9,128,128]{3,2,1,0:T(8,128)}, f32[1,9,128,128]{3,2,1,0:T(8,128)S(1)}, u32[]{:S(2)}, u32[]{:S(2)}) %collective-permute-start.2) | collective-permute-done | bytes 589856 | tf_op jit(solution)/shard_map/ppermute | solution.py:16
  62.1 0.6 gather_fusion.1
  62.7 0.8 %fusion.1 = f32[1,15,128,128]{3,2,1,0:T(8,128)S(1)} fusion(f32[15,128,128]{2,1,0:T(8,128)S(1)} %gather_fusion.1, f32[15,128,128]{2,1,0:T(8,128)S(1)} %gather_fusion, pred[15]{0:T(512)(128)(4,1)} %get-tuple-element.22, pred[15]{0:T(512)(128)(4,1)S(1)} %get-tuple-element.21), kind=kLoop, calls=%fused_computation.6 | loop fusion | flops 737280 | bytes 2949150 | tf_op jit(solution)/shard_map/add | solution.py:198
  63.5 0.7 %collective-permute-done.3 = f32[1,9,128,128]{3,2,1,0:T(8,128)S(1)} collective-permute-done((f32[1,9,128,128]{3,2,1,0:T(8,128)}, f32[1,9,128,128]{3,2,1,0:T(8,128)S(1)}, u32[]{:S(2)}, u32[]{:S(2)}) %collective-permute-start.3) | collective-permute-done | bytes 589856 | tf_op jit(solution)/shard_map/ppermute | solution.py:16
  64.3 0.6 gather_fusion.2
  64.9 1.1 %fusion = f32[1,15,128,128]{3,2,1,0:T(8,128)} fusion(f32[1,15,128,128]{3,2,1,0:T(8,128)S(1)} %fusion.1, f32[15,128,128]{2,1,0:T(8,128)S(1)} %gather_fusion.2, pred[15]{0:T(512)(128)(4,1)S(1)} %get-tuple-element.11), kind=kLoop, calls=%fused_computation.4 | loop fusion | flops 491520 | bytes 2949135 | tf_op jit(solution)/shard_map/add | solution.py:199
  (22 shorter events, 0.2 us)
Async XLA Ops:
  0.0 1.3 %copy-start.2 = (s32[16,2]{0,1:T(2,128)S(1)}, s32[16,2]{0,1:T(2,128)}, u32[]{:S(2)}) copy-start(s32[16,2]{0,1:T(2,128)} %param.8) | copy-start | bytes 388
  0.0 8.4 %copy-start.3 = (s32[16,8]{0,1:T(8,128)S(1)}, s32[16,8]{0,1:T(8,128)}, u32[]{:S(2)}) copy-start(s32[16,8]{0,1:T(8,128)} %param.6) | copy-start | bytes 1540
  0.0 8.9 %copy-start.4 = (s32[1,15]{1,0:T(1,128)S(1)}, s32[1,15]{1,0:T(1,128)}, u32[]{:S(2)}) copy-start(s32[1,15]{1,0:T(1,128)} %param.9) | copy-start | bytes 184
  1.6 11.4 %collective-permute-start.1 = (f32[1032,128]{1,0:T(8,128)S(1)}, f32[1032,128]{1,0:T(8,128)S(1)}, u32[]{:S(2)}, u32[]{:S(2)}) collective-permute-start(f32[1032,128]{1,0:T(8,128)S(1)} %select_maximum_fusion), channel_id=1, source_target_pairs={{8,0},{16,8},{24,16},{9,1},{17,9},{25,17},{10,2},{18,10},{26,18},{... | collective-permute-start | bytes 1585160 | tf_op jit(solution)/shard_map/ppermute | solution.py:121
  3.8 10.6 %collective-permute-start = (f32[1032,128]{1,0:T(8,128)S(1)}, f32[1032,128]{1,0:T(8,128)S(1)}, u32[]{:S(2)}, u32[]{:S(2)}) collective-permute-start(f32[1032,128]{1,0:T(8,128)S(1)} %select_maximum_fusion.1), channel_id=1, source_target_pairs={{0,8},{8,16},{16,24},{1,9},{9,17},{17,25},{2,10},{10,18},{18,26},{... | collective-permute-start | bytes 1585160 | tf_op jit(solution)/shard_map/ppermute | solution.py:120
  13.1 2.1 %copy-start = (f32[1032,128]{1,0:T(8,128)}, f32[1032,128]{1,0:T(8,128)S(1)}, u32[]{:S(2)}) copy-start(f32[1032,128]{1,0:T(8,128)S(1)} %collective-permute-done.1.up_ref) | copy-start | bytes 1585156
  14.5 0.8 %copy-start.1 = (f32[1032,128]{1,0:T(8,128)}, f32[1032,128]{1,0:T(8,128)S(1)}, u32[]{:S(2)}) copy-start(f32[1032,128]{1,0:T(8,128)S(1)} %collective-permute-done.low_ref) | copy-start | bytes 1585156
  39.1 23.0 %collective-permute-start.2 = (f32[1,9,128,128]{3,2,1,0:T(8,128)}, f32[1,9,128,128]{3,2,1,0:T(8,128)S(1)}, u32[]{:S(2)}, u32[]{:S(2)}) collective-permute-start(f32[1,9,128,128]{3,2,1,0:T(8,128)} %get-tuple-element.9), channel_id=1, source_target_pairs={{0,1},{1,2},{2,3},{3,4},{4,5},{5,6},{6,7},{7,0},{8,9},{9,10},{10,1... | collective-permute-start | bytes 1769480 | tf_op jit(solution)/shard_map/ppermute | solution.py:16
  40.4 23.9 %collective-permute-start.3 = (f32[1,9,128,128]{3,2,1,0:T(8,128)}, f32[1,9,128,128]{3,2,1,0:T(8,128)S(1)}, u32[]{:S(2)}, u32[]{:S(2)}) collective-permute-start(f32[1,9,128,128]{3,2,1,0:T(8,128)} %get-tuple-element.10), channel_id=1, source_target_pairs={{0,7},{1,0},{2,1},{3,2},{4,3},{5,4},{6,5},{7,6},{8,15},{9,8},{10,9... | collective-permute-start | bytes 1769480 | tf_op jit(solution)/shard_map/ppermute | solution.py:16

commit v17 on v16

--- a/solution.py
+++ b/solution.py
@@ -34,7 +34,7 @@
 
 def triple_kernel(
     coupling_slots, interp_slots, blocks, region,
-    idx_ref, rowslot_ref, a_ref, low_ref, mid_ref, up_ref, lo_ref, own_ref, hi_ref,
+    idx_ref, a_ref, low_ref, mid_ref, up_ref, lo_ref, own_ref, hi_ref,
     y_ref, acc_ref, p3_ref,
 ):
     g = pl.program_id(0)
@@ -44,6 +44,7 @@
     bs = a_ref.shape[2]
     slot_base = rows * coupling_slots
     owner_base = slot_base
+    rowslot_base = owner_base + rows * interp_slots
 
     @pl.when(g == 0)
     def _():
@@ -77,7 +78,7 @@
             row = idx_ref[gi * coupling_slots + a]
             prod = jnp.dot(stack_lhs(a_ref[i, a]), p3_ref[row], preferred_element_type=jnp.float32)
             for p in range(interp_slots):
-                slot = rowslot_ref[row * interp_slots + p]
+                slot = idx_ref[rowslot_base + row * interp_slots + p]
                 y_ref[slot] += prod[:, p * bs : (p + 1) * bs]
         pt = stack_lhs(jnp.concatenate([mid_ref[gi, q].T for q in range(interp_slots)], axis=0))
         owners = [idx_ref[owner_base + gi * interp_slots + q] for q in range(interp_slots)]
@@ -154,13 +155,13 @@
     part = jax.ShapeDtypeStruct((blocks, region, bs, bs), jnp.float32)
     part_spec = pl.BlockSpec((blocks, region, bs, bs), lambda g, *_: (0, 0, 0, 0))
     table = jnp.concatenate(
-        [local_index.reshape(-1), owner.reshape(-1)]
+        [local_index.reshape(-1), owner.reshape(-1), slot]
     ).astype(jnp.int32)
     to_lower, own_part, to_upper = pl.pallas_call(
         kernel,
         out_shape=(part, part, part),
         grid_spec=pltpu.PrefetchScalarGridSpec(
-            num_scalar_prefetch=2,
+            num_scalar_prefetch=1,
             grid=(rows // per_step,),
             in_specs=[
                 pl.BlockSpec((per_step, coupling_slots, bs, bs), lambda g, *_: (g, 0, 0, 0)),
@@ -176,7 +177,7 @@
             ],
         ),
         compiler_params=pltpu.CompilerParams(dimension_semantics=("arbitrary",)),
-    )(table, slot, a_tiles, low, p_tiles, up)
+    )(table, a_tiles, low, p_tiles, up)
 
     from_lower = passed_along(to_upper, "tile", 1)
     from_upper = passed_along(to_lower, "tile", -1)

time: 66.2 us -> 65.7 us (level)
  transfers between devices with their start and end apart: 4 -> 4, of which waited for: 4 -> 4; matrix products, arithmetic and copies ran while one was open for 8% -> 7% of each run, Pallas kernels for 0% -> 0%
where the time goes in v17:
time: 65.7 us; the launch traced here: 65.5 us
  Pallas kernels  23.8 us (36%)
  waiting for transfers between devices  22.1 us (34%)
  starting transfers between devices  10.8 us (16%)
  local copies, waits for them, and re-layouts  5.15 us (8%)
  other arithmetic  3.47 us (5%)
    pallas_call x1, Pallas kernels, shards(): pl.pallas_call(kernel, out_shape=(part, part, part), grid_spec=pltpu.Pref...  23.8 us
    ppermute x2, waiting for transfers between devices, passed_along(): return lax.ppermute(value, axis, pairs)  17.2 us
    ppermute x1, starting transfers between devices, shards(): lax.ppermute(halo(rows - RIM), 'slab', [(i, i + 1) for i in range(slabs -...  4.49 us
    ppermute x2, starting transfers between devices, passed_along(): return lax.ppermute(value, axis, pairs)  4.31 us
    ppermute x1, waiting for transfers between devices, shards(): up = lax.ppermute(halo(0), 'slab', [(i + 1, i) for i in range(slabs - 1)])  3.54 us
    gather x3, local copies, waits for them, and re-layouts, pick(): tiles_picked = part[r_idx, idx]  2.9 us
    ppermute x1, starting transfers between devices, shards(): up = lax.ppermute(halo(0), 'slab', [(i + 1, i) for i in range(slabs - 1)])  1.97 us
    ppermute x1, waiting for transfers between devices, shards(): lax.ppermute(halo(rows - RIM), 'slab', [(i, i + 1) for i in range(slabs -...  1.4 us
  transfers between devices with their start and end apart: 4, of which 4 were waited for; matrix products, arithmetic and copies ran while one was open for 7% of the time, Pallas kernels for 0%

profile of v17, /device:TPU:1, one launch (start us, length us, event | category | flops | bytes accessed | tf_op | source)
XLA Modules:
  0.0 65.5 jit_solution(6919349934365824721)
XLA Ops:
  0.0 1.3 %fusion.20 = (f32[4,2,128,128]{3,2,1,0:T(8,128)S(1)}, f32[4,2,128,128]{3,2,1,0:T(8,128)S(1)}) fusion(f32[16,2,128,128]{3,2,1,0:T(8,128)} %mid_ref.1), kind=kLoop, calls=%fused_computation.69 | loop fusion | bytes 2097152 | tf_op jit(solution)/shard_map/slice | solution.py:118
  1.3 0.0 copy-done.2
  1.3 0.1 slice_convert_fusion.1
  1.4 0.1 copy.15
  1.5 0.1 reshape.68
  1.6 2.0 %collective-permute-start.1 = (f32[1032,128]{1,0:T(8,128)S(1)}, f32[1032,128]{1,0:T(8,128)S(1)}, u32[]{:S(2)}, u32[]{:S(2)}) collective-permute-start(f32[1032,128]{1,0:T(8,128)S(1)} %select_maximum_fusion), channel_id=1, source_target_pairs={{8,0},{16,8},{24,16},{9,1},{17,9},{25,17},{10,2},{18,10},{26,18},{... | collective-permute-start | bytes 1585160 | tf_op jit(solution)/shard_map/ppermute | solution.py:122
  3.6 0.1 copy.13
  3.7 0.1 reshape.65
  3.8 4.5 %collective-permute-start = (f32[1032,128]{1,0:T(8,128)S(1)}, f32[1032,128]{1,0:T(8,128)S(1)}, u32[]{:S(2)}, u32[]{:S(2)}) collective-permute-start(f32[1032,128]{1,0:T(8,128)S(1)} %select_maximum_fusion.1), channel_id=1, source_target_pairs={{0,8},{8,16},{16,24},{1,9},{9,17},{17,25},{2,10},{10,18},{18,26},{... | collective-permute-start | bytes 1585160 | tf_op jit(solution)/shard_map/ppermute | solution.py:121
  8.3 0.1 copy.14
  8.4 0.0 copy-done.3
  8.5 0.1 copy.11
  8.5 0.1 reshape.62
  8.6 0.1 reshape.66
  8.7 0.1 copy.12
  8.8 0.1 reshape.63
  9.0 0.5 and_bitcast_fusion.2
  9.5 3.5 %collective-permute-done.1.up_ref = f32[1032,128]{1,0:T(8,128)S(1)} collective-permute-done((f32[1032,128]{1,0:T(8,128)S(1)}, f32[1032,128]{1,0:T(8,128)S(1)}, u32[]{:S(2)}, u32[]{:S(2)}) %collective-permute-start.1) | collective-permute-done | bytes 528416 | tf_op jit(solution)/shard_map/ppermute | solution.py:122
  13.1 1.4 %collective-permute-done.low_ref = f32[1032,128]{1,0:T(8,128)S(1)} collective-permute-done((f32[1032,128]{1,0:T(8,128)S(1)}, f32[1032,128]{1,0:T(8,128)S(1)}, u32[]{:S(2)}, u32[]{:S(2)}) %collective-permute-start) | collective-permute-done | bytes 528416 | tf_op jit(solution)/shard_map/ppermute | solution.py:121
  14.5 0.1 fusion.18
  14.6 0.7 pad_add_fusion.idx_ref
  15.2 0.0 copy-done.1
  15.3 23.8 %shard_map.55 = (f32[1,9,128,128]{3,2,1,0:T(8,128)}, f32[1,9,128,128]{3,2,1,0:T(8,128)}, f32[1,9,128,128]{3,2,1,0:T(8,128)}) custom-call(s32[208]{0:T(256)} %pad_add_fusion.idx_ref, f32[16,8,128,128]{3,2,1,0:T(8,128)} %a_ref.1, f32[1032,128]{1,0:T(8,128)} %copy-done.1, f32[16,2,128,128]{3,2,1,0:T(8,128)} %mid_ref.1, f32[1032,128]{1,0:T(8,128)} %copy-done), custom_call_target="tpu_custom_call" | custom-call | tf_op jit(solution)/shard_map/pallas_call | solution.py:160
  39.1 1.2 %collective-permute-start.2 = (f32[1,9,128,128]{3,2,1,0:T(8,128)}, f32[1,9,128,128]{3,2,1,0:T(8,128)S(1)}, u32[]{:S(2)}, u32[]{:S(2)}) collective-permute-start(f32[1,9,128,128]{3,2,1,0:T(8,128)} %get-tuple-element.9), channel_id=1, source_target_pairs={{0,1},{1,2},{2,3},{3,4},{4,5},{5,6},{6,7},{7,0},{8,9},{9,10},{10,1... | collective-permute-start | bytes 1769480 | tf_op jit(solution)/shard_map/ppermute | solution.py:16
  40.3 3.1 %collective-permute-start.3 = (f32[1,9,128,128]{3,2,1,0:T(8,128)}, f32[1,9,128,128]{3,2,1,0:T(8,128)S(1)}, u32[]{:S(2)}, u32[]{:S(2)}) collective-permute-start(f32[1,9,128,128]{3,2,1,0:T(8,128)} %get-tuple-element.10), channel_id=1, source_target_pairs={{0,7},{1,0},{2,1},{3,2},{4,3},{5,4},{6,5},{7,6},{8,15},{9,8},{10,9... | collective-permute-start | bytes 1769480 | tf_op jit(solution)/shard_map/ppermute | solution.py:16
  43.4 1.7 %gather_fusion = f32[15,128,128]{2,1,0:T(8,128)S(1)} fusion(f32[1,9,128,128]{3,2,1,0:T(8,128)} %get-tuple-element.8, s32[15]{0:T(128)S(1)} %or_bitcast_fusion.2), kind=kCustom, calls=%fused_computation | custom fusion | bytes 1966200 | tf_op jit(solution)/shard_map/gather | solution.py:196
  45.1 16.5 %collective-permute-done.2 = f32[1,9,128,128]{3,2,1,0:T(8,128)S(1)} collective-permute-done((f32[1,9,128,128]{3,2,1,0:T(8,128)}, f32[1,9,128,128]{3,2,1,0:T(8,128)S(1)}, u32[]{:S(2)}, u32[]{:S(2)}) %collective-permute-start.2) | collective-permute-done | bytes 589856 | tf_op jit(solution)/shard_map/ppermute | solution.py:16
  61.6 0.6 gather_fusion.1
  62.2 0.8 %fusion.1 = f32[1,15,128,128]{3,2,1,0:T(8,128)S(1)} fusion(f32[15,128,128]{2,1,0:T(8,128)S(1)} %gather_fusion.1, f32[15,128,128]{2,1,0:T(8,128)S(1)} %gather_fusion, pred[15]{0:T(512)(128)(4,1)} %get-tuple-element.22, pred[15]{0:T(512)(128)(4,1)S(1)} %get-tuple-element.21), kind=kLoop, calls=%fused_computation.6 | loop fusion | flops 737280 | bytes 2949150 | tf_op jit(solution)/shard_map/add | solution.py:199
  63.0 0.7 %collective-permute-done.3 = f32[1,9,128,128]{3,2,1,0:T(8,128)S(1)} collective-permute-done((f32[1,9,128,128]{3,2,1,0:T(8,128)}, f32[1,9,128,128]{3,2,1,0:T(8,128)S(1)}, u32[]{:S(2)}, u32[]{:S(2)}) %collective-permute-start.3) | collective-permute-done | bytes 589856 | tf_op jit(solution)/shard_map/ppermute | solution.py:16
  63.7 0.6 gather_fusion.2
  64.4 1.1 %fusion = f32[1,15,128,128]{3,2,1,0:T(8,128)} fusion(f32[1,15,128,128]{3,2,1,0:T(8,128)S(1)} %fusion.1, f32[15,128,128]{2,1,0:T(8,128)S(1)} %gather_fusion.2, pred[15]{0:T(512)(128)(4,1)S(1)} %get-tuple-element.11), kind=kLoop, calls=%fused_computation.4 | loop fusion | flops 491520 | bytes 2949135 | tf_op jit(solution)/shard_map/add | solution.py:200
  (22 shorter events, 0.2 us)
Async XLA Ops:
  0.0 1.3 %copy-start.2 = (s32[16,2]{0,1:T(2,128)S(1)}, s32[16,2]{0,1:T(2,128)}, u32[]{:S(2)}) copy-start(s32[16,2]{0,1:T(2,128)} %param.8) | copy-start | bytes 388
  0.0 8.4 %copy-start.3 = (s32[16,8]{0,1:T(8,128)S(1)}, s32[16,8]{0,1:T(8,128)}, u32[]{:S(2)}) copy-start(s32[16,8]{0,1:T(8,128)} %param.6) | copy-start | bytes 1540
  0.0 8.9 %copy-start.4 = (s32[1,15]{1,0:T(1,128)S(1)}, s32[1,15]{1,0:T(1,128)}, u32[]{:S(2)}) copy-start(s32[1,15]{1,0:T(1,128)} %param.9) | copy-start | bytes 184
  1.6 11.4 %collective-permute-start.1 = (f32[1032,128]{1,0:T(8,128)S(1)}, f32[1032,128]{1,0:T(8,128)S(1)}, u32[]{:S(2)}, u32[]{:S(2)}) collective-permute-start(f32[1032,128]{1,0:T(8,128)S(1)} %select_maximum_fusion), channel_id=1, source_target_pairs={{8,0},{16,8},{24,16},{9,1},{17,9},{25,17},{10,2},{18,10},{26,18},{... | collective-permute-start | bytes 1585160 | tf_op jit(solution)/shard_map/ppermute | solution.py:122
  3.8 10.6 %collective-permute-start = (f32[1032,128]{1,0:T(8,128)S(1)}, f32[1032,128]{1,0:T(8,128)S(1)}, u32[]{:S(2)}, u32[]{:S(2)}) collective-permute-start(f32[1032,128]{1,0:T(8,128)S(1)} %select_maximum_fusion.1), channel_id=1, source_target_pairs={{0,8},{8,16},{16,24},{1,9},{9,17},{17,25},{2,10},{10,18},{18,26},{... | collective-permute-start | bytes 1585160 | tf_op jit(solution)/shard_map/ppermute | solution.py:121
  13.1 2.2 %copy-start = (f32[1032,128]{1,0:T(8,128)}, f32[1032,128]{1,0:T(8,128)S(1)}, u32[]{:S(2)}) copy-start(f32[1032,128]{1,0:T(8,128)S(1)} %collective-permute-done.1.up_ref) | copy-start | bytes 1585156
  14.5 0.8 %copy-start.1 = (f32[1032,128]{1,0:T(8,128)}, f32[1032,128]{1,0:T(8,128)S(1)}, u32[]{:S(2)}) copy-start(f32[1032,128]{1,0:T(8,128)S(1)} %collective-permute-done.low_ref) | copy-start | bytes 1585156
  39.1 22.5 %collective-permute-start.2 = (f32[1,9,128,128]{3,2,1,0:T(8,128)}, f32[1,9,128,128]{3,2,1,0:T(8,128)S(1)}, u32[]{:S(2)}, u32[]{:S(2)}) collective-permute-start(f32[1,9,128,128]{3,2,1,0:T(8,128)} %get-tuple-element.9), channel_id=1, source_target_pairs={{0,1},{1,2},{2,3},{3,4},{4,5},{5,6},{6,7},{7,0},{8,9},{9,10},{10,1... | collective-permute-start | bytes 1769480 | tf_op jit(solution)/shard_map/ppermute | solution.py:16
  40.3 23.4 %collective-permute-start.3 = (f32[1,9,128,128]{3,2,1,0:T(8,128)}, f32[1,9,128,128]{3,2,1,0:T(8,128)S(1)}, u32[]{:S(2)}, u32[]{:S(2)}) collective-permute-start(f32[1,9,128,128]{3,2,1,0:T(8,128)} %get-tuple-element.10), channel_id=1, source_target_pairs={{0,7},{1,0},{2,1},{3,2},{4,3},{5,4},{6,5},{7,6},{8,15},{9,8},{10,9... | collective-permute-start | bytes 1769480 | tf_op jit(solution)/shard_map/ppermute | solution.py:16

commit v18 on v17

--- a/solution.py
+++ b/solution.py
@@ -181,6 +181,7 @@
 
     from_lower = passed_along(to_upper, "tile", 1)
     from_upper = passed_along(to_lower, "tile", -1)
+    c_cols, from_lower = lax.optimization_barrier((c_cols, from_lower))
 
     c_slab = c_cols // (tiles * blocks)
     c_tile = (c_cols // blocks) % tiles

time: 65.7 us -> 67.1 us (1.021)
  waiting for transfers between devices: 22.1 us -> 23.8 us
  local copies, waits for them, and re-layouts: 5.15 us -> 4.1 us
  other arithmetic: 3.47 us -> 4.15 us
    gather x3, local copies, waits for them, and re-layouts: 2.9 us -> 1.84 us  [pick(): tiles_picked = part[r_idx, idx]]
    ppermute x2, waiting for transfers between devices: 17.2 us -> 18.2 us  [passed_along(): return lax.ppermute(value, axis, pairs)]
    convert_element_type x1, other arithmetic: 0.07 us -> 0.83 us  [halo(): keys = p_cols[first:first + RIM].astype(jnp.float32).reshape(1, key_count)]
  transfers between devices with their start and end apart: 4 -> 4, of which waited for: 4 -> 3; matrix products, arithmetic and copies ran while one was open for 7% -> 5% of each run, Pallas kernels for 0% -> 0%
where the time goes in v18:
time: 67.1 us; the launch traced here: 66.9 us
  Pallas kernels  23.9 us (36%)
  waiting for transfers between devices  23.8 us (35%)
  starting transfers between devices  10.8 us (16%)
  other arithmetic  4.15 us (6%)
  local copies, waits for them, and re-layouts  4.1 us (6%)
    pallas_call x1, Pallas kernels, shards(): pl.pallas_call(kernel, out_shape=(part, part, part), grid_spec=pltpu.Pref...  23.9 us
    ppermute x2, waiting for transfers between devices, passed_along(): return lax.ppermute(value, axis, pairs)  18.2 us
    ppermute x1, starting transfers between devices, shards(): lax.ppermute(halo(rows - RIM), 'slab', [(i, i + 1) for i in range(slabs -...  4.49 us
    ppermute x2, starting transfers between devices, passed_along(): return lax.ppermute(value, axis, pairs)  4.3 us
    ppermute x1, waiting for transfers between devices, shards(): up = lax.ppermute(halo(0), 'slab', [(i + 1, i) for i in range(slabs - 1)])  4.16 us
    ppermute x1, starting transfers between devices, shards(): up = lax.ppermute(halo(0), 'slab', [(i + 1, i) for i in range(slabs - 1)])  1.97 us
    gather x3, local copies, waits for them, and re-layouts, pick(): tiles_picked = part[r_idx, idx]  1.84 us
    ppermute x1, waiting for transfers between devices, shards(): lax.ppermute(halo(rows - RIM), 'slab', [(i, i + 1) for i in range(slabs -...  1.4 us
  transfers between devices with their start and end apart: 4, of which 3 were waited for; matrix products, arithmetic and copies ran while one was open for 5% of the time, Pallas kernels for 0%

profile of v18, /device:TPU:1, one launch (start us, length us, event | category | flops | bytes accessed | tf_op | source)
XLA Modules:
  0.0 66.9 jit_solution(6344201112364553610)
XLA Ops:
  0.0 0.8 %slice_convert_fusion.1 = (f32[4,2]{0,1:T(2,128)S(1)}, f32[4,2]{0,1:T(2,128)S(1)}) fusion(s32[16,2]{0,1:T(2,128)} %param.8), kind=kLoop, calls=%fused_computation.47 | loop fusion | flops 16 | bytes 128 | tf_op jit(solution)/shard_map/convert_element_type | solution.py:116
  0.8 0.1 copy.15
  0.9 0.1 reshape.68
  1.0 1.3 %fusion.20 = (f32[4,2,128,128]{3,2,1,0:T(8,128)S(1)}, f32[4,2,128,128]{3,2,1,0:T(8,128)S(1)}) fusion(f32[16,2,128,128]{3,2,1,0:T(8,128)} %mid_ref.1), kind=kLoop, calls=%fused_computation.69 | loop fusion | bytes 2097152 | tf_op jit(solution)/shard_map/slice | solution.py:118
  2.4 2.0 %collective-permute-start.1 = (f32[1032,128]{1,0:T(8,128)S(1)}, f32[1032,128]{1,0:T(8,128)S(1)}, u32[]{:S(2)}, u32[]{:S(2)}) collective-permute-start(f32[1032,128]{1,0:T(8,128)S(1)} %select_maximum_fusion), channel_id=1, source_target_pairs={{8,0},{16,8},{24,16},{9,1},{17,9},{25,17},{10,2},{18,10},{26,18},{... | collective-permute-start | bytes 1585160 | tf_op jit(solution)/shard_map/ppermute | solution.py:122
  4.3 0.1 copy.13
  4.4 0.1 reshape.65
  4.6 4.5 %collective-permute-start = (f32[1032,128]{1,0:T(8,128)S(1)}, f32[1032,128]{1,0:T(8,128)S(1)}, u32[]{:S(2)}, u32[]{:S(2)}) collective-permute-start(f32[1032,128]{1,0:T(8,128)S(1)} %select_maximum_fusion.1), channel_id=1, source_target_pairs={{0,8},{8,16},{16,24},{1,9},{9,17},{17,25},{2,10},{10,18},{18,26},{... | collective-permute-start | bytes 1585160 | tf_op jit(solution)/shard_map/ppermute | solution.py:121
  9.1 0.0 copy-done.3
  9.1 0.1 copy.14
  9.2 0.1 reshape.66
  9.3 0.1 copy.12
  9.4 0.1 reshape.63
  9.5 0.0 copy-done.4
  9.5 0.1 copy.11
  9.6 0.1 reshape.62
  9.7 4.2 %collective-permute-done.1.up_ref = f32[1032,128]{1,0:T(8,128)S(1)} collective-permute-done((f32[1032,128]{1,0:T(8,128)S(1)}, f32[1032,128]{1,0:T(8,128)S(1)}, u32[]{:S(2)}, u32[]{:S(2)}) %collective-permute-start.1) | collective-permute-done | bytes 528416 | tf_op jit(solution)/shard_map/ppermute | solution.py:122
  13.8 1.4 %collective-permute-done.low_ref = f32[1032,128]{1,0:T(8,128)S(1)} collective-permute-done((f32[1032,128]{1,0:T(8,128)S(1)}, f32[1032,128]{1,0:T(8,128)S(1)}, u32[]{:S(2)}, u32[]{:S(2)}) %collective-permute-start) | collective-permute-done | bytes 528416 | tf_op jit(solution)/shard_map/ppermute | solution.py:121
  15.2 0.1 fusion.18
  15.3 0.6 pad_add_fusion.idx_ref
  16.0 0.1 copy-done.2
  16.0 23.9 %shard_map.55 = (f32[1,9,128,128]{3,2,1,0:T(8,128)}, f32[1,9,128,128]{3,2,1,0:T(8,128)}, f32[1,9,128,128]{3,2,1,0:T(8,128)}) custom-call(s32[208]{0:T(256)} %pad_add_fusion.idx_ref, f32[16,8,128,128]{3,2,1,0:T(8,128)} %a_ref.1, f32[1032,128]{1,0:T(8,128)} %copy-done.2, f32[16,2,128,128]{3,2,1,0:T(8,128)} %mid_ref.1, f32[1032,128]{1,0:T(8,128)} %copy-done.1), custom_call_target="tpu_custom_call" | custom-call | tf_op jit(solution)/shard_map/pallas_call | solution.py:160
  39.9 1.2 %collective-permute-start.2 = (f32[1,9,128,128]{3,2,1,0:T(8,128)}, f32[1,9,128,128]{3,2,1,0:T(8,128)S(1)}, u32[]{:S(2)}, u32[]{:S(2)}) collective-permute-start(f32[1,9,128,128]{3,2,1,0:T(8,128)} %get-tuple-element.10), channel_id=1, source_target_pairs={{0,1},{1,2},{2,3},{3,4},{4,5},{5,6},{6,7},{7,0},{8,9},{9,10},{10,1... | collective-permute-start | bytes 1769480 | tf_op jit(solution)/shard_map/ppermute | solution.py:16
  41.2 3.1 %collective-permute-start.3 = (f32[1,9,128,128]{3,2,1,0:T(8,128)}, f32[1,9,128,128]{3,2,1,0:T(8,128)S(1)}, u32[]{:S(2)}, u32[]{:S(2)}) collective-permute-start(f32[1,9,128,128]{3,2,1,0:T(8,128)} %get-tuple-element.14), channel_id=1, source_target_pairs={{0,7},{1,0},{2,1},{3,2},{4,3},{5,4},{6,5},{7,6},{8,15},{9,8},{10,9... | collective-permute-start | bytes 1769480 | tf_op jit(solution)/shard_map/ppermute | solution.py:16
  44.2 18.2 %collective-permute-done.2 = f32[1,9,128,128]{3,2,1,0:T(8,128)S(1)} collective-permute-done((f32[1,9,128,128]{3,2,1,0:T(8,128)}, f32[1,9,128,128]{3,2,1,0:T(8,128)S(1)}, u32[]{:S(2)}, u32[]{:S(2)}) %collective-permute-start.2) | collective-permute-done | bytes 589856 | tf_op jit(solution)/shard_map/ppermute | solution.py:16
  62.5 0.5 and_bitcast_fusion.2
  63.1 0.6 gather_fusion.1
  63.7 0.6 gather_fusion
  64.3 0.8 %fusion.1 = f32[1,15,128,128]{3,2,1,0:T(8,128)S(1)} fusion(f32[15,128,128]{2,1,0:T(8,128)S(1)} %gather_fusion.1, f32[15,128,128]{2,1,0:T(8,128)S(1)} %gather_fusion, pred[15]{0:T(512)(128)(4,1)} %get-tuple-element.26, pred[15]{0:T(512)(128)(4,1)S(1)} %get-tuple-element.25), kind=kLoop, calls=%fused_computation.6 | loop fusion | flops 737280 | bytes 2949150 | tf_op jit(solution)/shard_map/add | solution.py:200
  65.1 0.0 collective-permute-done.3
  65.2 0.6 gather_fusion.2
  65.8 1.1 %fusion = f32[1,15,128,128]{3,2,1,0:T(8,128)} fusion(f32[1,15,128,128]{3,2,1,0:T(8,128)S(1)} %fusion.1, f32[15,128,128]{2,1,0:T(8,128)S(1)} %gather_fusion.2, pred[15]{0:T(512)(128)(4,1)S(1)} %get-tuple-element.15), kind=kLoop, calls=%fused_computation.4 | loop fusion | flops 491520 | bytes 2949135 | tf_op jit(solution)/shard_map/add | solution.py:201
  (23 shorter events, 0.2 us)
Async XLA Ops:
  1.0 8.1 %copy-start.3 = (s32[16,2]{0,1:T(2,128)S(1)}, s32[16,2]{0,1:T(2,128)}, u32[]{:S(2)}) copy-start(s32[16,2]{0,1:T(2,128)} %param.8) | copy-start | bytes 388
  1.0 8.5 %copy-start.4 = (s32[16,8]{0,1:T(8,128)S(1)}, s32[16,8]{0,1:T(8,128)}, u32[]{:S(2)}) copy-start(s32[16,8]{0,1:T(8,128)} %param.6) | copy-start | bytes 1540
  2.4 11.4 %collective-permute-start.1 = (f32[1032,128]{1,0:T(8,128)S(1)}, f32[1032,128]{1,0:T(8,128)S(1)}, u32[]{:S(2)}, u32[]{:S(2)}) collective-permute-start(f32[1032,128]{1,0:T(8,128)S(1)} %select_maximum_fusion), channel_id=1, source_target_pairs={{8,0},{16,8},{24,16},{9,1},{17,9},{25,17},{10,2},{18,10},{26,18},{... | collective-permute-start | bytes 1585160 | tf_op jit(solution)/shard_map/ppermute | solution.py:122
  4.6 10.6 %collective-permute-start = (f32[1032,128]{1,0:T(8,128)S(1)}, f32[1032,128]{1,0:T(8,128)S(1)}, u32[]{:S(2)}, u32[]{:S(2)}) collective-permute-start(f32[1032,128]{1,0:T(8,128)S(1)} %select_maximum_fusion.1), channel_id=1, source_target_pairs={{0,8},{8,16},{16,24},{1,9},{9,17},{17,25},{2,10},{10,18},{18,26},{... | collective-permute-start | bytes 1585160 | tf_op jit(solution)/shard_map/ppermute | solution.py:121
  13.8 2.2 %copy-start.1 = (f32[1032,128]{1,0:T(8,128)}, f32[1032,128]{1,0:T(8,128)S(1)}, u32[]{:S(2)}) copy-start(f32[1032,128]{1,0:T(8,128)S(1)} %collective-permute-done.1.up_ref) | copy-start | bytes 1585156
  15.2 0.8 %copy-start.2 = (f32[1032,128]{1,0:T(8,128)}, f32[1032,128]{1,0:T(8,128)S(1)}, u32[]{:S(2)}) copy-start(f32[1032,128]{1,0:T(8,128)S(1)} %collective-permute-done.low_ref) | copy-start | bytes 1585156
  16.0 46.4 %copy-start.5 = (s32[1,15]{1,0:T(1,128)S(1)}, s32[1,15]{1,0:T(1,128)}, u32[]{:S(2)}) copy-start(s32[1,15]{1,0:T(1,128)} %param.9) | copy-start | bytes 184
  39.9 23.8 %copy-start = (f32[1,9,128,128]{3,2,1,0:T(8,128)S(1)}, f32[1,9,128,128]{3,2,1,0:T(8,128)}, u32[]{:S(2)}) copy-start(f32[1,9,128,128]{3,2,1,0:T(8,128)} %get-tuple-element.12) | copy-start | bytes 1769476
  39.9 22.5 %collective-permute-start.2 = (f32[1,9,128,128]{3,2,1,0:T(8,128)}, f32[1,9,128,128]{3,2,1,0:T(8,128)S(1)}, u32[]{:S(2)}, u32[]{:S(2)}) collective-permute-start(f32[1,9,128,128]{3,2,1,0:T(8,128)} %get-tuple-element.10), channel_id=1, source_target_pairs={{0,1},{1,2},{2,3},{3,4},{4,5},{5,6},{6,7},{7,0},{8,9},{9,10},{10,1... | collective-permute-start | bytes 1769480 | tf_op jit(solution)/shard_map/ppermute | solution.py:16
  41.2 24.0 %collective-permute-start.3 = (f32[1,9,128,128]{3,2,1,0:T(8,128)}, f32[1,9,128,128]{3,2,1,0:T(8,128)S(1)}, u32[]{:S(2)}, u32[]{:S(2)}) collective-permute-start(f32[1,9,128,128]{3,2,1,0:T(8,128)} %get-tuple-element.14), channel_id=1, source_target_pairs={{0,7},{1,0},{2,1},{3,2},{4,3},{5,4},{6,5},{7,6},{8,15},{9,8},{10,9... | collective-permute-start | bytes 1769480 | tf_op jit(solution)/shard_map/ppermute | solution.py:16

commit v19 on v17

--- a/solution.py
+++ b/solution.py
@@ -150,7 +150,7 @@
     relative = jnp.remainder(targets // blocks - t + 1, tiles)
     owner = jnp.clip(relative * blocks + targets % blocks, 0, 3 * blocks - 1)
 
-    per_step = next(d for d in (2, 1) if rows % d == 0)
+    per_step = 1
     kernel = functools.partial(triple_kernel, coupling_slots, interp_slots, blocks, region)
     part = jax.ShapeDtypeStruct((blocks, region, bs, bs), jnp.float32)
     part_spec = pl.BlockSpec((blocks, region, bs, bs), lambda g, *_: (0, 0, 0, 0))

time: 65.7 us -> 65.7 us (level)
  no operation moved by 1% of the time
where the time goes in v19:
time: 65.7 us; the launch traced here: 65.4 us
  Pallas kernels  23.8 us (36%)
  waiting for transfers between devices  22.2 us (34%)
  starting transfers between devices  10.8 us (16%)
  local copies, waits for them, and re-layouts  5.15 us (8%)
  other arithmetic  3.47 us (5%)
    pallas_call x1, Pallas kernels, shards(): pl.pallas_call(kernel, out_shape=(part, part, part), grid_spec=pltpu.Pref...  23.8 us
    ppermute x2, waiting for transfers between devices, passed_along(): return lax.ppermute(value, axis, pairs)  17.2 us
    ppermute x1, starting transfers between devices, shards(): lax.ppermute(halo(rows - RIM), 'slab', [(i, i + 1) for i in range(slabs -...  4.49 us
    ppermute x2, starting transfers between devices, passed_along(): return lax.ppermute(value, axis, pairs)  4.3 us
    ppermute x1, waiting for transfers between devices, shards(): up = lax.ppermute(halo(0), 'slab', [(i + 1, i) for i in range(slabs - 1)])  3.54 us
    gather x3, local copies, waits for them, and re-layouts, pick(): tiles_picked = part[r_idx, idx]  2.9 us
    ppermute x1, starting transfers between devices, shards(): up = lax.ppermute(halo(0), 'slab', [(i + 1, i) for i in range(slabs - 1)])  1.97 us
    ppermute x1, waiting for transfers between devices, shards(): lax.ppermute(halo(rows - RIM), 'slab', [(i, i + 1) for i in range(slabs -...  1.4 us
  transfers between devices with their start and end apart: 4, of which 4 were waited for; matrix products, arithmetic and copies ran while one was open for 7% of the time, Pallas kernels for 0%

profile of v19, /device:TPU:1, one launch (start us, length us, event | category | flops | bytes accessed | tf_op | source)
XLA Modules:
  0.0 65.4 jit_solution(2614792988692639846)
XLA Ops:
  0.0 1.3 %fusion.20 = (f32[4,2,128,128]{3,2,1,0:T(8,128)S(1)}, f32[4,2,128,128]{3,2,1,0:T(8,128)S(1)}) fusion(f32[16,2,128,128]{3,2,1,0:T(8,128)} %mid_ref.1), kind=kLoop, calls=%fused_computation.69 | loop fusion | bytes 2097152 | tf_op jit(solution)/shard_map/slice | solution.py:118
  1.3 0.0 copy-done.2
  1.3 0.1 slice_convert_fusion.1
  1.4 0.1 copy.15
  1.5 0.1 reshape.68
  1.6 2.0 %collective-permute-start.1 = (f32[1032,128]{1,0:T(8,128)S(1)}, f32[1032,128]{1,0:T(8,128)S(1)}, u32[]{:S(2)}, u32[]{:S(2)}) collective-permute-start(f32[1032,128]{1,0:T(8,128)S(1)} %select_maximum_fusion), channel_id=1, source_target_pairs={{8,0},{16,8},{24,16},{9,1},{17,9},{25,17},{10,2},{18,10},{26,18},{... | collective-permute-start | bytes 1585160 | tf_op jit(solution)/shard_map/ppermute | solution.py:122
  3.6 0.1 copy.13
  3.7 0.1 reshape.65
  3.8 4.5 %collective-permute-start = (f32[1032,128]{1,0:T(8,128)S(1)}, f32[1032,128]{1,0:T(8,128)S(1)}, u32[]{:S(2)}, u32[]{:S(2)}) collective-permute-start(f32[1032,128]{1,0:T(8,128)S(1)} %select_maximum_fusion.1), channel_id=1, source_target_pairs={{0,8},{8,16},{16,24},{1,9},{9,17},{17,25},{2,10},{10,18},{18,26},{... | collective-permute-start | bytes 1585160 | tf_op jit(solution)/shard_map/ppermute | solution.py:121
  8.3 0.1 copy.14
  8.4 0.0 copy-done.3
  8.5 0.1 copy.11
  8.5 0.1 reshape.62
  8.6 0.1 reshape.66
  8.7 0.1 copy.12
  8.8 0.1 reshape.63
  9.0 0.5 and_bitcast_fusion.2
  9.5 3.5 %collective-permute-done.1.up_ref = f32[1032,128]{1,0:T(8,128)S(1)} collective-permute-done((f32[1032,128]{1,0:T(8,128)S(1)}, f32[1032,128]{1,0:T(8,128)S(1)}, u32[]{:S(2)}, u32[]{:S(2)}) %collective-permute-start.1) | collective-permute-done | bytes 528416 | tf_op jit(solution)/shard_map/ppermute | solution.py:122
  13.1 1.4 %collective-permute-done.low_ref = f32[1032,128]{1,0:T(8,128)S(1)} collective-permute-done((f32[1032,128]{1,0:T(8,128)S(1)}, f32[1032,128]{1,0:T(8,128)S(1)}, u32[]{:S(2)}, u32[]{:S(2)}) %collective-permute-start) | collective-permute-done | bytes 528416 | tf_op jit(solution)/shard_map/ppermute | solution.py:121
  14.5 0.1 fusion.18
  14.6 0.7 pad_add_fusion.idx_ref
  15.2 0.0 copy-done.1
  15.3 23.8 %shard_map.55 = (f32[1,9,128,128]{3,2,1,0:T(8,128)}, f32[1,9,128,128]{3,2,1,0:T(8,128)}, f32[1,9,128,128]{3,2,1,0:T(8,128)}) custom-call(s32[208]{0:T(256)} %pad_add_fusion.idx_ref, f32[16,8,128,128]{3,2,1,0:T(8,128)} %a_ref.1, f32[1032,128]{1,0:T(8,128)} %copy-done.1, f32[16,2,128,128]{3,2,1,0:T(8,128)} %mid_ref.1, f32[1032,128]{1,0:T(8,128)} %copy-done), custom_call_target="tpu_custom_call" | custom-call | tf_op jit(solution)/shard_map/pallas_call | solution.py:160
  39.0 1.2 %collective-permute-start.2 = (f32[1,9,128,128]{3,2,1,0:T(8,128)}, f32[1,9,128,128]{3,2,1,0:T(8,128)S(1)}, u32[]{:S(2)}, u32[]{:S(2)}) collective-permute-start(f32[1,9,128,128]{3,2,1,0:T(8,128)} %get-tuple-element.9), channel_id=1, source_target_pairs={{0,1},{1,2},{2,3},{3,4},{4,5},{5,6},{6,7},{7,0},{8,9},{9,10},{10,1... | collective-permute-start | bytes 1769480 | tf_op jit(solution)/shard_map/ppermute | solution.py:16
  40.3 3.1 %collective-permute-start.3 = (f32[1,9,128,128]{3,2,1,0:T(8,128)}, f32[1,9,128,128]{3,2,1,0:T(8,128)S(1)}, u32[]{:S(2)}, u32[]{:S(2)}) collective-permute-start(f32[1,9,128,128]{3,2,1,0:T(8,128)} %get-tuple-element.10), channel_id=1, source_target_pairs={{0,7},{1,0},{2,1},{3,2},{4,3},{5,4},{6,5},{7,6},{8,15},{9,8},{10,9... | collective-permute-start | bytes 1769480 | tf_op jit(solution)/shard_map/ppermute | solution.py:16
  43.4 1.7 %gather_fusion = f32[15,128,128]{2,1,0:T(8,128)S(1)} fusion(f32[1,9,128,128]{3,2,1,0:T(8,128)} %get-tuple-element.8, s32[15]{0:T(128)S(1)} %or_bitcast_fusion.2), kind=kCustom, calls=%fused_computation | custom fusion | bytes 1966200 | tf_op jit(solution)/shard_map/gather | solution.py:196
  45.1 16.5 %collective-permute-done.2 = f32[1,9,128,128]{3,2,1,0:T(8,128)S(1)} collective-permute-done((f32[1,9,128,128]{3,2,1,0:T(8,128)}, f32[1,9,128,128]{3,2,1,0:T(8,128)S(1)}, u32[]{:S(2)}, u32[]{:S(2)}) %collective-permute-start.2) | collective-permute-done | bytes 589856 | tf_op jit(solution)/shard_map/ppermute | solution.py:16
  61.6 0.6 gather_fusion.1
  62.2 0.8 %fusion.1 = f32[1,15,128,128]{3,2,1,0:T(8,128)S(1)} fusion(f32[15,128,128]{2,1,0:T(8,128)S(1)} %gather_fusion.1, f32[15,128,128]{2,1,0:T(8,128)S(1)} %gather_fusion, pred[15]{0:T(512)(128)(4,1)} %get-tuple-element.22, pred[15]{0:T(512)(128)(4,1)S(1)} %get-tuple-element.21), kind=kLoop, calls=%fused_computation.6 | loop fusion | flops 737280 | bytes 2949150 | tf_op jit(solution)/shard_map/add | solution.py:199
  63.0 0.7 %collective-permute-done.3 = f32[1,9,128,128]{3,2,1,0:T(8,128)S(1)} collective-permute-done((f32[1,9,128,128]{3,2,1,0:T(8,128)}, f32[1,9,128,128]{3,2,1,0:T(8,128)S(1)}, u32[]{:S(2)}, u32[]{:S(2)}) %collective-permute-start.3) | collective-permute-done | bytes 589856 | tf_op jit(solution)/shard_map/ppermute | solution.py:16
  63.7 0.6 gather_fusion.2
  64.3 1.1 %fusion = f32[1,15,128,128]{3,2,1,0:T(8,128)} fusion(f32[1,15,128,128]{3,2,1,0:T(8,128)S(1)} %fusion.1, f32[15,128,128]{2,1,0:T(8,128)S(1)} %gather_fusion.2, pred[15]{0:T(512)(128)(4,1)S(1)} %get-tuple-element.11), kind=kLoop, calls=%fused_computation.4 | loop fusion | flops 491520 | bytes 2949135 | tf_op jit(solution)/shard_map/add | solution.py:200
  (22 shorter events, 0.2 us)
Async XLA Ops:
  0.0 1.3 %copy-start.2 = (s32[16,2]{0,1:T(2,128)S(1)}, s32[16,2]{0,1:T(2,128)}, u32[]{:S(2)}) copy-start(s32[16,2]{0,1:T(2,128)} %param.8) | copy-start | bytes 388
  0.0 8.4 %copy-start.3 = (s32[16,8]{0,1:T(8,128)S(1)}, s32[16,8]{0,1:T(8,128)}, u32[]{:S(2)}) copy-start(s32[16,8]{0,1:T(8,128)} %param.6) | copy-start | bytes 1540
  0.0 8.9 %copy-start.4 = (s32[1,15]{1,0:T(1,128)S(1)}, s32[1,15]{1,0:T(1,128)}, u32[]{:S(2)}) copy-start(s32[1,15]{1,0:T(1,128)} %param.9) | copy-start | bytes 184
  1.6 11.4 %collective-permute-start.1 = (f32[1032,128]{1,0:T(8,128)S(1)}, f32[1032,128]{1,0:T(8,128)S(1)}, u32[]{:S(2)}, u32[]{:S(2)}) collective-permute-start(f32[1032,128]{1,0:T(8,128)S(1)} %select_maximum_fusion), channel_id=1, source_target_pairs={{8,0},{16,8},{24,16},{9,1},{17,9},{25,17},{10,2},{18,10},{26,18},{... | collective-permute-start | bytes 1585160 | tf_op jit(solution)/shard_map/ppermute | solution.py:122
  3.8 10.6 %collective-permute-start = (f32[1032,128]{1,0:T(8,128)S(1)}, f32[1032,128]{1,0:T(8,128)S(1)}, u32[]{:S(2)}, u32[]{:S(2)}) collective-permute-start(f32[1032,128]{1,0:T(8,128)S(1)} %select_maximum_fusion.1), channel_id=1, source_target_pairs={{0,8},{8,16},{16,24},{1,9},{9,17},{17,25},{2,10},{10,18},{18,26},{... | collective-permute-start | bytes 1585160 | tf_op jit(solution)/shard_map/ppermute | solution.py:121
  13.1 2.2 %copy-start = (f32[1032,128]{1,0:T(8,128)}, f32[1032,128]{1,0:T(8,128)S(1)}, u32[]{:S(2)}) copy-start(f32[1032,128]{1,0:T(8,128)S(1)} %collective-permute-done.1.up_ref) | copy-start | bytes 1585156
  14.5 0.8 %copy-start.1 = (f32[1032,128]{1,0:T(8,128)}, f32[1032,128]{1,0:T(8,128)S(1)}, u32[]{:S(2)}) copy-start(f32[1032,128]{1,0:T(8,128)S(1)} %collective-permute-done.low_ref) | copy-start | bytes 1585156
  39.0 22.5 %collective-permute-start.2 = (f32[1,9,128,128]{3,2,1,0:T(8,128)}, f32[1,9,128,128]{3,2,1,0:T(8,128)S(1)}, u32[]{:S(2)}, u32[]{:S(2)}) collective-permute-start(f32[1,9,128,128]{3,2,1,0:T(8,128)} %get-tuple-element.9), channel_id=1, source_target_pairs={{0,1},{1,2},{2,3},{3,4},{4,5},{5,6},{6,7},{7,0},{8,9},{9,10},{10,1... | collective-permute-start | bytes 1769480 | tf_op jit(solution)/shard_map/ppermute | solution.py:16
  40.3 23.4 %collective-permute-start.3 = (f32[1,9,128,128]{3,2,1,0:T(8,128)}, f32[1,9,128,128]{3,2,1,0:T(8,128)S(1)}, u32[]{:S(2)}, u32[]{:S(2)}) collective-permute-start(f32[1,9,128,128]{3,2,1,0:T(8,128)} %get-tuple-element.10), channel_id=1, source_target_pairs={{0,7},{1,0},{2,1},{3,2},{4,3},{5,4},{6,5},{7,6},{8,15},{9,8},{10,9... | collective-permute-start | bytes 1769480 | tf_op jit(solution)/shard_map/ppermute | solution.py:16

commit v20 on v17

--- a/solution.py
+++ b/solution.py
@@ -197,7 +197,12 @@
         return jnp.where(valid[:, :, None, None], tiles_picked, 0.0)
 
     early = lax.optimization_barrier(pick(own_part, c_dt) + pick(from_lower, c_dt + 1))
-    return early + pick(from_upper, c_dt - 1)
+    dt_up = c_dt - 1
+    up_idx = jnp.where((dt_up >= -1) & (dt_up <= 1), (base + dt_up + 1) * blocks + c_w, -1)
+    late = sum(
+        jnp.where((up_idx == k)[:, :, None, None], from_upper[:, k : k + 1], 0.0) for k in range(region)
+    )
+    return early + late
 
 
 def solution(mesh):

time: 65.7 us -> 65.7 us (level)
  waiting for transfers between devices: 22.1 us -> 23.3 us
    gather x3 -> x2, local copies, waits for them, and re-layouts: 2.9 us -> 2.29 us  [pick(): tiles_picked = part[r_idx, idx]]
  transfers between devices with their start and end apart: 4 -> 4, of which waited for: 4 -> 4; matrix products, arithmetic and copies ran while one was open for 7% -> 5% of each run, Pallas kernels for 0% -> 0%
where the time goes in v20:
time: 65.7 us; the launch traced here: 65.5 us
  Pallas kernels  23.8 us (36%)
  waiting for transfers between devices  23.3 us (35%)
  starting transfers between devices  10.8 us (16%)
  local copies, waits for them, and re-layouts  4.57 us (7%)
  other arithmetic  2.84 us (4%)
    pallas_call x1, Pallas kernels, shards(): pl.pallas_call(kernel, out_shape=(part, part, part), grid_spec=pltpu.Pref...  23.8 us
    ppermute x2, waiting for transfers between devices, passed_along(): return lax.ppermute(value, axis, pairs)  17.8 us
    ppermute x1, starting transfers between devices, shards(): lax.ppermute(halo(rows - RIM), 'slab', [(i, i + 1) for i in range(slabs -...  4.49 us
    ppermute x2, starting transfers between devices, passed_along(): return lax.ppermute(value, axis, pairs)  4.3 us
    ppermute x1, waiting for transfers between devices, shards(): up = lax.ppermute(halo(0), 'slab', [(i + 1, i) for i in range(slabs - 1)])  4.09 us
    gather x2, local copies, waits for them, and re-layouts, pick(): tiles_picked = part[r_idx, idx]  2.29 us
    ppermute x1, starting transfers between devices, shards(): up = lax.ppermute(halo(0), 'slab', [(i + 1, i) for i in range(slabs - 1)])  1.97 us
    add x1, other arithmetic, shards(): return early + late  1.67 us
  transfers between devices with their start and end apart: 4, of which 4 were waited for; matrix products, arithmetic and copies ran while one was open for 5% of the time, Pallas kernels for 0%

profile of v20, /device:TPU:1, one launch (start us, length us, event | category | flops | bytes accessed | tf_op | source)
XLA Modules:
  0.0 65.5 jit_solution(833619725765250813)
XLA Ops:
  0.0 1.3 %fusion.18 = (f32[4,2,128,128]{3,2,1,0:T(8,128)S(1)}, f32[4,2,128,128]{3,2,1,0:T(8,128)S(1)}) fusion(f32[16,2,128,128]{3,2,1,0:T(8,128)} %mid_ref.1), kind=kLoop, calls=%fused_computation.81 | loop fusion | bytes 2097152 | tf_op jit(solution)/shard_map/slice | solution.py:118
  1.3 0.0 copy-done.2
  1.3 0.1 slice_convert_fusion.1
  1.4 0.1 copy.15
  1.5 0.1 reshape.170
  1.6 2.0 %collective-permute-start.1 = (f32[1032,128]{1,0:T(8,128)S(1)}, f32[1032,128]{1,0:T(8,128)S(1)}, u32[]{:S(2)}, u32[]{:S(2)}) collective-permute-start(f32[1032,128]{1,0:T(8,128)S(1)} %select_maximum_fusion), channel_id=1, source_target_pairs={{8,0},{16,8},{24,16},{9,1},{17,9},{25,17},{10,2},{18,10},{26,18},{... | collective-permute-start | bytes 1585160 | tf_op jit(solution)/shard_map/ppermute | solution.py:122
  3.6 0.1 copy.13
  3.7 0.1 reshape.167
  3.8 4.5 %collective-permute-start = (f32[1032,128]{1,0:T(8,128)S(1)}, f32[1032,128]{1,0:T(8,128)S(1)}, u32[]{:S(2)}, u32[]{:S(2)}) collective-permute-start(f32[1032,128]{1,0:T(8,128)S(1)} %select_maximum_fusion.1), channel_id=1, source_target_pairs={{0,8},{8,16},{16,24},{1,9},{9,17},{17,25},{2,10},{10,18},{18,26},{... | collective-permute-start | bytes 1585160 | tf_op jit(solution)/shard_map/ppermute | solution.py:121
  8.3 0.1 copy.14
  8.4 0.0 copy-done.3
  8.5 0.1 copy.11
  8.5 0.1 reshape.164
  8.6 0.1 reshape.168
  8.7 0.1 copy.12
  8.8 0.1 reshape.165
  8.9 0.0 copy-done.4
  9.0 4.1 %collective-permute-done.1.up_ref = f32[1032,128]{1,0:T(8,128)S(1)} collective-permute-done((f32[1032,128]{1,0:T(8,128)S(1)}, f32[1032,128]{1,0:T(8,128)S(1)}, u32[]{:S(2)}, u32[]{:S(2)}) %collective-permute-start.1) | collective-permute-done | bytes 528416 | tf_op jit(solution)/shard_map/ppermute | solution.py:122
  13.1 1.4 %collective-permute-done.low_ref = f32[1032,128]{1,0:T(8,128)S(1)} collective-permute-done((f32[1032,128]{1,0:T(8,128)S(1)}, f32[1032,128]{1,0:T(8,128)S(1)}, u32[]{:S(2)}, u32[]{:S(2)}) %collective-permute-start) | collective-permute-done | bytes 528416 | tf_op jit(solution)/shard_map/ppermute | solution.py:121
  14.5 0.1 fusion.16
  14.6 0.6 pad_add_fusion.idx_ref
  15.2 0.0 copy-done
  15.2 0.0 copy-done.1
  15.3 23.8 %shard_map.55 = (f32[1,9,128,128]{3,2,1,0:T(8,128)}, f32[1,9,128,128]{3,2,1,0:T(8,128)}, f32[1,9,128,128]{3,2,1,0:T(8,128)}) custom-call(s32[208]{0:T(256)} %pad_add_fusion.idx_ref, f32[16,8,128,128]{3,2,1,0:T(8,128)} %a_ref.1, f32[1032,128]{1,0:T(8,128)} %copy-done.1, f32[16,2,128,128]{3,2,1,0:T(8,128)} %mid_ref.1, f32[1032,128]{1,0:T(8,128)} %copy-done), custom_call_target="tpu_custom_call" | custom-call | tf_op jit(solution)/shard_map/pallas_call | solution.py:160
  39.1 1.2 %collective-permute-start.2 = (f32[1,9,128,128]{3,2,1,0:T(8,128)}, f32[1,9,128,128]{3,2,1,0:T(8,128)S(1)}, u32[]{:S(2)}, u32[]{:S(2)}) collective-permute-start(f32[1,9,128,128]{3,2,1,0:T(8,128)} %get-tuple-element.9), channel_id=1, source_target_pairs={{0,1},{1,2},{2,3},{3,4},{4,5},{5,6},{6,7},{7,0},{8,9},{9,10},{10,1... | collective-permute-start | bytes 1769480 | tf_op jit(solution)/shard_map/ppermute | solution.py:16
  40.3 3.1 %collective-permute-start.3 = (f32[1,9,128,128]{3,2,1,0:T(8,128)}, f32[1,9,128,128]{3,2,1,0:T(8,128)S(1)}, u32[]{:S(2)}, u32[]{:S(2)}) collective-permute-start(f32[1,9,128,128]{3,2,1,0:T(8,128)} %get-tuple-element.10), channel_id=1, source_target_pairs={{0,7},{1,0},{2,1},{3,2},{4,3},{5,4},{6,5},{7,6},{8,15},{9,8},{10,9... | collective-permute-start | bytes 1769480 | tf_op jit(solution)/shard_map/ppermute | solution.py:16
  43.4 1.7 %gather_fusion = f32[15,128,128]{2,1,0:T(8,128)S(1)} fusion(f32[1,9,128,128]{3,2,1,0:T(8,128)} %get-tuple-element.8, s32[15]{0:T(128)S(1)} %or_bitcast_fusion.1), kind=kCustom, calls=%fused_computation | custom fusion | bytes 1966200 | tf_op jit(solution)/shard_map/gather | solution.py:196
  45.1 16.5 %collective-permute-done.2 = f32[1,9,128,128]{3,2,1,0:T(8,128)S(1)} collective-permute-done((f32[1,9,128,128]{3,2,1,0:T(8,128)}, f32[1,9,128,128]{3,2,1,0:T(8,128)S(1)}, u32[]{:S(2)}, u32[]{:S(2)}) %collective-permute-start.2) | collective-permute-done | bytes 589856 | tf_op jit(solution)/shard_map/ppermute | solution.py:16
  61.6 0.6 gather_fusion.1
  62.2 0.2 fusion
  62.4 1.3 %collective-permute-done.3 = f32[1,9,128,128]{3,2,1,0:T(8,128)S(1)} collective-permute-done((f32[1,9,128,128]{3,2,1,0:T(8,128)}, f32[1,9,128,128]{3,2,1,0:T(8,128)S(1)}, u32[]{:S(2)}, u32[]{:S(2)}) %collective-permute-start.3) | collective-permute-done | bytes 589856 | tf_op jit(solution)/shard_map/ppermute | solution.py:16
  63.8 1.7 %add_add_fusion = f32[1,15,128,128]{3,2,1,0:T(8,128)} fusion(f32[1,15,128,128]{3,2,1,0:T(8,128)S(1)} %fusion, f32[128,128]{1,0:T(8,128)S(1)} %get-tuple-element.18, f32[128,128]{1,0:T(8,128)S(1)} %get-tuple-element.19, f32[128,128]{1,0:T(8,128)S(1)} %get-tuple-element.20, f32[128,128]{1,0:T(8,128)S(1)} %get-tuple-element.21, ...), kind=kLoop, calls=%fused_computation.5 | loop fusion | flops 4423680 | bytes 2556039 | tf_op jit(solution)/shard_map/add | solution.py:205
  (20 shorter events, 0.2 us)
Async XLA Ops:
  0.0 1.3 %copy-start.2 = (s32[16,2]{0,1:T(2,128)S(1)}, s32[16,2]{0,1:T(2,128)}, u32[]{:S(2)}) copy-start(s32[16,2]{0,1:T(2,128)} %param.8) | copy-start | bytes 388
  0.0 8.4 %copy-start.3 = (s32[16,8]{0,1:T(8,128)S(1)}, s32[16,8]{0,1:T(8,128)}, u32[]{:S(2)}) copy-start(s32[16,8]{0,1:T(8,128)} %param.6) | copy-start | bytes 1540
  0.0 8.9 %copy-start.4 = (s32[1,15]{1,0:T(1,128)S(1)}, s32[1,15]{1,0:T(1,128)}, u32[]{:S(2)}) copy-start(s32[1,15]{1,0:T(1,128)} %param.9) | copy-start | bytes 184
  1.6 11.4 %collective-permute-start.1 = (f32[1032,128]{1,0:T(8,128)S(1)}, f32[1032,128]{1,0:T(8,128)S(1)}, u32[]{:S(2)}, u32[]{:S(2)}) collective-permute-start(f32[1032,128]{1,0:T(8,128)S(1)} %select_maximum_fusion), channel_id=1, source_target_pairs={{8,0},{16,8},{24,16},{9,1},{17,9},{25,17},{10,2},{18,10},{26,18},{... | collective-permute-start | bytes 1585160 | tf_op jit(solution)/shard_map/ppermute | solution.py:122
  3.8 10.6 %collective-permute-start = (f32[1032,128]{1,0:T(8,128)S(1)}, f32[1032,128]{1,0:T(8,128)S(1)}, u32[]{:S(2)}, u32[]{:S(2)}) collective-permute-start(f32[1032,128]{1,0:T(8,128)S(1)} %select_maximum_fusion.1), channel_id=1, source_target_pairs={{0,8},{8,16},{16,24},{1,9},{9,17},{17,25},{2,10},{10,18},{18,26},{... | collective-permute-start | bytes 1585160 | tf_op jit(solution)/shard_map/ppermute | solution.py:121
  13.1 2.1 %copy-start = (f32[1032,128]{1,0:T(8,128)}, f32[1032,128]{1,0:T(8,128)S(1)}, u32[]{:S(2)}) copy-start(f32[1032,128]{1,0:T(8,128)S(1)} %collective-permute-done.1.up_ref) | copy-start | bytes 1585156
  14.5 0.8 %copy-start.1 = (f32[1032,128]{1,0:T(8,128)}, f32[1032,128]{1,0:T(8,128)S(1)}, u32[]{:S(2)}) copy-start(f32[1032,128]{1,0:T(8,128)S(1)} %collective-permute-done.low_ref) | copy-start | bytes 1585156
  39.1 22.5 %collective-permute-start.2 = (f32[1,9,128,128]{3,2,1,0:T(8,128)}, f32[1,9,128,128]{3,2,1,0:T(8,128)S(1)}, u32[]{:S(2)}, u32[]{:S(2)}) collective-permute-start(f32[1,9,128,128]{3,2,1,0:T(8,128)} %get-tuple-element.9), channel_id=1, source_target_pairs={{0,1},{1,2},{2,3},{3,4},{4,5},{5,6},{6,7},{7,0},{8,9},{9,10},{10,1... | collective-permute-start | bytes 1769480 | tf_op jit(solution)/shard_map/ppermute | solution.py:16
  40.3 23.4 %collective-permute-start.3 = (f32[1,9,128,128]{3,2,1,0:T(8,128)}, f32[1,9,128,128]{3,2,1,0:T(8,128)S(1)}, u32[]{:S(2)}, u32[]{:S(2)}) collective-permute-start(f32[1,9,128,128]{3,2,1,0:T(8,128)} %get-tuple-element.10), channel_id=1, source_target_pairs={{0,7},{1,0},{2,1},{3,2},{4,3},{5,4},{6,5},{7,6},{8,15},{9,8},{10,9... | collective-permute-start | bytes 1769480 | tf_op jit(solution)/shard_map/ppermute | solution.py:16
